TPU v7x, 256 devices: a whole 4x4x8 slice. The times are simulated.
256 devices in a mesh: aa: 32 (over z, x), ba: 8 (over y, core).
Axes of the slice: x: 4, y: 4, z: 8, core: 2. Of those that a mesh axis runs over, the one named last changes fastest.
Arguments:
- snapshots: float32 [8192, 65536], P(('aa', 'ba')), may hold values from -125 to 125
Outputs:
- factors: float32 [8, 64, 64], replicated
- pod_modes: float32 [8, 64, 65536], P(None, None, ('aa', 'ba'))
All inputs are finite; a program needn't handle non-finite values.
Results may differ from a plain program's by a relative error of at most 0.000098.
Values sent between devices are 32-bit elements; how exact they have to be, the bound alone decides.
No kernel may reach another device: no remote copies, remote signals or barrier semaphores. Data moves between devices by JAX's collectives and lax.ppermute only.
A program may use at most 128 MiB of HBM per device.

v0:
```python
import math

import jax
import jax.numpy as jnp
from jax import lax
from jax.sharding import PartitionSpec as P

FREQS = 8


def spectral_table(block_len, points):
    sample = jnp.arange(block_len, dtype=jnp.int32)
    harmonic = jnp.arange(1, FREQS + 1, dtype=jnp.int32)
    phase_turns = (sample[:, None] * harmonic[None, :] % block_len).astype(jnp.float32) * (
        2.0 * math.pi / block_len
    )
    sample_angle = sample.astype(jnp.float32) * (2.0 * math.pi / block_len)
    window = 0.5 - 0.5 * jnp.cos(sample_angle)
    norm_scale = 1.0 / jnp.sqrt(points * jnp.sum(window * window))
    cosine = window[:, None] * jnp.cos(phase_turns) * norm_scale
    sine = -window[:, None] * jnp.sin(phase_turns) * norm_scale
    return jnp.stack([cosine, sine], axis=1)


def local(snapshots):
    time_dev, points = snapshots.shape
    n_aa = lax.axis_size("aa")
    n_ba = lax.axis_size("ba")
    pts_dev = points // (n_aa * n_ba)
    block_len = time_dev * n_ba
    table = spectral_table(block_len, points)
    regrouped = lax.all_to_all(
        lax.all_to_all(snapshots, "aa", split_axis=1, concat_axis=0, tiled=True),
        "ba",
        split_axis=1,
        concat_axis=0,
        tiled=True,
    )
    arranged = regrouped.reshape(n_ba, n_aa, time_dev, pts_dev)
    table_parts = table.reshape(n_ba, time_dev, 2, FREQS)
    spectra = jnp.einsum("uasp,usgf->agfp", arranged, table_parts, precision=lax.Precision.HIGHEST)
    blocks = spectra.shape[0]
    columns = 2 * blocks
    product = jnp.einsum("bgfp,chfp->fbgch", spectra, spectra, precision=lax.Precision.HIGHEST)
    gram_sum = lax.psum(product.reshape(FREQS, columns, columns), ("aa", "ba"))
    lower_factor = jnp.linalg.cholesky(gram_sum)
    identity = jnp.broadcast_to(jnp.eye(columns, dtype=gram_sum.dtype), lower_factor.shape)
    inverse = lax.linalg.triangular_solve(lower_factor, identity, left_side=True, lower=True)
    pod_modes = math.sqrt(points) * jnp.einsum(
        "fibg,bgfp->fip",
        inverse.reshape(FREQS, columns, blocks, 2),
        spectra,
        precision=lax.Precision.HIGHEST,
    )
    return (jnp.swapaxes(lower_factor, 1, 2), pod_modes)


def solution(mesh):
    placed = (P(("aa", "ba"), None),)
    return jax.shard_map(
        local,
        mesh=mesh,
        in_specs=placed,
        out_specs=(P(), P(None, None, ("aa", "ba"))),
        check_vma=False,
    )
```

profile of v0, /device:TPU:1, one launch (start us, length us, event | category | flops | bytes accessed | tf_op | source)
XLA Modules:
  0.0 674.6 jit_solution(12656147163398301146)
XLA Ops:
  7.2 4.0 copy.75
  11.1 195.2 %all_to_all.32 = f32[32,32,2048]{2,0,1:T(8,128)S(1)} all-to-all(f32[32,32,2048]{2,0,1:T(8,128)S(1)} %bitcast.46), channel_id=1, replica_groups=mesh['aa'=32,'ba'=8] {'aa'}, dimensions={1} | all-to-all | bytes 16777216 | tf_op jit(solution)/shard_map/all_to_all | solution.py:33
  206.3 4.1 copy.61
  210.4 5.8 copy.38
  216.2 7.7 %all-to-all-start.1 = ((f32[1024,8,256]{2,0,1:T(8,128)}), f32[1024,8,256]{2,0,1:T(8,128)}, u32[]{:S(2)}, u32[]{:S(2)}) async-start(f32[1024,8,256]{2,0,1:T(8,128)} %copy.38), calls=%async_computation.1 | async-start | bytes 16777216 | tf_op jit(solution)/shard_map/all_to_all | solution.py:32
  223.9 0.6 multiply_reduce_fusion
  225.3 0.2 multiply_multiply_fusion.1
  225.5 92.2 %all-to-all-done.1 = f32[1024,8,256]{2,0,1:T(8,128)} async-done(((f32[1024,8,256]{2,0,1:T(8,128)}), f32[1024,8,256]{2,0,1:T(8,128)}, u32[]{:S(2)}, u32[]{:S(2)}) %all-to-all-start.1) | async-done | bytes 8388640 | tf_op jit(solution)/shard_map/all_to_all | solution.py:32
  317.7 9.1 %fusion = f32[2,8,32,256,1]{3,1,4,2,0:T(8,128)S(1)} fusion(f32[8,32,32,256]{3,2,1,0:T(8,128)} %bitcast.4, f32[8,32,1,8]{1,3,0,2:T(8,128)S(1)} %get-tuple-element.13, f32[8,32,1,8]{1,3,0,2:T(8,128)S(1)} %get-tuple-element.12), kind=kOutput, calls=%fused_computation.1 | convolution fusion | flops 402657280 | bytes 8929280 | tf_op jit(solution)/shard_map/uasp,usgf->agfp/dot_general | solution.py:41
  326.9 1.6 fusion.4
  328.5 1.2 copy.42
  329.7 1.9 copy.43
  331.6 0.0 all-reduce.2.cloned.1.call-update
  331.6 244.4 %all-reduce.2.cloned.1.call-done = f32[8,64,64]{1,2,0:T(8,128)} async-done(((f32[8,64,64]{1,2,0:T(8,128)}), f32[8,64,64]{1,2,0:T(8,128)}) %all-reduce.2.cloned.1.call-update) | async-done | bytes 131088 | tf_op jit(solution)/shard_map/psum | solution.py:45
  576.0 1.1 copy.44
  577.1 1.0 fusion.10
  578.0 46.9 %custom-call.7 = f32[8,64,64]{2,1,0:T(8,128)S(1)} custom-call(f32[8,64,64]{2,1,0:T(8,128)S(1)} %fusion.10), custom_call_target="Cholesky" | custom-call | tf_op jit(solution)/shard_map/jit(cholesky)/cholesky | solution.py:46
  625.0 0.1 compare_reduce_fusion
  625.1 0.1 select_bitcast_fusion
  625.2 0.8 copy.49
  626.1 39.3 %custom-call.8 = f32[8,1,64,64]{2,3,1,0:T(8,128)S(1)} custom-call(f32[8,1,64,64]{3,2,1,0:T(8,128)S(1)} %get-tuple-element.10), custom_call_target="InvertDiagBlocksLowerTriangular" | custom-call | tf_op jit(solution)/shard_map/triangular_solve | solution.py:48
  665.4 0.6 fusion.8
  666.0 0.1 copy.46
  666.1 1.6 fusion.3
  (8 shorter events, 0.1 us)
Async XLA Ops:
  216.2 101.5 %all-to-all-start.1 = ((f32[1024,8,256]{2,0,1:T(8,128)}), f32[1024,8,256]{2,0,1:T(8,128)}, u32[]{:S(2)}, u32[]{:S(2)}) async-start(f32[1024,8,256]{2,0,1:T(8,128)} %copy.38), calls=%async_computation.1 | async-start | bytes 16777216 | tf_op jit(solution)/shard_map/all_to_all | solution.py:32
  223.8 352.1 %all-reduce.2.cloned.1.call-start = ((), (), s32[]{:S(2)}) async-start(), calls=%async_computation.2 | async-start | bytes 524288 | tf_op jit(solution)/shard_map/psum | solution.py:45
Sparse Core Ops, SparseCore 0:
  331.7 244.2 all-reduce.1
where the time goes:
time: 675 us
  waiting for transfers between devices  337 us (50%)
  blocking collectives  195 us (29%)
  other arithmetic  88.4 us (13%)
  local copies, waits for them, and re-layouts  19 us (3%)
  between operations  14.8 us (2%)
  matrix products  12.9 us (2%)
  starting transfers between devices  7.67 us (1%)
    psum x1, waiting for transfers between devices, local(): gram_sum = lax.psum(product.reshape(FREQS, columns, columns), ('aa', 'ba'))  244 us
    all_to_all x1, blocking collectives, local(): lax.all_to_all(snapshots, 'aa', split_axis=1, concat_axis=0, tiled=True)  195 us
    all_to_all x1, waiting for transfers between devices, local(): lax.all_to_all(lax.all_to_all(snapshots, 'aa', split_axis=1, concat_axis=...  92.2 us
    another operation x4, other arithmetic, local(): lower_factor = jnp.linalg.cholesky(gram_sum)  47.1 us
    another operation x2, other arithmetic, local(): lax.linalg.triangular_solve(lower_factor, identity, left_side=True, lower...  39.4 us
  transfers between devices with their start and end apart: 2, of which 2 were waited for; matrix products, arithmetic and copies ran while one was open for 0% of the time, Pallas kernels for 0%

commit v1 on v0

v1 whole, which is shorter than its diff:
```python
import math

import jax
import jax.numpy as jnp
from jax import lax
from jax.sharding import PartitionSpec as P

FREQS = 8


def spectral_rows(block_len, points, first, count):
    sample = first + jnp.arange(count, dtype=jnp.int32)
    harmonic = jnp.arange(1, FREQS + 1, dtype=jnp.int32)
    phase_turns = (sample[:, None] * harmonic[None, :] % block_len).astype(jnp.float32) * (
        2.0 * math.pi / block_len
    )
    full = jnp.arange(block_len, dtype=jnp.int32).astype(jnp.float32) * (2.0 * math.pi / block_len)
    full_window = 0.5 - 0.5 * jnp.cos(full)
    norm_scale = 1.0 / jnp.sqrt(points * jnp.sum(full_window * full_window))
    sample_angle = sample.astype(jnp.float32) * (2.0 * math.pi / block_len)
    window = 0.5 - 0.5 * jnp.cos(sample_angle)
    cosine = window[:, None] * jnp.cos(phase_turns) * norm_scale
    sine = -window[:, None] * jnp.sin(phase_turns) * norm_scale
    return jnp.stack([cosine, sine], axis=1)


def local(snapshots):
    time_dev, points = snapshots.shape
    n_aa = lax.axis_size("aa")
    n_ba = lax.axis_size("ba")
    pts_dev = points // (n_aa * n_ba)
    block_len = time_dev * n_ba
    u = lax.axis_index("ba")
    table = spectral_rows(block_len, points, u * time_dev, time_dev)
    arranged = snapshots.reshape(time_dev, n_aa, n_ba, pts_dev)
    partial = jnp.einsum("savq,sgf->vgfaq", arranged, table, precision=lax.Precision.HIGHEST)
    block_spec = lax.psum_scatter(partial, "ba", scatter_dimension=0, tiled=True)
    spectra = lax.all_to_all(block_spec, "aa", split_axis=3, concat_axis=0, tiled=True)
    blocks = spectra.shape[0]
    columns = 2 * blocks
    cols = jnp.transpose(spectra.reshape(blocks, 2, FREQS, pts_dev), (2, 0, 1, 3)).reshape(
        FREQS, columns, pts_dev
    )
    product = jnp.einsum("fip,fjp->fij", cols, cols, precision=lax.Precision.HIGHEST)
    gram_sum = lax.psum(product, ("aa", "ba"))
    lower_factor = jnp.linalg.cholesky(gram_sum)
    identity = jnp.broadcast_to(jnp.eye(columns, dtype=gram_sum.dtype), lower_factor.shape)
    inverse = lax.linalg.triangular_solve(lower_factor, identity, left_side=True, lower=True)
    pod_modes = math.sqrt(points) * jnp.einsum(
        "fij,fjp->fip", inverse, cols, precision=lax.Precision.HIGHEST
    )
    return (jnp.swapaxes(lower_factor, 1, 2), pod_modes)


def solution(mesh):
    placed = (P(("aa", "ba"), None),)
    return jax.shard_map(
        local,
        mesh=mesh,
        in_specs=placed,
        out_specs=(P(), P(None, None, ("aa", "ba"))),
        check_vma=False,
    )
```

time: 675 us -> 479 us (0.71)
  blocking collectives: 195 us -> 0 us
  local copies, waits for them, and re-layouts: 19 us -> 11 us
    all_to_all x1 -> x0, blocking collectives: 195 us -> none  [local(): lax.all_to_all(snapshots, 'aa', split_axis=1, concat_axis=0, tiled=True)]
    unnamed x1 -> x3, waiting for transfers between devices: 0.02 us -> 79.3 us
    all_to_all x1, waiting for transfers between devices: 92.2 us -> 13.8 us  [local(): lax.all_to_all(block_spec, 'aa', split_axis=3, concat_axis=0, tiled=True)]
    all_to_all x2 -> x0, local copies, waits for them, and re-layouts: 9.74 us -> none  [the longest x1 5.77 us: local(): lax.all_to_all(lax.all_to_all(snapshots, 'aa', split_axis=1, concat_axis=...]
  transfers between devices with their start and end apart: 2 -> 3, of which waited for: 2 -> 3; matrix products, arithmetic and copies ran while one was open for 0% -> 0% of each run, Pallas kernels for 0% -> 0%
where the time goes in v1:
time: 479 us
  waiting for transfers between devices  342 us (71%)
  other arithmetic  88.3 us (18%)
  between operations  14.8 us (3%)
  matrix products  12.9 us (3%)
  local copies, waits for them, and re-layouts  11 us (2%)
  starting transfers between devices  9.8 us (2%)
    psum x1, waiting for transfers between devices, local(): gram_sum = lax.psum(product, ('aa', 'ba'))  249 us
    unnamed x3, waiting for transfers between devices  79.3 us
    another operation x4, other arithmetic, local(): lower_factor = jnp.linalg.cholesky(gram_sum)  47.1 us
    another operation x2, other arithmetic, local(): lax.linalg.triangular_solve(lower_factor, identity, left_side=True, lower...  39.4 us
    all_to_all x1, waiting for transfers between devices, local(): lax.all_to_all(block_spec, 'aa', split_axis=3, concat_axis=0, tiled=True)  13.8 us
  transfers between devices with their start and end apart: 3, of which 3 were waited for; matrix products, arithmetic and copies ran while one was open for 0% of the time, Pallas kernels for 0%

profile of v1, /device:TPU:1, one launch (start us, length us, event | category | flops | bytes accessed | tf_op | source)
XLA Modules:
  0.0 478.6 jit_solution(12910174082356562652)
XLA Ops:
  7.2 0.0 all-reduce.6.cloned.1.call-start
  7.3 0.6 multiply_reduce_fusion
  8.6 5.9 %copy.38 = f32[4,8,256,256]{3,2,1,0:T(8,128)S(1)} copy(f32[4,8,256,256]{3,1,2,0:T(8,128)} %bitcast.42) | data formatting | bytes 16777216
  14.6 0.1 multiply_multiply_fusion.1
  14.7 9.2 %fusion.3 = f32[8,2,8,32,256]{4,2,0,3,1:T(8,128)} fusion(f32[32,32,8,256]{3,2,1,0:T(8,128)S(1)} %bitcast.41, f32[32,1,8]{0,2,1:T(8,128)S(1)} %get-tuple-element.13, f32[32,1,8]{0,2,1:T(8,128)S(1)} %get-tuple-element.12), kind=kOutput, calls=%fused_computation.3 | convolution fusion | flops 402653696 | bytes 12584960 | tf_op jit(solution)/shard_map/savq,sgf->vgfaq/dot_general | solution.py:36
  23.9 0.0 all-reduce.6.cloned.1.call-update
  23.9 0.6 dynamic-slice
  24.5 79.2 %all-reduce.6.cloned.1.call-done = f32[8,2,8,32,256]{4,2,0,3,1:T(8,128)} async-done(((f32[8,2,8,32,256]{4,2,0,3,1:T(8,128)}), f32[8,2,8,32,256]{4,2,0,3,1:T(8,128)}) %all-reduce.6.cloned.1.call-update) | async-done | bytes 4194320
  103.7 1.7 constant_dynamic-slice_fusion
  105.4 0.9 copy.25
  106.3 9.5 %all-to-all-start = ((f32[1,2,8,32,256]{4,2,0,1,3:T(8,128)}), f32[1,2,8,32,256]{4,2,0,1,3:T(8,128)S(1)}, u32[]{:S(2)}, u32[]{:S(2)}) async-start(f32[1,2,8,32,256]{4,2,0,1,3:T(8,128)} %copy.25), calls=%async_computation | async-start | bytes 1048576 | tf_op jit(solution)/shard_map/all_to_all | solution.py:38
  115.8 0.2 all-reduce.4.cloned.1.call-start
  116.1 13.8 %all-to-all-done = f32[1,2,8,32,256]{4,2,0,1,3:T(8,128)S(1)} async-done(((f32[1,2,8,32,256]{4,2,0,1,3:T(8,128)}), f32[1,2,8,32,256]{4,2,0,1,3:T(8,128)S(1)}, u32[]{:S(2)}, u32[]{:S(2)}) %all-to-all-start) | async-done | bytes 524320 | tf_op jit(solution)/shard_map/all_to_all | solution.py:38
  129.9 1.6 fusion.7
  131.5 248.6 %all-reduce.4.cloned.1.call-done = f32[8,64,64]{1,2,0:T(8,128)} async-done(((f32[8,64,64]{1,2,0:T(8,128)}), f32[8,64,64]{1,2,0:T(8,128)}) %all-reduce.4.cloned.1.call-update) | async-done | bytes 131088 | tf_op jit(solution)/shard_map/psum | solution.py:45
  380.2 1.1 copy.29
  381.3 1.0 fusion.11
  382.3 46.9 %custom-call.7 = f32[8,64,64]{2,1,0:T(8,128)S(1)} custom-call(f32[8,64,64]{2,1,0:T(8,128)S(1)} %fusion.11), custom_call_target="Cholesky" | custom-call | tf_op jit(solution)/shard_map/jit(cholesky)/cholesky | solution.py:46
  429.2 0.1 compare_reduce_fusion
  429.3 0.1 select_bitcast_fusion
  429.4 39.3 %custom-call.8 = f32[8,1,64,64]{2,3,1,0:T(8,128)S(1)} custom-call(f32[8,1,64,64]{3,2,1,0:T(8,128)S(1)} %get-tuple-element.10), custom_call_target="InvertDiagBlocksLowerTriangular" | custom-call | tf_op jit(solution)/shard_map/triangular_solve | solution.py:48
  468.8 0.6 fusion.9
  469.4 1.5 convolution_multiply_fusion
  470.9 0.8 copy.32
  (10 shorter events, 0.1 us)
Async XLA Ops:
  7.2 96.6 %all-reduce.6.cloned.1.call-start = ((), (), s32[]{:S(2)}) async-start(), calls=%async_computation.2 | async-start | bytes 8388608
  14.7 9.2 %copy-start = (u32[256]{0:T(256)S(1)}, u32[256]{0:T(256)}, u32[]{:S(2)}) copy-start(u32[256]{0:T(256)} %constant.81) | copy-start | bytes 3076
  106.3 23.6 %all-to-all-start = ((f32[1,2,8,32,256]{4,2,0,1,3:T(8,128)}), f32[1,2,8,32,256]{4,2,0,1,3:T(8,128)S(1)}, u32[]{:S(2)}, u32[]{:S(2)}) async-start(f32[1,2,8,32,256]{4,2,0,1,3:T(8,128)} %copy.25), calls=%async_computation | async-start | bytes 1048576 | tf_op jit(solution)/shard_map/all_to_all | solution.py:38
  115.8 264.3 %all-reduce.4.cloned.1.call-start = ((), (), s32[]{:S(2)}) async-start(), calls=%async_computation.1 | async-start | bytes 524288 | tf_op jit(solution)/shard_map/psum | solution.py:45
Sparse Core Ops, SparseCore 0:
  24.0 79.6 all-reduce.5
  131.6 248.4 all-reduce.3

commit v2 on v1

--- a/solution.py
+++ b/solution.py
@@ -24,6 +24,13 @@
     return jnp.stack([cosine, sine], axis=1)
 
 
+def all_sum(x, axes, count):
+    pieces = x.reshape(count, x.size // count)
+    mine = lax.all_to_all(pieces, axes, 0, 0, tiled=True).sum(0, keepdims=True)
+    spread = jnp.broadcast_to(mine, pieces.shape)
+    return lax.all_to_all(spread, axes, 0, 0, tiled=True).reshape(x.shape)
+
+
 def local(snapshots):
     time_dev, points = snapshots.shape
     n_aa = lax.axis_size("aa")
@@ -34,7 +41,7 @@
     table = spectral_rows(block_len, points, u * time_dev, time_dev)
     arranged = snapshots.reshape(time_dev, n_aa, n_ba, pts_dev)
     partial = jnp.einsum("savq,sgf->vgfaq", arranged, table, precision=lax.Precision.HIGHEST)
-    block_spec = lax.psum_scatter(partial, "ba", scatter_dimension=0, tiled=True)
+    block_spec = lax.all_to_all(partial, "ba", 0, 0, tiled=True).sum(0, keepdims=True)
     spectra = lax.all_to_all(block_spec, "aa", split_axis=3, concat_axis=0, tiled=True)
     blocks = spectra.shape[0]
     columns = 2 * blocks
@@ -42,7 +49,7 @@
         FREQS, columns, pts_dev
     )
     product = jnp.einsum("fip,fjp->fij", cols, cols, precision=lax.Precision.HIGHEST)
-    gram_sum = lax.psum(product, ("aa", "ba"))
+    gram_sum = all_sum(product, ("aa", "ba"), n_aa * n_ba)
     lower_factor = jnp.linalg.cholesky(gram_sum)
     identity = jnp.broadcast_to(jnp.eye(columns, dtype=gram_sum.dtype), lower_factor.shape)
     inverse = lax.linalg.triangular_solve(lower_factor, identity, left_side=True, lower=True)

time: 479 us -> 236 us (0.49)
  waiting for transfers between devices: 342 us -> 13 us
  blocking collectives: 0 us -> 103 us
  between operations: 14.8 us -> 1.49 us
    psum x1 -> x0, waiting for transfers between devices: 249 us -> none  [local(): gram_sum = lax.psum(product, ('aa', 'ba'))]
    all_to_all x0 -> x3, blocking collectives: none -> 103 us  [the longest x1 55.8 us: local(): lax.all_to_all(partial, 'ba', 0, 0, tiled=True).sum(0, keepdims=True)]
    unnamed x3 -> x0, waiting for transfers between devices: 79.3 us -> none
  transfers between devices with their start and end apart: 3 -> 1, of which waited for: 3 -> 1; matrix products, arithmetic and copies ran while one was open for 0% -> 0% of each run, Pallas kernels for 0% -> 0%
where the time goes in v2:
time: 236 us; the launch traced here: 235 us
  blocking collectives  103 us (44%)
  other arithmetic  91.1 us (39%)
  waiting for transfers between devices  13 us (6%)
  matrix products  11.6 us (5%)
  local copies, waits for them, and re-layouts  9.75 us (4%)
  starting transfers between devices  5.49 us (2%)
    all_to_all x1, blocking collectives, local(): lax.all_to_all(partial, 'ba', 0, 0, tiled=True).sum(0, keepdims=True)  55.8 us
    another operation x4, other arithmetic, local(): lower_factor = jnp.linalg.cholesky(gram_sum)  47.1 us
    another operation x2, other arithmetic, local(): lax.linalg.triangular_solve(lower_factor, identity, left_side=True, lower...  39.4 us
    all_to_all x1, blocking collectives, local(): lax.all_to_all(block_spec, 'aa', split_axis=3, concat_axis=0, tiled=True)  25.5 us
    all_to_all x1, blocking collectives, all_sum(): mine = lax.all_to_all(pieces, axes, 0, 0, tiled=True).sum(0, keepdims=True)  21.6 us
    all_to_all x1, waiting for transfers between devices, all_sum(): return lax.all_to_all(spread, axes, 0, 0, tiled=True).reshape(x.shape)  13 us
    dot_general x1, matrix products, local(): jnp.einsum('savq,sgf->vgfaq', arranged, table, precision=lax.Precision.HI...  9.02 us
    unnamed x2, local copies, waits for them, and re-layouts  6.78 us
  transfers between devices with their start and end apart: 1, of which 1 were waited for; matrix products, arithmetic and copies ran while one was open for 0% of the time, Pallas kernels for 0%

profile of v2, /device:TPU:1, one launch (start us, length us, event | category | flops | bytes accessed | tf_op | source)
XLA Modules:
  0.0 235.4 jit_solution(7419673230543097286)
XLA Ops:
  0.7 0.6 multiply_reduce_fusion
  2.0 5.9 %copy.30 = f32[4,8,256,256]{3,2,1,0:T(8,128)S(1)} copy(f32[4,8,256,256]{3,1,2,0:T(8,128)} %bitcast.40) | data formatting | bytes 16777216
  8.1 9.0 %fusion.3 = f32[8,2,8,32,256]{4,2,0,3,1:T(8,128)S(1)} fusion(f32[32,32,8,256]{3,2,1,0:T(8,128)S(1)} %bitcast.39, f32[32,1,8]{0,2,1:T(8,128)S(1)} %get-tuple-element.13, f32[32,1,8]{0,2,1:T(8,128)S(1)} %get-tuple-element.12), kind=kOutput, calls=%fused_computation.3 | convolution fusion | flops 402653696 | bytes 12584960 | tf_op jit(solution)/shard_map/savq,sgf->vgfaq/dot_general | solution.py:43
  17.1 0.4 copy.19
  17.6 55.8 %all_to_all.35 = f32[8,2,8,32,256]{4,2,3,1,0:T(8,128)} all-to-all(f32[8,2,8,32,256]{4,2,3,1,0:T(8,128)S(1)} %copy.19), channel_id=1, replica_groups=mesh['aa'=32,'ba'=8] {'ba'}, dimensions={0} | all-to-all | bytes 8388608 | tf_op jit(solution)/shard_map/all_to_all | solution.py:44
  73.4 2.5 %reduce_sum.28 = f32[2,8,32,256]{3,1,2,0:T(8,128)S(1)} reduce(f32[8,2,8,32,256]{4,2,3,1,0:T(8,128)} %all_to_all.35, f32[]{:T(128)} %constant.73.clone.1), dimensions={0}, to_apply=%region_1.2 | reduce | flops 917504 | bytes 4718596 | tf_op jit(solution)/shard_map/reduce_sum | solution.py:44
  75.9 0.4 copy.21
  76.3 25.5 %all_to_all.36 = f32[1,2,8,32,256]{4,1,2,0,3:T(2,128)S(1)} all-to-all(f32[1,2,8,32,256]{4,1,2,0,3:T(2,128)S(1)} %copy.21), channel_id=1, replica_groups=mesh['aa'=32,'ba'=8] {'aa'}, dimensions={3} | all-to-all | bytes 1048576 | tf_op jit(solution)/shard_map/all_to_all | solution.py:45
  101.8 0.2 copy.22
  102.0 0.4 reshape.227
  102.4 0.6 fusion.19
  103.1 21.6 %all_to_all.37 = f32[256,1,128]{2,1,0:T(1,128)S(1)} all-to-all(f32[256,1,128]{2,1,0:T(1,128)S(1)} %bitcast.43), channel_id=1, replica_groups=mesh['aa'=32,'ba'=8] {'aa','ba'}, dimensions={0} | all-to-all | bytes 262144 | tf_op jit(solution)/shard_map/all_to_all | solution.py:29
  124.7 0.3 reduce_sum.29
  125.0 0.7 broadcast_in_dim.26
  125.7 5.5 %all-to-all-start.3 = ((f32[256,1,128]{2,1,0:T(1,128)}), f32[256,1,128]{2,1,0:T(1,128)S(1)}, u32[]{:S(2)}, u32[]{:S(2)}) async-start(f32[256,1,128]{2,1,0:T(1,128)} %broadcast_in_dim.26), calls=%async_computation.3 | async-start | bytes 262144 | tf_op jit(solution)/shard_map/all_to_all | solution.py:31
  131.3 13.0 %all-to-all-done.3 = f32[256,1,128]{2,1,0:T(1,128)S(1)} async-done(((f32[256,1,128]{2,1,0:T(1,128)}), f32[256,1,128]{2,1,0:T(1,128)S(1)}, u32[]{:S(2)}, u32[]{:S(2)}) %all-to-all-start.3) | async-done | bytes 131104 | tf_op jit(solution)/shard_map/all_to_all | solution.py:31
  144.3 0.5 broadcast.285
  144.8 0.9 reduce.10
  145.9 0.1 copy.24
  146.0 46.9 %custom-call.7 = f32[8,64,64]{2,1,0:T(8,128)S(1)} custom-call(f32[8,64,64]{2,1,0:T(8,128)S(1)} %fusion.8), custom_call_target="Cholesky" | custom-call | tf_op jit(solution)/shard_map/jit(cholesky)/cholesky | solution.py:53
  193.2 39.3 %custom-call.8 = f32[8,1,64,64]{2,3,1,0:T(8,128)S(1)} custom-call(f32[8,1,64,64]{3,2,1,0:T(8,128)S(1)} %get-tuple-element.10), custom_call_target="InvertDiagBlocksLowerTriangular" | custom-call | tf_op jit(solution)/shard_map/triangular_solve | solution.py:55
  232.6 0.6 fusion.6
  233.2 1.4 convolution_multiply_fusion
  234.5 0.8 copy.26
  (13 shorter events, 0.7 us)
Async XLA Ops:
  125.7 18.6 %all-to-all-start.3 = ((f32[256,1,128]{2,1,0:T(1,128)}), f32[256,1,128]{2,1,0:T(1,128)S(1)}, u32[]{:S(2)}, u32[]{:S(2)}) async-start(f32[256,1,128]{2,1,0:T(1,128)} %broadcast_in_dim.26), calls=%async_computation.3 | async-start | bytes 262144 | tf_op jit(solution)/shard_map/all_to_all | solution.py:31

commit v3 on v2

--- a/solution.py
+++ b/solution.py
@@ -3,6 +3,8 @@
 import jax
 import jax.numpy as jnp
 from jax import lax
+from jax.experimental import pallas as pl
+from jax.experimental.pallas import tpu as pltpu
 from jax.sharding import PartitionSpec as P
 
 FREQS = 8
@@ -22,6 +24,40 @@
     cosine = window[:, None] * jnp.cos(phase_turns) * norm_scale
     sine = -window[:, None] * jnp.sin(phase_turns) * norm_scale
     return jnp.stack([cosine, sine], axis=1)
+
+
+def _factor_kernel(a_ref, upper_ref, inv_ref, m_ref):
+    freqs, n, _ = a_ref.shape
+    rows = lax.broadcasted_iota(jnp.int32, (n, 2 * n), 0)
+    lanes = lax.broadcasted_iota(jnp.int32, (n, 2 * n), 1)
+    for f in range(freqs):
+        m_ref[f] = jnp.concatenate([a_ref[f], (rows[:, :n] == lanes[:, :n]).astype(jnp.float32)], axis=1)
+
+    def step(j, carry):
+        for f in range(freqs):
+            mf = m_ref[f]
+            pivot_row = m_ref[f, pl.ds(j, 1), :]
+            pivot = jnp.sum(jnp.where(lanes[:1] == j, pivot_row, 0.0), axis=1, keepdims=True)
+            root = jnp.sqrt(pivot)
+            new_row = pivot_row / root
+            column = jnp.sum(jnp.where(lanes == j, mf, 0.0), axis=1, keepdims=True) / root
+            updated = jnp.where(rows > j, mf - column * new_row, mf)
+            m_ref[f] = jnp.where(rows == j, new_row, updated)
+        return carry
+
+    lax.fori_loop(0, n, step, 0)
+    for f in range(freqs):
+        mf = m_ref[f]
+        upper_ref[f] = jnp.where(rows[:, :n] <= lanes[:, :n], mf[:, :n], 0.0)
+        inv_ref[f] = mf[:, n:]
+
+def factor(gram):
+    freqs, n, _ = gram.shape
+    return pl.pallas_call(
+        _factor_kernel,
+        out_shape=(jax.ShapeDtypeStruct(gram.shape, gram.dtype), jax.ShapeDtypeStruct(gram.shape, gram.dtype)),
+        scratch_shapes=[pltpu.VMEM((freqs, n, 2 * n), jnp.float32)],
+    )(gram)
 
 
 def all_sum(x, axes, count):
@@ -50,13 +86,11 @@
     )
     product = jnp.einsum("fip,fjp->fij", cols, cols, precision=lax.Precision.HIGHEST)
     gram_sum = all_sum(product, ("aa", "ba"), n_aa * n_ba)
-    lower_factor = jnp.linalg.cholesky(gram_sum)
-    identity = jnp.broadcast_to(jnp.eye(columns, dtype=gram_sum.dtype), lower_factor.shape)
-    inverse = lax.linalg.triangular_solve(lower_factor, identity, left_side=True, lower=True)
+    upper_factor, inverse = factor(gram_sum)
     pod_modes = math.sqrt(points) * jnp.einsum(
         "fij,fjp->fip", inverse, cols, precision=lax.Precision.HIGHEST
     )
-    return (jnp.swapaxes(lower_factor, 1, 2), pod_modes)
+    return (upper_factor, pod_modes)
 
 
 def solution(mesh):

time: 236 us -> 202 us (0.86)
  other arithmetic: 91.1 us -> 4.58 us
  Pallas kernels: 0 us -> 53.4 us
  blocking collectives: 103 us -> 121 us
  waiting for transfers between devices: 13 us -> 0 us
  starting transfers between devices: 5.49 us -> 0 us
    another operation x6 -> x0, other arithmetic: 86.5 us -> none  [the longest x4 47.1 us: local(): lower_factor = jnp.linalg.cholesky(gram_sum)]
    pallas_call x0 -> x1, Pallas kernels: none -> 53.4 us  [factor(): pl.pallas_call(_factor_kernel, out_shape=(jax.ShapeDtypeStruct(gram.shape...]
    all_to_all x0 -> x1, blocking collectives: none -> 18.3 us  [all_sum(): return lax.all_to_all(spread, axes, 0, 0, tiled=True).reshape(x.shape)]
    all_to_all x1 -> x0, waiting for transfers between devices: 13 us -> none  [all_sum(): return lax.all_to_all(spread, axes, 0, 0, tiled=True).reshape(x.shape)]
    all_to_all x1 -> x0, starting transfers between devices: 5.49 us -> none  [all_sum(): return lax.all_to_all(spread, axes, 0, 0, tiled=True).reshape(x.shape)]
    unnamed x2 -> x1, local copies, waits for them, and re-layouts: 6.78 us -> 5.95 us
  transfers between devices with their start and end apart: 1 -> 0, of which waited for: 1 -> 0; matrix products, arithmetic and copies ran while one was open for 0% -> 0% of each run, Pallas kernels for 0% -> 0%
where the time goes in v3:
time: 202 us; the launch traced here: 201 us
  blocking collectives  121 us (60%)
  Pallas kernels  53.4 us (26%)
  matrix products  11.9 us (6%)
  local copies, waits for them, and re-layouts  8.84 us (4%)
  other arithmetic  4.58 us (2%)
    all_to_all x1, blocking collectives, local(): lax.all_to_all(partial, 'ba', 0, 0, tiled=True).sum(0, keepdims=True)  55.8 us
    pallas_call x1, Pallas kernels, factor(): pl.pallas_call(_factor_kernel, out_shape=(jax.ShapeDtypeStruct(gram.shape...  53.4 us
    all_to_all x1, blocking collectives, local(): lax.all_to_all(block_spec, 'aa', split_axis=3, concat_axis=0, tiled=True)  25.5 us
    all_to_all x1, blocking collectives, all_sum(): mine = lax.all_to_all(pieces, axes, 0, 0, tiled=True).sum(0, keepdims=True)  21.6 us
    all_to_all x1, blocking collectives, all_sum(): return lax.all_to_all(spread, axes, 0, 0, tiled=True).reshape(x.shape)  18.3 us
    dot_general x1, matrix products, local(): jnp.einsum('savq,sgf->vgfaq', arranged, table, precision=lax.Precision.HI...  9.02 us
    unnamed x1, local copies, waits for them, and re-layouts  5.95 us

profile of v3, /device:TPU:1, one launch (start us, length us, event | category | flops | bytes accessed | tf_op | source)
XLA Modules:
  0.0 201.4 jit_solution(14832021415087454293)
XLA Ops:
  0.7 0.6 multiply_reduce_fusion
  2.0 5.9 %copy.12 = f32[4,8,256,256]{3,2,1,0:T(8,128)S(1)} copy(f32[4,8,256,256]{3,1,2,0:T(8,128)} %bitcast.29) | data formatting | bytes 16777216
  8.0 0.1 multiply_multiply_fusion.1
  8.1 9.0 %fusion.3 = f32[8,2,8,32,256]{4,2,0,3,1:T(8,128)S(1)} fusion(f32[32,32,8,256]{3,2,1,0:T(8,128)S(1)} %bitcast.28, f32[32,1,8]{0,2,1:T(8,128)S(1)} %get-tuple-element.7, f32[32,1,8]{0,2,1:T(8,128)S(1)} %get-tuple-element.6), kind=kOutput, calls=%fused_computation.3 | convolution fusion | flops 402653696 | bytes 12584960 | tf_op jit(solution)/shard_map/savq,sgf->vgfaq/dot_general | solution.py:79
  17.1 0.4 copy.5
  17.6 55.8 %all_to_all.35 = f32[8,2,8,32,256]{4,2,3,1,0:T(8,128)} all-to-all(f32[8,2,8,32,256]{4,2,3,1,0:T(8,128)S(1)} %copy.5), channel_id=1, replica_groups=mesh['aa'=32,'ba'=8] {'ba'}, dimensions={0} | all-to-all | bytes 8388608 | tf_op jit(solution)/shard_map/all_to_all | solution.py:80
  73.4 2.5 %reduce_sum.28 = f32[2,8,32,256]{3,1,2,0:T(8,128)S(1)} reduce(f32[8,2,8,32,256]{4,2,3,1,0:T(8,128)} %all_to_all.35, f32[]{:T(128)} %constant.34.clone.1), dimensions={0}, to_apply=%region_1.2 | reduce | flops 917504 | bytes 4718596 | tf_op jit(solution)/shard_map/reduce_sum | solution.py:80
  75.9 0.4 copy.7
  76.3 25.5 %all_to_all.36 = f32[1,2,8,32,256]{4,1,2,0,3:T(2,128)S(1)} all-to-all(f32[1,2,8,32,256]{4,1,2,0,3:T(2,128)S(1)} %copy.7), channel_id=1, replica_groups=mesh['aa'=32,'ba'=8] {'aa'}, dimensions={3} | all-to-all | bytes 1048576 | tf_op jit(solution)/shard_map/all_to_all | solution.py:81
  101.8 0.2 copy.8
  102.0 0.4 reshape.217
  102.4 0.6 fusion.13
  103.0 0.1 all_to_all.28
  103.1 21.6 %all_to_all.37 = f32[256,1,128]{2,1,0:T(1,128)S(1)} all-to-all(f32[256,1,128]{2,1,0:T(1,128)S(1)} %bitcast.32), channel_id=1, replica_groups=mesh['aa'=32,'ba'=8] {'aa','ba'}, dimensions={0} | all-to-all | bytes 262144 | tf_op jit(solution)/shard_map/all_to_all | solution.py:65
  124.7 0.3 reduce_sum.29
  125.0 0.1 broadcast_in_dim.5
  125.1 18.3 %all_to_all.38 = f32[256,1,128]{2,1,0:T(1,128)S(1)} all-to-all(f32[256,1,128]{2,1,0:T(1,128)S(1)} %broadcast_in_dim.5), channel_id=1, replica_groups=mesh['aa'=32,'ba'=8] {'aa','ba'}, dimensions={0} | all-to-all | bytes 262144 | tf_op jit(solution)/shard_map/all_to_all | solution.py:67
  143.4 0.5 broadcast.238
  143.9 0.9 reduce.4
  144.9 0.8 reshape.218.a_ref
  145.7 53.4 %shard_map.30 = (f32[8,64,64]{2,1,0:T(8,128)}, f32[8,64,64]{2,1,0:T(8,128)}) custom-call(f32[8,64,64]{2,1,0:T(8,128)} %reshape.218.a_ref), custom_call_target="tpu_custom_call" | custom-call | tf_op jit(solution)/shard_map/pallas_call | solution.py:56
  199.1 2.3 %convolution_multiply_fusion = f32[8,64,256]{2,1,0:T(8,128)} fusion(f32[8,64,64]{2,1,0:T(8,128)} %get-tuple-element.5, f32[8,64,256]{2,1,0:T(8,128)S(1)} %reshape.217), kind=kOutput, calls=%fused_computation.4 | convolution fusion | flops 100794368 | bytes 1179648 | tf_op jit(solution)/shard_map/fij,fjp->fip/dot_general | solution.py:90
  (3 shorter events, 0.1 us)

commit v4 on v3

--- a/solution.py
+++ b/solution.py
@@ -38,11 +38,11 @@
             mf = m_ref[f]
             pivot_row = m_ref[f, pl.ds(j, 1), :]
             pivot = jnp.sum(jnp.where(lanes[:1] == j, pivot_row, 0.0), axis=1, keepdims=True)
-            root = jnp.sqrt(pivot)
-            new_row = pivot_row / root
-            column = jnp.sum(jnp.where(lanes == j, mf, 0.0), axis=1, keepdims=True) / root
-            updated = jnp.where(rows > j, mf - column * new_row, mf)
-            m_ref[f] = jnp.where(rows == j, new_row, updated)
+            scaled_row = pivot_row / pivot
+            column = jnp.sum(jnp.where(lanes == j, mf, 0.0), axis=1, keepdims=True)
+            column = jnp.where(rows[:, :1] > j, column, 0.0)
+            m_ref[f] = mf - column * scaled_row
+            m_ref[f, pl.ds(j, 1), :] = pivot_row / jnp.sqrt(pivot)
         return carry
 
     lax.fori_loop(0, n, step, 0)

time: 202 us -> 198 us (0.980)
  Pallas kernels: 53.4 us -> 49.2 us
    pallas_call x1, Pallas kernels: 53.4 us -> 49.2 us  [factor(): pl.pallas_call(_factor_kernel, out_shape=(jax.ShapeDtypeStruct(gram.shape...]
where the time goes in v4:
time: 198 us; the launch traced here: 197 us
  blocking collectives  121 us (61%)
  Pallas kernels  49.2 us (25%)
  matrix products  11.9 us (6%)
  local copies, waits for them, and re-layouts  8.84 us (4%)
  other arithmetic  4.58 us (2%)
    all_to_all x1, blocking collectives, local(): lax.all_to_all(partial, 'ba', 0, 0, tiled=True).sum(0, keepdims=True)  55.8 us
    pallas_call x1, Pallas kernels, factor(): pl.pallas_call(_factor_kernel, out_shape=(jax.ShapeDtypeStruct(gram.shape...  49.2 us
    all_to_all x1, blocking collectives, local(): lax.all_to_all(block_spec, 'aa', split_axis=3, concat_axis=0, tiled=True)  25.5 us
    all_to_all x1, blocking collectives, all_sum(): mine = lax.all_to_all(pieces, axes, 0, 0, tiled=True).sum(0, keepdims=True)  21.6 us
    all_to_all x1, blocking collectives, all_sum(): return lax.all_to_all(spread, axes, 0, 0, tiled=True).reshape(x.shape)  18.3 us
    dot_general x1, matrix products, local(): jnp.einsum('savq,sgf->vgfaq', arranged, table, precision=lax.Precision.HI...  9.02 us
    unnamed x1, local copies, waits for them, and re-layouts  5.95 us

profile of v4, /device:TPU:1, one launch (start us, length us, event | category | flops | bytes accessed | tf_op | source)
XLA Modules:
  0.0 197.2 jit_solution(1188703198394066681)
XLA Ops:
  0.7 0.6 multiply_reduce_fusion
  2.0 5.9 %copy.12 = f32[4,8,256,256]{3,2,1,0:T(8,128)S(1)} copy(f32[4,8,256,256]{3,1,2,0:T(8,128)} %bitcast.29) | data formatting | bytes 16777216
  8.0 0.1 multiply_multiply_fusion.1
  8.1 9.0 %fusion.3 = f32[8,2,8,32,256]{4,2,0,3,1:T(8,128)S(1)} fusion(f32[32,32,8,256]{3,2,1,0:T(8,128)S(1)} %bitcast.28, f32[32,1,8]{0,2,1:T(8,128)S(1)} %get-tuple-element.7, f32[32,1,8]{0,2,1:T(8,128)S(1)} %get-tuple-element.6), kind=kOutput, calls=%fused_computation.3 | convolution fusion | flops 402653696 | bytes 12584960 | tf_op jit(solution)/shard_map/savq,sgf->vgfaq/dot_general | solution.py:79
  17.1 0.4 copy.5
  17.6 55.8 %all_to_all.35 = f32[8,2,8,32,256]{4,2,3,1,0:T(8,128)} all-to-all(f32[8,2,8,32,256]{4,2,3,1,0:T(8,128)S(1)} %copy.5), channel_id=1, replica_groups=mesh['aa'=32,'ba'=8] {'ba'}, dimensions={0} | all-to-all | bytes 8388608 | tf_op jit(solution)/shard_map/all_to_all | solution.py:80
  73.4 2.5 %reduce_sum.28 = f32[2,8,32,256]{3,1,2,0:T(8,128)S(1)} reduce(f32[8,2,8,32,256]{4,2,3,1,0:T(8,128)} %all_to_all.35, f32[]{:T(128)} %constant.34.clone.1), dimensions={0}, to_apply=%region_1.2 | reduce | flops 917504 | bytes 4718596 | tf_op jit(solution)/shard_map/reduce_sum | solution.py:80
  75.9 0.4 copy.7
  76.3 25.5 %all_to_all.36 = f32[1,2,8,32,256]{4,1,2,0,3:T(2,128)S(1)} all-to-all(f32[1,2,8,32,256]{4,1,2,0,3:T(2,128)S(1)} %copy.7), channel_id=1, replica_groups=mesh['aa'=32,'ba'=8] {'aa'}, dimensions={3} | all-to-all | bytes 1048576 | tf_op jit(solution)/shard_map/all_to_all | solution.py:81
  101.8 0.2 copy.8
  102.0 0.4 reshape.217
  102.4 0.6 fusion.13
  103.0 0.1 all_to_all.28
  103.1 21.6 %all_to_all.37 = f32[256,1,128]{2,1,0:T(1,128)S(1)} all-to-all(f32[256,1,128]{2,1,0:T(1,128)S(1)} %bitcast.32), channel_id=1, replica_groups=mesh['aa'=32,'ba'=8] {'aa','ba'}, dimensions={0} | all-to-all | bytes 262144 | tf_op jit(solution)/shard_map/all_to_all | solution.py:65
  124.7 0.3 reduce_sum.29
  125.0 0.1 broadcast_in_dim.5
  125.1 18.3 %all_to_all.38 = f32[256,1,128]{2,1,0:T(1,128)S(1)} all-to-all(f32[256,1,128]{2,1,0:T(1,128)S(1)} %broadcast_in_dim.5), channel_id=1, replica_groups=mesh['aa'=32,'ba'=8] {'aa','ba'}, dimensions={0} | all-to-all | bytes 262144 | tf_op jit(solution)/shard_map/all_to_all | solution.py:67
  143.4 0.5 broadcast.238
  143.9 0.9 reduce.4
  144.9 0.8 reshape.218.a_ref
  145.7 49.2 %shard_map.30 = (f32[8,64,64]{2,1,0:T(8,128)}, f32[8,64,64]{2,1,0:T(8,128)}) custom-call(f32[8,64,64]{2,1,0:T(8,128)} %reshape.218.a_ref), custom_call_target="tpu_custom_call" | custom-call | tf_op jit(solution)/shard_map/pallas_call | solution.py:56
  194.9 2.3 %convolution_multiply_fusion = f32[8,64,256]{2,1,0:T(8,128)} fusion(f32[8,64,64]{2,1,0:T(8,128)} %get-tuple-element.5, f32[8,64,256]{2,1,0:T(8,128)S(1)} %reshape.217), kind=kOutput, calls=%fused_computation.4 | convolution fusion | flops 100794368 | bytes 1179648 | tf_op jit(solution)/shard_map/fij,fjp->fip/dot_general | solution.py:90
  (3 shorter events, 0.1 us)

commit v5 on v4

--- a/solution.py
+++ b/solution.py
@@ -28,28 +28,26 @@
 
 def _factor_kernel(a_ref, upper_ref, inv_ref, m_ref):
     freqs, n, _ = a_ref.shape
-    rows = lax.broadcasted_iota(jnp.int32, (n, 2 * n), 0)
-    lanes = lax.broadcasted_iota(jnp.int32, (n, 2 * n), 1)
-    for f in range(freqs):
-        m_ref[f] = jnp.concatenate([a_ref[f], (rows[:, :n] == lanes[:, :n]).astype(jnp.float32)], axis=1)
+    rows = lax.broadcasted_iota(jnp.int32, (freqs, n, 2 * n), 1)
+    lanes = lax.broadcasted_iota(jnp.int32, (freqs, n, 2 * n), 2)
+    m_ref[...] = jnp.concatenate([a_ref[...], (rows[:, :, :n] == lanes[:, :, :n]).astype(jnp.float32)], axis=2)
 
     def step(j, carry):
-        for f in range(freqs):
-            mf = m_ref[f]
-            pivot_row = m_ref[f, pl.ds(j, 1), :]
-            pivot = jnp.sum(jnp.where(lanes[:1] == j, pivot_row, 0.0), axis=1, keepdims=True)
-            scaled_row = pivot_row / pivot
-            column = jnp.sum(jnp.where(lanes == j, mf, 0.0), axis=1, keepdims=True)
-            column = jnp.where(rows[:, :1] > j, column, 0.0)
-            m_ref[f] = mf - column * scaled_row
-            m_ref[f, pl.ds(j, 1), :] = pivot_row / jnp.sqrt(pivot)
+        m = m_ref[...]
+        pivot_row = m_ref[:, pl.ds(j, 1), :]
+        pivot = jnp.sum(jnp.where(lanes[:, :1] == j, pivot_row, 0.0), axis=2, keepdims=True)
+        scaled_row = pivot_row / pivot
+        column = jnp.sum(jnp.where(lanes == j, m, 0.0), axis=2, keepdims=True)
+        column = jnp.where(rows[:, :, :1] > j, column, 0.0)
+        m_ref[...] = m - column * scaled_row
+        m_ref[:, pl.ds(j, 1), :] = pivot_row / jnp.sqrt(pivot)
         return carry
 
     lax.fori_loop(0, n, step, 0)
-    for f in range(freqs):
-        mf = m_ref[f]
-        upper_ref[f] = jnp.where(rows[:, :n] <= lanes[:, :n], mf[:, :n], 0.0)
-        inv_ref[f] = mf[:, n:]
+    m = m_ref[...]
+    upper_ref[...] = jnp.where(rows[:, :, :n] <= lanes[:, :, :n], m[:, :, :n], 0.0)
+    inv_ref[...] = m[:, :, n:]
+
 
 def factor(gram):
     freqs, n, _ = gram.shape

time: 198 us -> 161 us (0.81)
  Pallas kernels: 49.2 us -> 12.2 us
    pallas_call x1, Pallas kernels: 49.2 us -> 12.2 us  [factor(): pl.pallas_call(_factor_kernel, out_shape=(jax.ShapeDtypeStruct(gram.shape...]
where the time goes in v5:
time: 161 us; the launch traced here: 160 us
  blocking collectives  121 us (75%)
  Pallas kernels  12.2 us (8%)
  matrix products  11.9 us (7%)
  local copies, waits for them, and re-layouts  8.84 us (5%)
  other arithmetic  4.58 us (3%)
    all_to_all x1, blocking collectives, local(): lax.all_to_all(partial, 'ba', 0, 0, tiled=True).sum(0, keepdims=True)  55.8 us
    all_to_all x1, blocking collectives, local(): lax.all_to_all(block_spec, 'aa', split_axis=3, concat_axis=0, tiled=True)  25.5 us
    all_to_all x1, blocking collectives, all_sum(): mine = lax.all_to_all(pieces, axes, 0, 0, tiled=True).sum(0, keepdims=True)  21.6 us
    all_to_all x1, blocking collectives, all_sum(): return lax.all_to_all(spread, axes, 0, 0, tiled=True).reshape(x.shape)  18.3 us
    pallas_call x1, Pallas kernels, factor(): pl.pallas_call(_factor_kernel, out_shape=(jax.ShapeDtypeStruct(gram.shape...  12.2 us
    dot_general x1, matrix products, local(): jnp.einsum('savq,sgf->vgfaq', arranged, table, precision=lax.Precision.HI...  9.02 us
    unnamed x1, local copies, waits for them, and re-layouts  5.95 us

profile of v5, /device:TPU:1, one launch (start us, length us, event | category | flops | bytes accessed | tf_op | source)
XLA Modules:
  0.0 160.3 jit_solution(6374985464275368682)
XLA Ops:
  0.7 0.6 multiply_reduce_fusion
  2.0 5.9 %copy.12 = f32[4,8,256,256]{3,2,1,0:T(8,128)S(1)} copy(f32[4,8,256,256]{3,1,2,0:T(8,128)} %bitcast.29) | data formatting | bytes 16777216
  8.0 0.1 multiply_multiply_fusion.1
  8.1 9.0 %fusion.3 = f32[8,2,8,32,256]{4,2,0,3,1:T(8,128)S(1)} fusion(f32[32,32,8,256]{3,2,1,0:T(8,128)S(1)} %bitcast.28, f32[32,1,8]{0,2,1:T(8,128)S(1)} %get-tuple-element.7, f32[32,1,8]{0,2,1:T(8,128)S(1)} %get-tuple-element.6), kind=kOutput, calls=%fused_computation.3 | convolution fusion | flops 402653696 | bytes 12584960 | tf_op jit(solution)/shard_map/savq,sgf->vgfaq/dot_general | solution.py:77
  17.1 0.4 copy.5
  17.6 55.8 %all_to_all.35 = f32[8,2,8,32,256]{4,2,3,1,0:T(8,128)} all-to-all(f32[8,2,8,32,256]{4,2,3,1,0:T(8,128)S(1)} %copy.5), channel_id=1, replica_groups=mesh['aa'=32,'ba'=8] {'ba'}, dimensions={0} | all-to-all | bytes 8388608 | tf_op jit(solution)/shard_map/all_to_all | solution.py:78
  73.4 2.5 %reduce_sum.28 = f32[2,8,32,256]{3,1,2,0:T(8,128)S(1)} reduce(f32[8,2,8,32,256]{4,2,3,1,0:T(8,128)} %all_to_all.35, f32[]{:T(128)} %constant.34.clone.1), dimensions={0}, to_apply=%region_1.2 | reduce | flops 917504 | bytes 4718596 | tf_op jit(solution)/shard_map/reduce_sum | solution.py:78
  75.9 0.4 copy.7
  76.3 25.5 %all_to_all.36 = f32[1,2,8,32,256]{4,1,2,0,3:T(2,128)S(1)} all-to-all(f32[1,2,8,32,256]{4,1,2,0,3:T(2,128)S(1)} %copy.7), channel_id=1, replica_groups=mesh['aa'=32,'ba'=8] {'aa'}, dimensions={3} | all-to-all | bytes 1048576 | tf_op jit(solution)/shard_map/all_to_all | solution.py:79
  101.8 0.2 copy.8
  102.0 0.4 reshape.217
  102.4 0.6 fusion.13
  103.0 0.1 all_to_all.28
  103.1 21.6 %all_to_all.37 = f32[256,1,128]{2,1,0:T(1,128)S(1)} all-to-all(f32[256,1,128]{2,1,0:T(1,128)S(1)} %bitcast.32), channel_id=1, replica_groups=mesh['aa'=32,'ba'=8] {'aa','ba'}, dimensions={0} | all-to-all | bytes 262144 | tf_op jit(solution)/shard_map/all_to_all | solution.py:63
  124.7 0.3 reduce_sum.29
  125.0 0.1 broadcast_in_dim.5
  125.1 18.3 %all_to_all.38 = f32[256,1,128]{2,1,0:T(1,128)S(1)} all-to-all(f32[256,1,128]{2,1,0:T(1,128)S(1)} %broadcast_in_dim.5), channel_id=1, replica_groups=mesh['aa'=32,'ba'=8] {'aa','ba'}, dimensions={0} | all-to-all | bytes 262144 | tf_op jit(solution)/shard_map/all_to_all | solution.py:65
  143.4 0.5 broadcast.238
  143.9 0.9 reduce.4
  144.9 0.8 reshape.218.a_ref
  145.7 12.2 %shard_map.30 = (f32[8,64,64]{2,1,0:T(8,128)}, f32[8,64,64]{2,1,0:T(8,128)}) custom-call(f32[8,64,64]{2,1,0:T(8,128)} %reshape.218.a_ref), custom_call_target="tpu_custom_call" | custom-call | tf_op jit(solution)/shard_map/pallas_call | solution.py:54
  157.9 2.3 %convolution_multiply_fusion = f32[8,64,256]{2,1,0:T(8,128)} fusion(f32[8,64,64]{2,1,0:T(8,128)} %get-tuple-element.5, f32[8,64,256]{2,1,0:T(8,128)S(1)} %reshape.217), kind=kOutput, calls=%fused_computation.4 | convolution fusion | flops 100794368 | bytes 1179648 | tf_op jit(solution)/shard_map/fij,fjp->fip/dot_general | solution.py:88
  (3 shorter events, 0.1 us)

commit v6 on v5

--- a/solution.py
+++ b/solution.py
@@ -65,6 +65,25 @@
     return lax.all_to_all(spread, axes, 0, 0, tiled=True).reshape(x.shape)
 
 
+def sum_over_ba(partial, n_ba):
+    u = lax.axis_index("ba")
+    cores = 2
+    if n_ba % cores:
+        return lax.all_to_all(partial, "ba", 0, 0, tiled=True).sum(0, keepdims=True)
+    chips = n_ba // cores
+    y, c = u // cores, u % cores
+    parts = partial.reshape(chips, cores, *partial.shape[1:])
+    send = lax.dynamic_index_in_dim(parts, cores - 1 - c, axis=1, keepdims=False)
+    keep = lax.dynamic_index_in_dim(parts, c, axis=1, keepdims=False)
+    chip_sum = keep + lax.ppermute(send, "ba", [(i, i ^ 1) for i in range(n_ba)])
+    total = lax.dynamic_index_in_dim(chip_sum, y, axis=0, keepdims=True)
+    for shift in range(1, chips):
+        out = lax.dynamic_index_in_dim(chip_sum, (y + shift) % chips, axis=0, keepdims=True)
+        perm = [(i, ((i // cores + shift) % chips) * cores + i % cores) for i in range(n_ba)]
+        total = total + lax.ppermute(out, "ba", perm)
+    return total
+
+
 def local(snapshots):
     time_dev, points = snapshots.shape
     n_aa = lax.axis_size("aa")
@@ -75,7 +94,7 @@
     table = spectral_rows(block_len, points, u * time_dev, time_dev)
     arranged = snapshots.reshape(time_dev, n_aa, n_ba, pts_dev)
     partial = jnp.einsum("savq,sgf->vgfaq", arranged, table, precision=lax.Precision.HIGHEST)
-    block_spec = lax.all_to_all(partial, "ba", 0, 0, tiled=True).sum(0, keepdims=True)
+    block_spec = sum_over_ba(partial, n_ba)
     spectra = lax.all_to_all(block_spec, "aa", split_axis=3, concat_axis=0, tiled=True)
     blocks = spectra.shape[0]
     columns = 2 * blocks

time: 161 us -> 152 us (0.944)
  blocking collectives: 121 us -> 65.7 us
  waiting for transfers between devices: 0 us -> 29.7 us
  local copies, waits for them, and re-layouts: 8.84 us -> 15.6 us
  starting transfers between devices: 0 us -> 5.36 us
  matrix products: 11.9 us -> 15.8 us
    all_to_all x1 -> x0, blocking collectives: 55.8 us -> none  [local(): lax.all_to_all(partial, 'ba', 0, 0, tiled=True).sum(0, keepdims=True)]
    ppermute x0 -> x4, waiting for transfers between devices: none -> 29.7 us  [the longest x3 25.5 us: sum_over_ba(): total = total + lax.ppermute(out, 'ba', perm)]
    unnamed x1 -> x4, local copies, waits for them, and re-layouts: 5.95 us -> 13.1 us
    ppermute x0 -> x4, starting transfers between devices: none -> 5.36 us  [the longest x1 3.24 us: sum_over_ba(): lax.ppermute(send, 'ba', [(i, i ^ 1) for i in range(n_ba)])]
    add x0 -> x2, other arithmetic: none -> 4.09 us  [the longest x1 2.9 us: sum_over_ba(): keep + lax.ppermute(send, 'ba', [(i, i ^ 1) for i in range(n_ba)])]
    dot_general x1, matrix products: 9.02 us -> 12.4 us  [local(): jnp.einsum('savq,sgf->vgfaq', arranged, table, precision=lax.Precision.HI...]
    reduce_sum x1 -> x0, other arithmetic: 2.52 us -> none  [local(): lax.all_to_all(partial, 'ba', 0, 0, tiled=True).sum(0, keepdims=True)]
    all_to_all x1, blocking collectives: 25.5 us -> 27.3 us  [local(): lax.all_to_all(block_spec, 'aa', split_axis=3, concat_axis=0, tiled=True)]
  transfers between devices with their start and end apart: 0 -> 4, of which waited for: 0 -> 4; matrix products, arithmetic and copies ran while one was open for 0% -> 0% of each run, Pallas kernels for 0% -> 0%
where the time goes in v6:
time: 152 us
  blocking collectives  65.7 us (43%)
  waiting for transfers between devices  29.7 us (20%)
  matrix products  15.8 us (10%)
  local copies, waits for them, and re-layouts  15.6 us (10%)
  Pallas kernels  12.2 us (8%)
  other arithmetic  6.15 us (4%)
  starting transfers between devices  5.36 us (4%)
    all_to_all x1, blocking collectives, local(): lax.all_to_all(block_spec, 'aa', split_axis=3, concat_axis=0, tiled=True)  27.3 us
    ppermute x3, waiting for transfers between devices, sum_over_ba(): total = total + lax.ppermute(out, 'ba', perm)  25.5 us
    all_to_all x1, blocking collectives, all_sum(): mine = lax.all_to_all(pieces, axes, 0, 0, tiled=True).sum(0, keepdims=True)  20.1 us
    all_to_all x1, blocking collectives, all_sum(): return lax.all_to_all(spread, axes, 0, 0, tiled=True).reshape(x.shape)  18.3 us
    unnamed x4, local copies, waits for them, and re-layouts  13.1 us
    dot_general x1, matrix products, local(): jnp.einsum('savq,sgf->vgfaq', arranged, table, precision=lax.Precision.HI...  12.4 us
    pallas_call x1, Pallas kernels, factor(): pl.pallas_call(_factor_kernel, out_shape=(jax.ShapeDtypeStruct(gram.shape...  12.2 us
    ppermute x1, waiting for transfers between devices, sum_over_ba(): lax.ppermute(send, 'ba', [(i, i ^ 1) for i in range(n_ba)])  4.13 us
  transfers between devices with their start and end apart: 4, of which 4 were waited for; matrix products, arithmetic and copies ran while one was open for 0% of the time, Pallas kernels for 0%

profile of v6, /device:TPU:1, one launch (start us, length us, event | category | flops | bytes accessed | tf_op | source)
XLA Modules:
  0.0 152.0 jit_solution(9692431245797043803)
XLA Ops:
  0.6 0.6 multiply_reduce_fusion
  1.3 9.2 %copy.18 = f32[4,8,256,256]{3,2,1,0:T(8,128)} copy(f32[4,8,256,256]{3,1,2,0:T(8,128)} %bitcast.34) | data formatting | bytes 16777216
  11.3 12.4 %fusion = f32[2,8,32,8,256]{4,1,3,2,0:T(8,128)S(1)} fusion(f32[32,32,8,256]{3,2,1,0:T(8,128)} %bitcast.32, f32[32,1,8]{0,2,1:T(8,128)S(1)} %get-tuple-element.12, f32[32,1,8]{0,2,1:T(8,128)S(1)} %get-tuple-element.11), kind=kOutput, calls=%fused_computation | convolution fusion | flops 402653696 | bytes 12584960 | tf_op jit(solution)/shard_map/savq,sgf->vgfaq/dot_general | solution.py:96
  23.8 0.6 constant_dynamic-slice_fusion.4
  24.4 2.6 %copy.31 = f32[4,1,2,8,32,256]{5,4,3,2,0,1:T(8,128)} copy(f32[4,1,2,8,32,256]{5,3,1,0,4,2:T(8,128)S(1)} %get-tuple-element.7) | data formatting | bytes 4194304
  27.0 3.2 %collective-permute-start = (f32[4,2,8,32,256]{4,3,2,1,0:T(8,128)}, f32[4,2,8,32,256]{4,3,2,1,0:T(8,128)}, u32[]{:S(2)}, u32[]{:S(2)}) collective-permute-start(f32[4,2,8,32,256]{4,3,2,1,0:T(8,128)} %bitcast.31), channel_id=1, source_target_pairs={{0,1},{1,0},{2,3},{3,2},{4,5},{5,4},{6,7},{7,6},{8,9},{9,8},{10,11... | collective-permute-start | bytes 6291464 | tf_op jit(solution)/shard_map/ppermute | solution.py:78
  30.2 4.1 %collective-permute-done = f32[4,2,8,32,256]{4,3,2,1,0:T(8,128)} collective-permute-done((f32[4,2,8,32,256]{4,3,2,1,0:T(8,128)}, f32[4,2,8,32,256]{4,3,2,1,0:T(8,128)}, u32[]{:S(2)}, u32[]{:S(2)}) %collective-permute-start) | collective-permute-done | bytes 2097184 | tf_op jit(solution)/shard_map/ppermute | solution.py:78
  34.3 2.9 %fusion.3 = f32[4,2,8,32,256]{4,3,2,1,0:T(8,128)S(1)} fusion(f32[4,2,8,32,256]{4,3,2,1,0:T(8,128)} %collective-permute-done, f32[4,1,2,8,32,256]{5,3,1,0,4,2:T(8,128)S(1)} %get-tuple-element.6), kind=kLoop, calls=%fused_computation.5 | loop fusion | flops 524288 | bytes 6291456 | tf_op jit(solution)/shard_map/add | solution.py:78
  37.2 1.3 copy-done
  38.7 1.1 collective-permute-start.3
  40.2 0.7 collective-permute-start.1
  40.9 11.1 %collective-permute-done.3 = f32[1,2,8,32,256]{4,3,2,1,0:T(8,128)S(1)} collective-permute-done((f32[1,2,8,32,256]{4,3,2,1,0:T(8,128)S(1)}, f32[1,2,8,32,256]{4,3,2,1,0:T(8,128)S(1)}, u32[]{:S(2)}, u32[]{:S(2)}) %collective-permute-start.3) | collective-permute-done | bytes 524320 | tf_op jit(solution)/shard_map/ppermute | solution.py:83
  52.0 2.2 %collective-permute-done.2 = f32[1,2,8,32,256]{4,3,2,1,0:T(8,128)S(1)} collective-permute-done((f32[1,2,8,32,256]{4,3,2,1,0:T(8,128)S(1)}, f32[1,2,8,32,256]{4,3,2,1,0:T(8,128)S(1)}, u32[]{:S(2)}, u32[]{:S(2)}) %collective-permute-start.2) | collective-permute-done | bytes 524320 | tf_op jit(solution)/shard_map/ppermute | solution.py:83
  54.2 12.2 %collective-permute-done.1 = f32[1,2,8,32,256]{4,3,2,1,0:T(8,128)S(1)} collective-permute-done((f32[1,2,8,32,256]{4,3,2,1,0:T(8,128)S(1)}, f32[1,2,8,32,256]{4,3,2,1,0:T(8,128)S(1)}, u32[]{:S(2)}, u32[]{:S(2)}) %collective-permute-start.1) | collective-permute-done | bytes 524320 | tf_op jit(solution)/shard_map/ppermute | solution.py:83
  66.4 1.2 add_add_fusion
  67.9 27.3 %all_to_all.30 = f32[1,2,8,32,256]{4,2,1,0,3:T(8,128)S(1)} all-to-all(f32[1,2,8,32,256]{4,2,1,0,3:T(8,128)S(1)} %copy.11), channel_id=1, replica_groups=mesh['aa'=32,'ba'=8] {'aa'}, dimensions={3} | all-to-all | bytes 1048576 | tf_op jit(solution)/shard_map/all_to_all | solution.py:98
  95.2 0.9 fusion.5
  96.2 20.1 %all_to_all.31 = f32[256,1,128]{2,1,0:T(1,128)S(1)} all-to-all(f32[256,1,128]{2,1,0:T(1,128)S(1)} %bitcast.37), channel_id=1, replica_groups=mesh['aa'=32,'ba'=8] {'aa','ba'}, dimensions={0} | all-to-all | bytes 262144 | tf_op jit(solution)/shard_map/all_to_all | solution.py:63
  116.7 18.3 %all_to_all.32 = f32[256,1,128]{2,1,0:T(1,128)S(1)} all-to-all(f32[256,1,128]{2,1,0:T(1,128)S(1)} %broadcast_in_dim.2), channel_id=1, replica_groups=mesh['aa'=32,'ba'=8] {'aa','ba'}, dimensions={0} | all-to-all | bytes 262144 | tf_op jit(solution)/shard_map/all_to_all | solution.py:65
  135.0 0.5 broadcast.243
  135.5 0.9 reduce.4
  136.5 0.8 reshape.222.a_ref
  137.3 12.2 %shard_map.30 = (f32[8,64,64]{2,1,0:T(8,128)}, f32[8,64,64]{2,1,0:T(8,128)}) custom-call(f32[8,64,64]{2,1,0:T(8,128)} %reshape.222.a_ref), custom_call_target="tpu_custom_call" | custom-call | tf_op jit(solution)/shard_map/pallas_call | solution.py:54
  149.5 2.4 %convolution_multiply_fusion = f32[8,64,256]{2,1,0:T(8,128)} fusion(f32[8,64,64]{2,1,0:T(8,128)} %get-tuple-element.5, f32[8,64,256]{2,0,1:T(8,128)S(1)} %bitcast.36), kind=kOutput, calls=%fused_computation.6 | convolution fusion | flops 100794368 | bytes 1179648 | tf_op jit(solution)/shard_map/fij,fjp->fip/dot_general | solution.py:107
  (11 shorter events, 1.5 us)
Async XLA Ops:
  27.0 7.4 %collective-permute-start = (f32[4,2,8,32,256]{4,3,2,1,0:T(8,128)}, f32[4,2,8,32,256]{4,3,2,1,0:T(8,128)}, u32[]{:S(2)}, u32[]{:S(2)}) collective-permute-start(f32[4,2,8,32,256]{4,3,2,1,0:T(8,128)} %bitcast.31), channel_id=1, source_target_pairs={{0,1},{1,0},{2,3},{3,2},{4,5},{5,4},{6,7},{7,6},{8,9},{9,8},{10,11... | collective-permute-start | bytes 6291464 | tf_op jit(solution)/shard_map/ppermute | solution.py:78
  37.2 1.3 copy-start
  38.7 13.2 %collective-permute-start.3 = (f32[1,2,8,32,256]{4,3,2,1,0:T(8,128)S(1)}, f32[1,2,8,32,256]{4,3,2,1,0:T(8,128)S(1)}, u32[]{:S(2)}, u32[]{:S(2)}) collective-permute-start(f32[1,2,8,32,256]{4,3,2,1,0:T(8,128)S(1)} %get-tuple-element.9), channel_id=1, source_target_pairs={{0,6},{1,7},{2,0},{3,1},{4,2},{5,3},{6,4},{7,5},{8,14},{9,15},{10,... | collective-permute-start | bytes 1572872 | tf_op jit(solution)/shard_map/ppermute | solution.py:83
  39.8 14.4 %collective-permute-start.2 = (f32[1,2,8,32,256]{4,3,2,1,0:T(8,128)S(1)}, f32[1,2,8,32,256]{4,3,2,1,0:T(8,128)S(1)}, u32[]{:S(2)}, u32[]{:S(2)}) collective-permute-start(f32[1,2,8,32,256]{4,3,2,1,0:T(8,128)S(1)} %get-tuple-element.10), channel_id=1, source_target_pairs={{0,4},{1,5},{2,6},{3,7},{4,0},{5,1},{6,2},{7,3},{8,12},{9,13},{10,... | collective-permute-start | bytes 1572872 | tf_op jit(solution)/shard_map/ppermute | solution.py:83
  40.2 26.2 %collective-permute-start.1 = (f32[1,2,8,32,256]{4,3,2,1,0:T(8,128)S(1)}, f32[1,2,8,32,256]{4,3,2,1,0:T(8,128)S(1)}, u32[]{:S(2)}, u32[]{:S(2)}) collective-permute-start(f32[1,2,8,32,256]{4,3,2,1,0:T(8,128)S(1)} %get-tuple-element.8), channel_id=1, source_target_pairs={{0,2},{1,3},{2,4},{3,5},{4,6},{5,7},{6,0},{7,1},{8,10},{9,11},{10,... | collective-permute-start | bytes 1572872 | tf_op jit(solution)/shard_map/ppermute | solution.py:83

commit v7 on v6

--- a/solution.py
+++ b/solution.py
@@ -65,6 +65,34 @@
     return lax.all_to_all(spread, axes, 0, 0, tiled=True).reshape(x.shape)
 
 
+def _dft_kernel(table_ref, snap_ref, out_ref):
+    n_ba, a_step, _, pts_dev = out_ref.shape
+    res = jnp.dot(table_ref[...], snap_ref[...], precision=lax.Precision.HIGHEST,
+                  preferred_element_type=jnp.float32)
+    for a in range(a_step):
+        for v in range(n_ba):
+            start = (a * n_ba + v) * pts_dev
+            out_ref[v, a] = res[:, start:start + pts_dev]
+
+
+def partial_dft(table_t, snapshots, n_aa, n_ba):
+    a_step = math.gcd(4, n_aa)
+    rows, time_dev = table_t.shape
+    points = snapshots.shape[1]
+    pts_dev = points // (n_aa * n_ba)
+    width = a_step * n_ba * pts_dev
+    return pl.pallas_call(
+        _dft_kernel,
+        grid=(n_aa // a_step,),
+        in_specs=[
+            pl.BlockSpec((rows, time_dev), lambda i: (0, 0)),
+            pl.BlockSpec((time_dev, width), lambda i: (0, i)),
+        ],
+        out_specs=pl.BlockSpec((n_ba, a_step, rows, pts_dev), lambda i: (0, i, 0, 0)),
+        out_shape=jax.ShapeDtypeStruct((n_ba, n_aa, rows, pts_dev), jnp.float32),
+    )(table_t, snapshots)
+
+
 def sum_over_ba(partial, n_ba):
     u = lax.axis_index("ba")
     cores = 2
@@ -92,13 +120,13 @@
     block_len = time_dev * n_ba
     u = lax.axis_index("ba")
     table = spectral_rows(block_len, points, u * time_dev, time_dev)
-    arranged = snapshots.reshape(time_dev, n_aa, n_ba, pts_dev)
-    partial = jnp.einsum("savq,sgf->vgfaq", arranged, table, precision=lax.Precision.HIGHEST)
+    table_t = jnp.transpose(table, (2, 1, 0)).reshape(2 * FREQS, time_dev)
+    partial = partial_dft(table_t, snapshots, n_aa, n_ba)
     block_spec = sum_over_ba(partial, n_ba)
-    spectra = lax.all_to_all(block_spec, "aa", split_axis=3, concat_axis=0, tiled=True)
+    spectra = lax.all_to_all(block_spec, "aa", split_axis=1, concat_axis=0, tiled=True)
     blocks = spectra.shape[0]
     columns = 2 * blocks
-    cols = jnp.transpose(spectra.reshape(blocks, 2, FREQS, pts_dev), (2, 0, 1, 3)).reshape(
+    cols = jnp.transpose(spectra.reshape(blocks, FREQS, 2, pts_dev), (1, 0, 2, 3)).reshape(
         FREQS, columns, pts_dev
     )
     product = jnp.einsum("fip,fjp->fij", cols, cols, precision=lax.Precision.HIGHEST)

time: 152 us -> 142 us (0.934)
  matrix products: 15.8 us -> 2.92 us
  Pallas kernels: 12.2 us -> 22.3 us
  local copies, waits for them, and re-layouts: 15.6 us -> 9.2 us
  waiting for transfers between devices: 29.7 us -> 26.8 us
    dot_general x1 -> x0, matrix products: 12.4 us -> none  [local(): jnp.einsum('savq,sgf->vgfaq', arranged, table, precision=lax.Precision.HI...]
    unnamed x4 -> x2, local copies, waits for them, and re-layouts: 13.1 us -> 1.33 us
    pallas_call x0 -> x1, Pallas kernels: none -> 10.1 us  [partial_dft(): pl.pallas_call(_dft_kernel, grid=(n_aa // a_step,), in_specs=[pl.BlockSpe...]
    all_to_all x1, blocking collectives: 20.1 us -> 23.3 us  [all_sum(): mine = lax.all_to_all(pieces, axes, 0, 0, tiled=True).sum(0, keepdims=True)]
    ppermute x3, waiting for transfers between devices: 25.5 us -> 22.6 us  [sum_over_ba(): total = total + lax.ppermute(out, 'ba', perm)]
    dynamic_slice x1, local copies, waits for them, and re-layouts: 0.61 us -> 2.97 us  [sum_over_ba(): keep = lax.dynamic_index_in_dim(parts, c, axis=1, keepdims=False)]
    all_to_all x1, blocking collectives: 27.3 us -> 25.4 us  [local(): lax.all_to_all(block_spec, 'aa', split_axis=1, concat_axis=0, tiled=True)]
    dynamic_slice x0 -> x1, local copies, waits for them, and re-layouts: none -> 1.59 us  [sum_over_ba(): lax.dynamic_index_in_dim(parts, cores - 1 - c, axis=1, keepdims=False)]
where the time goes in v7:
time: 142 us
  blocking collectives  67 us (47%)
  waiting for transfers between devices  26.8 us (19%)
  Pallas kernels  22.3 us (16%)
  local copies, waits for them, and re-layouts  9.2 us (6%)
  starting transfers between devices  6.56 us (5%)
  other arithmetic  5.4 us (4%)
  matrix products  2.92 us (2%)
  between operations  1.44 us (1%)
    all_to_all x1, blocking collectives, local(): lax.all_to_all(block_spec, 'aa', split_axis=1, concat_axis=0, tiled=True)  25.4 us
    all_to_all x1, blocking collectives, all_sum(): mine = lax.all_to_all(pieces, axes, 0, 0, tiled=True).sum(0, keepdims=True)  23.3 us
    ppermute x3, waiting for transfers between devices, sum_over_ba(): total = total + lax.ppermute(out, 'ba', perm)  22.6 us
    all_to_all x1, blocking collectives, all_sum(): return lax.all_to_all(spread, axes, 0, 0, tiled=True).reshape(x.shape)  18.3 us
    pallas_call x1, Pallas kernels, factor(): pl.pallas_call(_factor_kernel, out_shape=(jax.ShapeDtypeStruct(gram.shape...  12.2 us
    pallas_call x1, Pallas kernels, partial_dft(): pl.pallas_call(_dft_kernel, grid=(n_aa // a_step,), in_specs=[pl.BlockSpe...  10.1 us
    ppermute x1, waiting for transfers between devices, sum_over_ba(): lax.ppermute(send, 'ba', [(i, i ^ 1) for i in range(n_ba)])  4.13 us
    ppermute x3, starting transfers between devices, sum_over_ba(): total = total + lax.ppermute(out, 'ba', perm)  3.32 us
  transfers between devices with their start and end apart: 4, of which 4 were waited for; matrix products, arithmetic and copies ran while one was open for 0% of the time, Pallas kernels for 0%

profile of v7, /device:TPU:1, one launch (start us, length us, event | category | flops | bytes accessed | tf_op | source)
XLA Modules:
  0.0 141.6 jit_solution(17603219520024322805)
XLA Ops:
  0.7 0.6 multiply_reduce_fusion
  2.2 0.6 copy.11
  2.8 10.1 %shard_map.30 = f32[8,32,16,256]{3,2,1,0:T(8,128)} custom-call(f32[16,32]{1,0:T(8,128)} %bitcast.20, f32[32,65536]{1,0:T(8,128)} %snap_ref.1), custom_call_target="tpu_custom_call" | custom-call | tf_op jit(solution)/shard_map/pallas_call | solution.py:84
  12.8 3.0 %constant_dynamic-slice_fusion.4 = (f32[4,1,32,16,256]{4,3,2,1,0:T(8,128)S(1)}, f32[4,1,32,16,256]{4,3,2,1,0:T(8,128)S(1)}) fusion(f32[4,2,32,16,256]{4,3,2,1,0:T(8,128)} %bitcast.17, s32[]{:T(128)S(6)} %select_n.62, s32[]{:T(128)S(6)} %select_n.63), kind=kLoop, calls=%fused_computation.19 | loop fusion | bytes 8388616 | tf_op jit(solution)/shard_map/jit(dynamic_index_in_dim)/dynamic_slice | solution.py:105
  15.8 1.6 %copy.19 = f32[4,1,32,16,256]{4,3,0,2,1:T(8,128)} copy(f32[4,1,32,16,256]{4,3,2,1,0:T(8,128)S(1)} %get-tuple-element.7) | data formatting | bytes 4194304 | tf_op jit(solution)/shard_map/jit(dynamic_index_in_dim)/dynamic_slice | solution.py:104
  17.4 3.2 %collective-permute-start = (f32[4,32,16,256]{3,2,0,1:T(8,128)}, f32[4,32,16,256]{3,2,0,1:T(8,128)}, u32[]{:S(2)}, u32[]{:S(2)}) collective-permute-start(f32[4,32,16,256]{3,2,0,1:T(8,128)} %bitcast.16), channel_id=1, source_target_pairs={{0,1},{1,0},{2,3},{3,2},{4,5},{5,4},{6,7},{7,6},{8,9},{9,8},{10,11... | collective-permute-start | bytes 6291464 | tf_op jit(solution)/shard_map/ppermute | solution.py:106
  20.7 4.1 %collective-permute-done = f32[4,32,16,256]{3,2,0,1:T(8,128)} collective-permute-done((f32[4,32,16,256]{3,2,0,1:T(8,128)}, f32[4,32,16,256]{3,2,0,1:T(8,128)}, u32[]{:S(2)}, u32[]{:S(2)}) %collective-permute-start) | collective-permute-done | bytes 2097184 | tf_op jit(solution)/shard_map/ppermute | solution.py:106
  24.8 2.1 %bitcast_add_fusion = f32[4,32,16,256]{3,2,0,1:T(8,128)S(1)} fusion(f32[4,32,16,256]{3,2,0,1:T(8,128)} %collective-permute-done, f32[4,1,32,16,256]{4,3,2,1,0:T(8,128)S(1)} %get-tuple-element.6), kind=kLoop, calls=%fused_computation | loop fusion | flops 524288 | bytes 6291456 | tf_op jit(solution)/shard_map/add | solution.py:106
  26.9 1.3 copy-done
  28.4 2.2 %collective-permute-start.2 = (f32[1,32,16,256]{3,2,0,1:T(8,128)S(1)}, f32[1,32,16,256]{3,2,0,1:T(8,128)S(1)}, u32[]{:S(2)}, u32[]{:S(2)}) collective-permute-start(f32[1,32,16,256]{3,2,0,1:T(8,128)S(1)} %get-tuple-element.10), channel_id=1, source_target_pairs={{0,4},{1,5},{2,6},{3,7},{4,0},{5,1},{6,2},{7,3},{8,12},{9,13},{10,... | collective-permute-start | bytes 1572872 | tf_op jit(solution)/shard_map/ppermute | solution.py:111
  30.6 1.1 collective-permute-start.3
  31.7 11.6 %collective-permute-done.1 = f32[1,32,16,256]{3,2,0,1:T(8,128)S(1)} collective-permute-done((f32[1,32,16,256]{3,2,0,1:T(8,128)S(1)}, f32[1,32,16,256]{3,2,0,1:T(8,128)S(1)}, u32[]{:S(2)}, u32[]{:S(2)}) %collective-permute-start.1) | collective-permute-done | bytes 524320 | tf_op jit(solution)/shard_map/ppermute | solution.py:111
  43.2 10.3 %collective-permute-done.2 = f32[1,32,16,256]{3,2,0,1:T(8,128)S(1)} collective-permute-done((f32[1,32,16,256]{3,2,0,1:T(8,128)S(1)}, f32[1,32,16,256]{3,2,0,1:T(8,128)S(1)}, u32[]{:S(2)}, u32[]{:S(2)}) %collective-permute-start.2) | collective-permute-done | bytes 524320 | tf_op jit(solution)/shard_map/ppermute | solution.py:111
  53.6 0.7 collective-permute-done.3
  54.3 1.3 add_add_fusion
  55.6 25.4 %all_to_all.24 = f32[1,32,16,256]{3,2,0,1:T(8,128)S(1)} all-to-all(f32[1,32,16,256]{3,2,0,1:T(8,128)S(1)} %add_add_fusion), channel_id=1, replica_groups=mesh['aa'=32,'ba'=8] {'aa'}, dimensions={1} | all-to-all | bytes 1048576 | tf_op jit(solution)/shard_map/all_to_all | solution.py:126
  82.1 0.6 fusion.4
  82.8 23.3 %all_to_all.25 = f32[256,1,128]{2,1,0:T(1,128)S(1)} all-to-all(f32[256,1,128]{2,1,0:T(1,128)S(1)} %bitcast.19), channel_id=1, replica_groups=mesh['aa'=32,'ba'=8] {'aa','ba'}, dimensions={0} | all-to-all | bytes 262144 | tf_op jit(solution)/shard_map/all_to_all | solution.py:63
  106.4 18.3 %all_to_all.26 = f32[256,1,128]{2,1,0:T(1,128)S(1)} all-to-all(f32[256,1,128]{2,1,0:T(1,128)S(1)} %broadcast_in_dim.2), channel_id=1, replica_groups=mesh['aa'=32,'ba'=8] {'aa','ba'}, dimensions={0} | all-to-all | bytes 262144 | tf_op jit(solution)/shard_map/all_to_all | solution.py:65
  124.8 0.5 broadcast.243
  125.3 0.9 reduce.4
  126.2 0.8 reshape.225.a_ref
  127.0 12.2 %shard_map.31 = (f32[8,64,64]{2,1,0:T(8,128)}, f32[8,64,64]{2,1,0:T(8,128)}) custom-call(f32[8,64,64]{2,1,0:T(8,128)} %reshape.225.a_ref), custom_call_target="tpu_custom_call" | custom-call | tf_op jit(solution)/shard_map/pallas_call | solution.py:54
  139.3 2.3 %convolution_multiply_fusion = f32[8,64,256]{2,1,0:T(8,128)} fusion(f32[8,64,64]{2,1,0:T(8,128)} %get-tuple-element.5, f32[8,64,256]{2,1,0:T(8,128)S(1)} %reshape.224), kind=kOutput, calls=%fused_computation.2 | convolution fusion | flops 100794368 | bytes 1179648 | tf_op jit(solution)/shard_map/fij,fjp->fip/dot_general | solution.py:135
  (14 shorter events, 1.9 us)
Async XLA Ops:
  17.4 7.4 %collective-permute-start = (f32[4,32,16,256]{3,2,0,1:T(8,128)}, f32[4,32,16,256]{3,2,0,1:T(8,128)}, u32[]{:S(2)}, u32[]{:S(2)}) collective-permute-start(f32[4,32,16,256]{3,2,0,1:T(8,128)} %bitcast.16), channel_id=1, source_target_pairs={{0,1},{1,0},{2,3},{3,2},{4,5},{5,4},{6,7},{7,6},{8,9},{9,8},{10,11... | collective-permute-start | bytes 6291464 | tf_op jit(solution)/shard_map/ppermute | solution.py:106
  26.9 1.3 copy-start
  28.3 14.9 %collective-permute-start.1 = (f32[1,32,16,256]{3,2,0,1:T(8,128)S(1)}, f32[1,32,16,256]{3,2,0,1:T(8,128)S(1)}, u32[]{:S(2)}, u32[]{:S(2)}) collective-permute-start(f32[1,32,16,256]{3,2,0,1:T(8,128)S(1)} %get-tuple-element.8), channel_id=1, source_target_pairs={{0,2},{1,3},{2,4},{3,5},{4,6},{5,7},{6,0},{7,1},{8,10},{9,11},{10,... | collective-permute-start | bytes 1572872 | tf_op jit(solution)/shard_map/ppermute | solution.py:111
  28.4 25.1 %collective-permute-start.2 = (f32[1,32,16,256]{3,2,0,1:T(8,128)S(1)}, f32[1,32,16,256]{3,2,0,1:T(8,128)S(1)}, u32[]{:S(2)}, u32[]{:S(2)}) collective-permute-start(f32[1,32,16,256]{3,2,0,1:T(8,128)S(1)} %get-tuple-element.10), channel_id=1, source_target_pairs={{0,4},{1,5},{2,6},{3,7},{4,0},{5,1},{6,2},{7,3},{8,12},{9,13},{10,... | collective-permute-start | bytes 1572872 | tf_op jit(solution)/shard_map/ppermute | solution.py:111
  30.6 23.7 %collective-permute-start.3 = (f32[1,32,16,256]{3,2,0,1:T(8,128)S(1)}, f32[1,32,16,256]{3,2,0,1:T(8,128)S(1)}, u32[]{:S(2)}, u32[]{:S(2)}) collective-permute-start(f32[1,32,16,256]{3,2,0,1:T(8,128)S(1)} %get-tuple-element.9), channel_id=1, source_target_pairs={{0,6},{1,7},{2,0},{3,1},{4,2},{5,3},{6,4},{7,5},{8,14},{9,15},{10,... | collective-permute-start | bytes 1572872 | tf_op jit(solution)/shard_map/ppermute | solution.py:111

commit v8 on v7

--- a/solution.py
+++ b/solution.py
@@ -66,16 +66,17 @@
 
 
 def _dft_kernel(table_ref, snap_ref, out_ref):
-    n_ba, a_step, _, pts_dev = out_ref.shape
+    halves, n_ba, a_step, rows, pts_dev = out_ref.shape
     res = jnp.dot(table_ref[...], snap_ref[...], precision=lax.Precision.HIGHEST,
                   preferred_element_type=jnp.float32)
-    for a in range(a_step):
-        for v in range(n_ba):
-            start = (a * n_ba + v) * pts_dev
-            out_ref[v, a] = res[:, start:start + pts_dev]
+    for h in range(halves):
+        for a in range(a_step):
+            for v in range(n_ba):
+                start = (a * n_ba + v) * pts_dev
+                out_ref[h, v, a] = res[h * rows:(h + 1) * rows, start:start + pts_dev]
 
 
-def partial_dft(table_t, snapshots, n_aa, n_ba):
+def partial_dft(table_t, snapshots, n_aa, n_ba, halves):
     a_step = math.gcd(4, n_aa)
     rows, time_dev = table_t.shape
     points = snapshots.shape[1]
@@ -88,8 +89,8 @@
             pl.BlockSpec((rows, time_dev), lambda i: (0, 0)),
             pl.BlockSpec((time_dev, width), lambda i: (0, i)),
         ],
-        out_specs=pl.BlockSpec((n_ba, a_step, rows, pts_dev), lambda i: (0, i, 0, 0)),
-        out_shape=jax.ShapeDtypeStruct((n_ba, n_aa, rows, pts_dev), jnp.float32),
+        out_specs=pl.BlockSpec((halves, n_ba, a_step, rows // halves, pts_dev), lambda i: (0, 0, i, 0, 0)),
+        out_shape=jax.ShapeDtypeStruct((halves, n_ba, n_aa, rows // halves, pts_dev), jnp.float32),
     )(table_t, snapshots)
 
 
@@ -121,9 +122,13 @@
     u = lax.axis_index("ba")
     table = spectral_rows(block_len, points, u * time_dev, time_dev)
     table_t = jnp.transpose(table, (2, 1, 0)).reshape(2 * FREQS, time_dev)
-    partial = partial_dft(table_t, snapshots, n_aa, n_ba)
-    block_spec = sum_over_ba(partial, n_ba)
-    spectra = lax.all_to_all(block_spec, "aa", split_axis=1, concat_axis=0, tiled=True)
+    halves = 2
+    partial = partial_dft(table_t, snapshots, n_aa, n_ba, halves)
+    shares = []
+    for h in range(halves):
+        block_spec = sum_over_ba(partial[h], n_ba)
+        shares.append(lax.all_to_all(block_spec, "aa", split_axis=1, concat_axis=0, tiled=True))
+    spectra = jnp.concatenate(shares, axis=2)
     blocks = spectra.shape[0]
     columns = 2 * blocks
     cols = jnp.transpose(spectra.reshape(blocks, FREQS, 2, pts_dev), (1, 0, 2, 3)).reshape(

time: 142 us -> 143 us (level)
  blocking collectives: 67 us -> 40.1 us
  starting transfers between devices: 6.56 us -> 24.6 us
  waiting for transfers between devices: 26.8 us -> 31.5 us
  local copies, waits for them, and re-layouts: 9.2 us -> 12.1 us
  other arithmetic: 5.4 us -> 7.35 us
    all_to_all x1 -> x0, blocking collectives: 25.4 us -> none  [local(): lax.all_to_all(block_spec, 'aa', split_axis=1, concat_axis=0, tiled=True)]
    all_to_all x0 -> x2, waiting for transfers between devices: none -> 19.8 us  [local(): lax.all_to_all(block_spec, 'aa', split_axis=1, concat_axis=0, tiled=True)]
    all_to_all x0 -> x2, starting transfers between devices: none -> 15.7 us  [local(): lax.all_to_all(block_spec, 'aa', split_axis=1, concat_axis=0, tiled=True)]
    ppermute x3 -> x6, waiting for transfers between devices: 22.6 us -> 10.4 us  [sum_over_ba(): total = total + lax.ppermute(out, 'ba', perm)]
    slice x0 -> x1, local copies, waits for them, and re-layouts: none -> 3.94 us  [local(): block_spec = sum_over_ba(partial[h], n_ba)]
    ppermute x1 -> x2, waiting for transfers between devices: 4.13 us -> 1.38 us  [sum_over_ba(): lax.ppermute(send, 'ba', [(i, i ^ 1) for i in range(n_ba)])]
    ppermute x3 -> x6, starting transfers between devices: 3.32 us -> 5.6 us  [sum_over_ba(): total = total + lax.ppermute(out, 'ba', perm)]
    all_to_all x1, blocking collectives: 23.3 us -> 21.6 us  [all_sum(): mine = lax.all_to_all(pieces, axes, 0, 0, tiled=True).sum(0, keepdims=True)]
  transfers between devices with their start and end apart: 4 -> 10, of which waited for: 4 -> 6; matrix products, arithmetic and copies ran while one was open for 0% -> 5% of each run, Pallas kernels for 0% -> 0%
where the time goes in v8:
time: 143 us; the launch traced here: 142 us
  blocking collectives  40.1 us (28%)
  waiting for transfers between devices  31.5 us (22%)
  starting transfers between devices  24.6 us (17%)
  Pallas kernels  22.4 us (16%)
  local copies, waits for them, and re-layouts  12.1 us (8%)
  other arithmetic  7.35 us (5%)
  matrix products  2.92 us (2%)
  between operations  1.49 us (1%)
    all_to_all x1, blocking collectives, all_sum(): mine = lax.all_to_all(pieces, axes, 0, 0, tiled=True).sum(0, keepdims=True)  21.6 us
    all_to_all x2, waiting for transfers between devices, local(): lax.all_to_all(block_spec, 'aa', split_axis=1, concat_axis=0, tiled=True)  19.8 us
    all_to_all x1, blocking collectives, all_sum(): return lax.all_to_all(spread, axes, 0, 0, tiled=True).reshape(x.shape)  18.5 us
    all_to_all x2, starting transfers between devices, local(): lax.all_to_all(block_spec, 'aa', split_axis=1, concat_axis=0, tiled=True)  15.7 us
    pallas_call x1, Pallas kernels, factor(): pl.pallas_call(_factor_kernel, out_shape=(jax.ShapeDtypeStruct(gram.shape...  12.3 us
    ppermute x6, waiting for transfers between devices, sum_over_ba(): total = total + lax.ppermute(out, 'ba', perm)  10.4 us
    pallas_call x1, Pallas kernels, partial_dft(): pl.pallas_call(_dft_kernel, grid=(n_aa // a_step,), in_specs=[pl.BlockSpe...  10.1 us
    ppermute x6, starting transfers between devices, sum_over_ba(): total = total + lax.ppermute(out, 'ba', perm)  5.6 us
  transfers between devices with their start and end apart: 10, of which 6 were waited for; matrix products, arithmetic and copies ran while one was open for 5% of the time, Pallas kernels for 0%

profile of v8, /device:TPU:1, one launch (start us, length us, event | category | flops | bytes accessed | tf_op | source)
XLA Modules:
  0.0 142.4 jit_solution(17366318066363000229)
XLA Ops:
  2.8 10.1 %shard_map.30 = f32[2,8,32,8,256]{4,3,2,1,0:T(8,128)} custom-call(f32[16,32]{1,0:T(8,128)} %bitcast.35, f32[32,65536]{1,0:T(8,128)} %snap_ref.1), custom_call_target="tpu_custom_call" | custom-call | tf_op jit(solution)/shard_map/pallas_call | solution.py:85
  12.9 3.9 %fusion.4 = (f32[1,8,32,8,256]{4,3,2,1,0:T(8,128)S(1)}, f32[1,8,32,8,256]{4,3,2,1,0:T(8,128)}) fusion(f32[2,8,32,8,256]{4,3,2,1,0:T(8,128)} %shard_map.30), kind=kLoop, calls=%fused_computation.36 | loop fusion | bytes 8388608 | tf_op jit(solution)/shard_map/slice | solution.py:129
  16.8 2.6 %constant_dynamic-slice_fusion.4 = (f32[4,1,32,8,256]{4,3,2,1,0:T(8,128)}, f32[4,1,32,8,256]{4,3,2,1,0:T(8,128)S(1)}) fusion(f32[4,2,32,8,256]{4,3,2,1,0:T(8,128)} %bitcast.30, s32[]{:T(128)S(6)} %select_n.77, s32[]{:T(128)S(6)} %select_n.78), kind=kLoop, calls=%fused_computation.25 | loop fusion | bytes 4194312 | tf_op jit(solution)/shard_map/jit(dynamic_index_in_dim)/dynamic_slice | solution.py:106
  19.5 1.1 copy.31
  20.6 3.2 %collective-permute-start.4 = (f32[4,32,8,256]{3,2,0,1:T(8,128)}, f32[4,32,8,256]{3,2,0,1:T(8,128)}, u32[]{:S(2)}, u32[]{:S(2)}) collective-permute-start(f32[4,32,8,256]{3,2,0,1:T(8,128)} %bitcast.25), channel_id=1, source_target_pairs={{0,1},{1,0},{2,3},{3,2},{4,5},{5,4},{6,7},{7,6},{8,9},{9,8},{10,11... | collective-permute-start | bytes 3145736 | tf_op jit(solution)/shard_map/ppermute | solution.py:107
  24.0 1.1 copy.32
  25.1 1.4 collective-permute-done.4
  26.4 1.4 bitcast_add_fusion
  27.9 1.1 collective-permute-start.7
  30.0 1.4 bitcast_add_fusion.1
  31.5 2.1 %collective-permute-start.3 = (f32[1,32,8,256]{3,2,0,1:T(8,128)S(1)}, f32[1,32,8,256]{3,2,0,1:T(8,128)S(1)}, u32[]{:S(2)}, u32[]{:S(2)}) collective-permute-start(f32[1,32,8,256]{3,2,0,1:T(8,128)S(1)} %get-tuple-element.13), channel_id=1, source_target_pairs={{0,6},{1,7},{2,0},{3,1},{4,2},{5,3},{6,4},{7,5},{8,14},{9,15},{10,... | collective-permute-start | bytes 786440 | tf_op jit(solution)/shard_map/ppermute | solution.py:112
  33.6 1.4 collective-permute-start.2
  35.5 2.2 %collective-permute-done.6 = f32[1,32,8,256]{3,2,0,1:T(8,128)S(1)} collective-permute-done((f32[1,32,8,256]{3,2,0,1:T(8,128)S(1)}, f32[1,32,8,256]{3,2,0,1:T(8,128)S(1)}, u32[]{:S(2)}, u32[]{:S(2)}) %collective-permute-start.6) | collective-permute-done | bytes 262176 | tf_op jit(solution)/shard_map/ppermute | solution.py:112
  37.7 7.6 %collective-permute-done.5 = f32[1,32,8,256]{3,2,0,1:T(8,128)S(1)} collective-permute-done((f32[1,32,8,256]{3,2,0,1:T(8,128)S(1)}, f32[1,32,8,256]{3,2,0,1:T(8,128)S(1)}, u32[]{:S(2)}, u32[]{:S(2)}) %collective-permute-start.5) | collective-permute-done | bytes 262176 | tf_op jit(solution)/shard_map/ppermute | solution.py:112
  46.1 11.0 %all-to-all-start.1 = ((f32[1,32,8,256]{3,2,0,1:T(8,128)}), f32[1,32,8,256]{3,2,0,1:T(8,128)S(1)}, u32[]{:S(2)}, u32[]{:S(2)}) async-start(f32[1,32,8,256]{3,2,0,1:T(8,128)} %add_add_fusion), calls=%async_computation.1 | async-start | bytes 524288 | tf_op jit(solution)/shard_map/all_to_all | solution.py:130
  57.2 1.7 %add_add_fusion.1 = f32[1,32,8,256]{3,2,0,1:T(8,128)} fusion(f32[1,32,8,256]{3,2,0,1:T(8,128)S(1)} %collective-permute-done.3, f32[1,32,8,256]{3,2,0,1:T(8,128)S(1)} %collective-permute-done.2, f32[1,32,8,256]{3,2,0,1:T(8,128)} %collective-permute-done.1, f32[4,32,8,256]{3,2,0,1:T(8,128)S(1)} %bitcast_add_fusion.1, s32[]{:T(128)S(6)} %select_n.80), kind=kLoop, calls=%fused_computation.9 | loop fusion | flops 196608 | bytes 1310724 | tf_op jit(solution)/shard_map/add | solution.py:112
  58.9 9.5 %all-to-all-done.1 = f32[1,32,8,256]{3,2,0,1:T(8,128)S(1)} async-done(((f32[1,32,8,256]{3,2,0,1:T(8,128)}), f32[1,32,8,256]{3,2,0,1:T(8,128)S(1)}, u32[]{:S(2)}, u32[]{:S(2)}) %all-to-all-start.1) | async-done | bytes 262176 | tf_op jit(solution)/shard_map/all_to_all | solution.py:130
  68.4 4.7 %all-to-all-start = ((f32[1,32,8,256]{3,2,0,1:T(8,128)}), f32[1,32,8,256]{3,2,0,1:T(8,128)S(1)}, u32[]{:S(2)}, u32[]{:S(2)}) async-start(f32[1,32,8,256]{3,2,0,1:T(8,128)} %add_add_fusion.1), calls=%async_computation | async-start | bytes 524288 | tf_op jit(solution)/shard_map/all_to_all | solution.py:130
  73.2 10.3 %all-to-all-done = f32[1,32,8,256]{3,2,0,1:T(8,128)S(1)} async-done(((f32[1,32,8,256]{3,2,0,1:T(8,128)}), f32[1,32,8,256]{3,2,0,1:T(8,128)S(1)}, u32[]{:S(2)}, u32[]{:S(2)}) %all-to-all-start) | async-done | bytes 262176 | tf_op jit(solution)/shard_map/all_to_all | solution.py:130
  85.1 21.6 %all_to_all.39 = f32[256,1,128]{2,1,0:T(1,128)S(1)} all-to-all(f32[256,1,128]{2,1,0:T(1,128)S(1)} %bitcast.34), channel_id=1, replica_groups=mesh['aa'=32,'ba'=8] {'aa','ba'}, dimensions={0} | all-to-all | bytes 262144 | tf_op jit(solution)/shard_map/all_to_all | solution.py:63
  107.1 18.5 %all_to_all.40 = f32[256,1,128]{2,1,0:T(1,128)S(1)} all-to-all(f32[256,1,128]{2,1,0:T(1,128)S(1)} %broadcast_in_dim.2), channel_id=1, replica_groups=mesh['aa'=32,'ba'=8] {'aa','ba'}, dimensions={0} | all-to-all | bytes 262144 | tf_op jit(solution)/shard_map/all_to_all | solution.py:65
  126.1 0.9 reduce.4
  127.9 12.3 %shard_map.31 = (f32[8,64,64]{2,1,0:T(8,128)}, f32[8,64,64]{2,1,0:T(8,128)}) custom-call(f32[8,64,64]{2,1,0:T(8,128)} %reshape.223.a_ref), custom_call_target="tpu_custom_call" | custom-call | tf_op jit(solution)/shard_map/pallas_call | solution.py:54
  140.1 2.3 %convolution_multiply_fusion = f32[8,64,256]{2,1,0:T(8,128)} fusion(f32[8,64,64]{2,1,0:T(8,128)} %get-tuple-element.5, f32[8,64,256]{2,1,0:T(8,128)S(1)} %reshape.222), kind=kOutput, calls=%fused_computation | convolution fusion | flops 100794368 | bytes 1179648 | tf_op jit(solution)/shard_map/fij,fjp->fip/dot_general | solution.py:140
  (33 shorter events, 7.5 us)
Async XLA Ops:
  20.6 5.9 %collective-permute-start.4 = (f32[4,32,8,256]{3,2,0,1:T(8,128)}, f32[4,32,8,256]{3,2,0,1:T(8,128)}, u32[]{:S(2)}, u32[]{:S(2)}) collective-permute-start(f32[4,32,8,256]{3,2,0,1:T(8,128)} %bitcast.25), channel_id=1, source_target_pairs={{0,1},{1,0},{2,3},{3,2},{4,5},{5,4},{6,7},{7,6},{8,9},{9,8},{10,11... | collective-permute-start | bytes 3145736 | tf_op jit(solution)/shard_map/ppermute | solution.py:107
  23.9 2.5 %copy-start = (f32[4,1,32,8,256]{4,3,2,1,0:T(8,128)S(1)}, f32[4,1,32,8,256]{4,3,2,1,0:T(8,128)}, u32[]{:S(2)}) copy-start(f32[4,1,32,8,256]{4,3,2,1,0:T(8,128)} %get-tuple-element.10) | copy-start | bytes 3145732
  25.1 5.0 %collective-permute-start = (f32[4,32,8,256]{3,2,0,1:T(8,128)}, f32[4,32,8,256]{3,2,0,1:T(8,128)}, u32[]{:S(2)}, u32[]{:S(2)}) collective-permute-start(f32[4,32,8,256]{3,2,0,1:T(8,128)} %bitcast.26), channel_id=1, source_target_pairs={{0,1},{1,0},{2,3},{3,2},{4,5},{5,4},{6,7},{7,6},{8,9},{9,8},{10,11... | collective-permute-start | bytes 3145736 | tf_op jit(solution)/shard_map/ppermute | solution.py:107
  27.9 7.6 %collective-permute-start.7 = (f32[1,32,8,256]{3,2,0,1:T(8,128)S(1)}, f32[1,32,8,256]{3,2,0,1:T(8,128)S(1)}, u32[]{:S(2)}, u32[]{:S(2)}) collective-permute-start(f32[1,32,8,256]{3,2,0,1:T(8,128)S(1)} %get-tuple-element.16), channel_id=1, source_target_pairs={{0,6},{1,7},{2,0},{3,1},{4,2},{5,3},{6,4},{7,5},{8,14},{9,15},{10,... | collective-permute-start | bytes 786440 | tf_op jit(solution)/shard_map/ppermute | solution.py:112
  29.0 8.7 %collective-permute-start.6 = (f32[1,32,8,256]{3,2,0,1:T(8,128)S(1)}, f32[1,32,8,256]{3,2,0,1:T(8,128)S(1)}, u32[]{:S(2)}, u32[]{:S(2)}) collective-permute-start(f32[1,32,8,256]{3,2,0,1:T(8,128)S(1)} %get-tuple-element.17), channel_id=1, source_target_pairs={{0,4},{1,5},{2,6},{3,7},{4,0},{5,1},{6,2},{7,3},{8,12},{9,13},{10,... | collective-permute-start | bytes 786440 | tf_op jit(solution)/shard_map/ppermute | solution.py:112
  29.3 16.0 %collective-permute-start.5 = (f32[1,32,8,256]{3,2,0,1:T(8,128)S(1)}, f32[1,32,8,256]{3,2,0,1:T(8,128)S(1)}, u32[]{:S(2)}, u32[]{:S(2)}) collective-permute-start(f32[1,32,8,256]{3,2,0,1:T(8,128)S(1)} %get-tuple-element.15), channel_id=1, source_target_pairs={{0,2},{1,3},{2,4},{3,5},{4,6},{5,7},{6,0},{7,1},{8,10},{9,11},{10,... | collective-permute-start | bytes 786440 | tf_op jit(solution)/shard_map/ppermute | solution.py:112
  31.5 25.6 %collective-permute-start.3 = (f32[1,32,8,256]{3,2,0,1:T(8,128)S(1)}, f32[1,32,8,256]{3,2,0,1:T(8,128)S(1)}, u32[]{:S(2)}, u32[]{:S(2)}) collective-permute-start(f32[1,32,8,256]{3,2,0,1:T(8,128)S(1)} %get-tuple-element.13), channel_id=1, source_target_pairs={{0,6},{1,7},{2,0},{3,1},{4,2},{5,3},{6,4},{7,5},{8,14},{9,15},{10,... | collective-permute-start | bytes 786440 | tf_op jit(solution)/shard_map/ppermute | solution.py:112
  33.6 23.6 %collective-permute-start.2 = (f32[1,32,8,256]{3,2,0,1:T(8,128)S(1)}, f32[1,32,8,256]{3,2,0,1:T(8,128)S(1)}, u32[]{:S(2)}, u32[]{:S(2)}) collective-permute-start(f32[1,32,8,256]{3,2,0,1:T(8,128)S(1)} %get-tuple-element.14), channel_id=1, source_target_pairs={{0,4},{1,5},{2,6},{3,7},{4,0},{5,1},{6,2},{7,3},{8,12},{9,13},{10,... | collective-permute-start | bytes 786440 | tf_op jit(solution)/shard_map/ppermute | solution.py:112
  35.5 21.7 %collective-permute-start.1 = (f32[1,32,8,256]{3,2,0,1:T(8,128)S(1)}, f32[1,32,8,256]{3,2,0,1:T(8,128)}, u32[]{:S(2)}, u32[]{:S(2)}) collective-permute-start(f32[1,32,8,256]{3,2,0,1:T(8,128)S(1)} %get-tuple-element.12), channel_id=1, source_target_pairs={{0,2},{1,3},{2,4},{3,5},{4,6},{5,7},{6,0},{7,1},{8,10},{9,11},{10,... | collective-permute-start | bytes 786440 | tf_op jit(solution)/shard_map/ppermute | solution.py:112
  46.1 22.3 %all-to-all-start.1 = ((f32[1,32,8,256]{3,2,0,1:T(8,128)}), f32[1,32,8,256]{3,2,0,1:T(8,128)S(1)}, u32[]{:S(2)}, u32[]{:S(2)}) async-start(f32[1,32,8,256]{3,2,0,1:T(8,128)} %add_add_fusion), calls=%async_computation.1 | async-start | bytes 524288 | tf_op jit(solution)/shard_map/all_to_all | solution.py:130
  68.4 15.1 %all-to-all-start = ((f32[1,32,8,256]{3,2,0,1:T(8,128)}), f32[1,32,8,256]{3,2,0,1:T(8,128)S(1)}, u32[]{:S(2)}, u32[]{:S(2)}) async-start(f32[1,32,8,256]{3,2,0,1:T(8,128)} %add_add_fusion.1), calls=%async_computation | async-start | bytes 524288 | tf_op jit(solution)/shard_map/all_to_all | solution.py:130

commit v9 on v7

--- a/solution.py
+++ b/solution.py
@@ -31,19 +31,21 @@
     rows = lax.broadcasted_iota(jnp.int32, (freqs, n, 2 * n), 1)
     lanes = lax.broadcasted_iota(jnp.int32, (freqs, n, 2 * n), 2)
     m_ref[...] = jnp.concatenate([a_ref[...], (rows[:, :, :n] == lanes[:, :, :n]).astype(jnp.float32)], axis=2)
+    tile = math.gcd(8, n)
+    for lo in range(0, n, tile):
+        def step(jj, carry, lo=lo):
+            j = lo + jj
+            m = m_ref[:, lo:, :]
+            pivot_row = m_ref[:, pl.ds(j, 1), :]
+            pivot = jnp.sum(jnp.where(lanes[:, :1] == j, pivot_row, 0.0), axis=2, keepdims=True)
+            scaled_row = pivot_row / pivot
+            column = jnp.sum(jnp.where(lanes[:, lo:] == j, m, 0.0), axis=2, keepdims=True)
+            column = jnp.where(rows[:, lo:, :1] > j, column, 0.0)
+            m_ref[:, lo:, :] = m - column * scaled_row
+            m_ref[:, pl.ds(j, 1), :] = pivot_row / jnp.sqrt(pivot)
+            return carry
 
-    def step(j, carry):
-        m = m_ref[...]
-        pivot_row = m_ref[:, pl.ds(j, 1), :]
-        pivot = jnp.sum(jnp.where(lanes[:, :1] == j, pivot_row, 0.0), axis=2, keepdims=True)
-        scaled_row = pivot_row / pivot
-        column = jnp.sum(jnp.where(lanes == j, m, 0.0), axis=2, keepdims=True)
-        column = jnp.where(rows[:, :, :1] > j, column, 0.0)
-        m_ref[...] = m - column * scaled_row
-        m_ref[:, pl.ds(j, 1), :] = pivot_row / jnp.sqrt(pivot)
-        return carry
-
-    lax.fori_loop(0, n, step, 0)
+        lax.fori_loop(0, tile, step, 0)
     m = m_ref[...]
     upper_ref[...] = jnp.where(rows[:, :, :n] <= lanes[:, :, :n], m[:, :, :n], 0.0)
     inv_ref[...] = m[:, :, n:]

time: 142 us -> 140 us (0.986)
  Pallas kernels: 22.3 us -> 20.3 us
    pallas_call x1, Pallas kernels: 12.2 us -> 10.2 us  [factor(): pl.pallas_call(_factor_kernel, out_shape=(jax.ShapeDtypeStruct(gram.shape...]
where the time goes in v9:
time: 140 us
  blocking collectives  67 us (48%)
  waiting for transfers between devices  26.8 us (19%)
  Pallas kernels  20.3 us (14%)
  local copies, waits for them, and re-layouts  9.2 us (7%)
  starting transfers between devices  6.56 us (5%)
  other arithmetic  5.4 us (4%)
  matrix products  2.92 us (2%)
  between operations  1.44 us (1%)
    all_to_all x1, blocking collectives, local(): lax.all_to_all(block_spec, 'aa', split_axis=1, concat_axis=0, tiled=True)  25.4 us
    all_to_all x1, blocking collectives, all_sum(): mine = lax.all_to_all(pieces, axes, 0, 0, tiled=True).sum(0, keepdims=True)  23.3 us
    ppermute x3, waiting for transfers between devices, sum_over_ba(): total = total + lax.ppermute(out, 'ba', perm)  22.6 us
    all_to_all x1, blocking collectives, all_sum(): return lax.all_to_all(spread, axes, 0, 0, tiled=True).reshape(x.shape)  18.3 us
    pallas_call x1, Pallas kernels, factor(): pl.pallas_call(_factor_kernel, out_shape=(jax.ShapeDtypeStruct(gram.shape...  10.2 us
    pallas_call x1, Pallas kernels, partial_dft(): pl.pallas_call(_dft_kernel, grid=(n_aa // a_step,), in_specs=[pl.BlockSpe...  10.1 us
    ppermute x1, waiting for transfers between devices, sum_over_ba(): lax.ppermute(send, 'ba', [(i, i ^ 1) for i in range(n_ba)])  4.13 us
    ppermute x3, starting transfers between devices, sum_over_ba(): total = total + lax.ppermute(out, 'ba', perm)  3.32 us
  transfers between devices with their start and end apart: 4, of which 4 were waited for; matrix products, arithmetic and copies ran while one was open for 0% of the time, Pallas kernels for 0%

profile of v9, /device:TPU:1, one launch (start us, length us, event | category | flops | bytes accessed | tf_op | source)
XLA Modules:
  0.0 139.6 jit_solution(3045916084919547426)
XLA Ops:
  0.7 0.6 multiply_reduce_fusion
  2.2 0.6 copy.11
  2.8 10.1 %shard_map.30 = f32[8,32,16,256]{3,2,1,0:T(8,128)} custom-call(f32[16,32]{1,0:T(8,128)} %bitcast.20, f32[32,65536]{1,0:T(8,128)} %snap_ref.1), custom_call_target="tpu_custom_call" | custom-call | tf_op jit(solution)/shard_map/pallas_call | solution.py:86
  12.8 3.0 %constant_dynamic-slice_fusion.4 = (f32[4,1,32,16,256]{4,3,2,1,0:T(8,128)S(1)}, f32[4,1,32,16,256]{4,3,2,1,0:T(8,128)S(1)}) fusion(f32[4,2,32,16,256]{4,3,2,1,0:T(8,128)} %bitcast.17, s32[]{:T(128)S(6)} %select_n.62, s32[]{:T(128)S(6)} %select_n.63), kind=kLoop, calls=%fused_computation.19 | loop fusion | bytes 8388616 | tf_op jit(solution)/shard_map/jit(dynamic_index_in_dim)/dynamic_slice | solution.py:107
  15.8 1.6 %copy.19 = f32[4,1,32,16,256]{4,3,0,2,1:T(8,128)} copy(f32[4,1,32,16,256]{4,3,2,1,0:T(8,128)S(1)} %get-tuple-element.7) | data formatting | bytes 4194304 | tf_op jit(solution)/shard_map/jit(dynamic_index_in_dim)/dynamic_slice | solution.py:106
  17.4 3.2 %collective-permute-start = (f32[4,32,16,256]{3,2,0,1:T(8,128)}, f32[4,32,16,256]{3,2,0,1:T(8,128)}, u32[]{:S(2)}, u32[]{:S(2)}) collective-permute-start(f32[4,32,16,256]{3,2,0,1:T(8,128)} %bitcast.16), channel_id=1, source_target_pairs={{0,1},{1,0},{2,3},{3,2},{4,5},{5,4},{6,7},{7,6},{8,9},{9,8},{10,11... | collective-permute-start | bytes 6291464 | tf_op jit(solution)/shard_map/ppermute | solution.py:108
  20.7 4.1 %collective-permute-done = f32[4,32,16,256]{3,2,0,1:T(8,128)} collective-permute-done((f32[4,32,16,256]{3,2,0,1:T(8,128)}, f32[4,32,16,256]{3,2,0,1:T(8,128)}, u32[]{:S(2)}, u32[]{:S(2)}) %collective-permute-start) | collective-permute-done | bytes 2097184 | tf_op jit(solution)/shard_map/ppermute | solution.py:108
  24.8 2.1 %bitcast_add_fusion = f32[4,32,16,256]{3,2,0,1:T(8,128)S(1)} fusion(f32[4,32,16,256]{3,2,0,1:T(8,128)} %collective-permute-done, f32[4,1,32,16,256]{4,3,2,1,0:T(8,128)S(1)} %get-tuple-element.6), kind=kLoop, calls=%fused_computation | loop fusion | flops 524288 | bytes 6291456 | tf_op jit(solution)/shard_map/add | solution.py:108
  26.9 1.3 copy-done
  28.4 2.2 %collective-permute-start.2 = (f32[1,32,16,256]{3,2,0,1:T(8,128)S(1)}, f32[1,32,16,256]{3,2,0,1:T(8,128)S(1)}, u32[]{:S(2)}, u32[]{:S(2)}) collective-permute-start(f32[1,32,16,256]{3,2,0,1:T(8,128)S(1)} %get-tuple-element.10), channel_id=1, source_target_pairs={{0,4},{1,5},{2,6},{3,7},{4,0},{5,1},{6,2},{7,3},{8,12},{9,13},{10,... | collective-permute-start | bytes 1572872 | tf_op jit(solution)/shard_map/ppermute | solution.py:113
  30.6 1.1 collective-permute-start.3
  31.7 11.6 %collective-permute-done.1 = f32[1,32,16,256]{3,2,0,1:T(8,128)S(1)} collective-permute-done((f32[1,32,16,256]{3,2,0,1:T(8,128)S(1)}, f32[1,32,16,256]{3,2,0,1:T(8,128)S(1)}, u32[]{:S(2)}, u32[]{:S(2)}) %collective-permute-start.1) | collective-permute-done | bytes 524320 | tf_op jit(solution)/shard_map/ppermute | solution.py:113
  43.2 10.3 %collective-permute-done.2 = f32[1,32,16,256]{3,2,0,1:T(8,128)S(1)} collective-permute-done((f32[1,32,16,256]{3,2,0,1:T(8,128)S(1)}, f32[1,32,16,256]{3,2,0,1:T(8,128)S(1)}, u32[]{:S(2)}, u32[]{:S(2)}) %collective-permute-start.2) | collective-permute-done | bytes 524320 | tf_op jit(solution)/shard_map/ppermute | solution.py:113
  53.6 0.7 collective-permute-done.3
  54.3 1.3 add_add_fusion
  55.6 25.4 %all_to_all.24 = f32[1,32,16,256]{3,2,0,1:T(8,128)S(1)} all-to-all(f32[1,32,16,256]{3,2,0,1:T(8,128)S(1)} %add_add_fusion), channel_id=1, replica_groups=mesh['aa'=32,'ba'=8] {'aa'}, dimensions={1} | all-to-all | bytes 1048576 | tf_op jit(solution)/shard_map/all_to_all | solution.py:128
  82.1 0.6 fusion.4
  82.8 23.3 %all_to_all.25 = f32[256,1,128]{2,1,0:T(1,128)S(1)} all-to-all(f32[256,1,128]{2,1,0:T(1,128)S(1)} %bitcast.19), channel_id=1, replica_groups=mesh['aa'=32,'ba'=8] {'aa','ba'}, dimensions={0} | all-to-all | bytes 262144 | tf_op jit(solution)/shard_map/all_to_all | solution.py:65
  106.4 18.3 %all_to_all.26 = f32[256,1,128]{2,1,0:T(1,128)S(1)} all-to-all(f32[256,1,128]{2,1,0:T(1,128)S(1)} %broadcast_in_dim.2), channel_id=1, replica_groups=mesh['aa'=32,'ba'=8] {'aa','ba'}, dimensions={0} | all-to-all | bytes 262144 | tf_op jit(solution)/shard_map/all_to_all | solution.py:67
  124.8 0.5 broadcast.243
  125.3 0.9 reduce.4
  126.2 0.8 reshape.225.a_ref
  127.0 10.2 %shard_map.31 = (f32[8,64,64]{2,1,0:T(8,128)}, f32[8,64,64]{2,1,0:T(8,128)}) custom-call(f32[8,64,64]{2,1,0:T(8,128)} %reshape.225.a_ref), custom_call_target="tpu_custom_call" | custom-call | tf_op jit(solution)/shard_map/pallas_call | solution.py:56
  137.3 2.3 %convolution_multiply_fusion = f32[8,64,256]{2,1,0:T(8,128)} fusion(f32[8,64,64]{2,1,0:T(8,128)} %get-tuple-element.5, f32[8,64,256]{2,1,0:T(8,128)S(1)} %reshape.224), kind=kOutput, calls=%fused_computation.2 | convolution fusion | flops 100794368 | bytes 1179648 | tf_op jit(solution)/shard_map/fij,fjp->fip/dot_general | solution.py:137
  (14 shorter events, 1.9 us)
Async XLA Ops:
  17.4 7.4 %collective-permute-start = (f32[4,32,16,256]{3,2,0,1:T(8,128)}, f32[4,32,16,256]{3,2,0,1:T(8,128)}, u32[]{:S(2)}, u32[]{:S(2)}) collective-permute-start(f32[4,32,16,256]{3,2,0,1:T(8,128)} %bitcast.16), channel_id=1, source_target_pairs={{0,1},{1,0},{2,3},{3,2},{4,5},{5,4},{6,7},{7,6},{8,9},{9,8},{10,11... | collective-permute-start | bytes 6291464 | tf_op jit(solution)/shard_map/ppermute | solution.py:108
  26.9 1.3 copy-start
  28.3 14.9 %collective-permute-start.1 = (f32[1,32,16,256]{3,2,0,1:T(8,128)S(1)}, f32[1,32,16,256]{3,2,0,1:T(8,128)S(1)}, u32[]{:S(2)}, u32[]{:S(2)}) collective-permute-start(f32[1,32,16,256]{3,2,0,1:T(8,128)S(1)} %get-tuple-element.8), channel_id=1, source_target_pairs={{0,2},{1,3},{2,4},{3,5},{4,6},{5,7},{6,0},{7,1},{8,10},{9,11},{10,... | collective-permute-start | bytes 1572872 | tf_op jit(solution)/shard_map/ppermute | solution.py:113
  28.4 25.1 %collective-permute-start.2 = (f32[1,32,16,256]{3,2,0,1:T(8,128)S(1)}, f32[1,32,16,256]{3,2,0,1:T(8,128)S(1)}, u32[]{:S(2)}, u32[]{:S(2)}) collective-permute-start(f32[1,32,16,256]{3,2,0,1:T(8,128)S(1)} %get-tuple-element.10), channel_id=1, source_target_pairs={{0,4},{1,5},{2,6},{3,7},{4,0},{5,1},{6,2},{7,3},{8,12},{9,13},{10,... | collective-permute-start | bytes 1572872 | tf_op jit(solution)/shard_map/ppermute | solution.py:113
  30.6 23.7 %collective-permute-start.3 = (f32[1,32,16,256]{3,2,0,1:T(8,128)S(1)}, f32[1,32,16,256]{3,2,0,1:T(8,128)S(1)}, u32[]{:S(2)}, u32[]{:S(2)}) collective-permute-start(f32[1,32,16,256]{3,2,0,1:T(8,128)S(1)} %get-tuple-element.9), channel_id=1, source_target_pairs={{0,6},{1,7},{2,0},{3,1},{4,2},{5,3},{6,4},{7,5},{8,14},{9,15},{10,... | collective-permute-start | bytes 1572872 | tf_op jit(solution)/shard_map/ppermute | solution.py:113

commit v10 on v9

--- a/solution.py
+++ b/solution.py
@@ -67,17 +67,20 @@
     return lax.all_to_all(spread, axes, 0, 0, tiled=True).reshape(x.shape)
 
 
-def _dft_kernel(table_ref, snap_ref, out_ref):
-    n_ba, a_step, _, pts_dev = out_ref.shape
+def _dft_kernel(core_ref, table_ref, snap_ref, out_ref):
+    _, chips, a_step, _, pts_dev = out_ref.shape
+    core = core_ref[0]
     res = jnp.dot(table_ref[...], snap_ref[...], precision=lax.Precision.HIGHEST,
                   preferred_element_type=jnp.float32)
     for a in range(a_step):
-        for v in range(n_ba):
-            start = (a * n_ba + v) * pts_dev
-            out_ref[v, a] = res[:, start:start + pts_dev]
+        for v in range(2 * chips):
+            cv = v % 2
+            keep = 1 - (cv + core - 2 * cv * core)
+            start = (a * 2 * chips + v) * pts_dev
+            out_ref[keep, v // 2, a] = res[:, start:start + pts_dev]
 
 
-def partial_dft(table_t, snapshots, n_aa, n_ba):
+def partial_dft(table_t, snapshots, core, n_aa, n_ba):
     a_step = math.gcd(4, n_aa)
     rows, time_dev = table_t.shape
     points = snapshots.shape[1]
@@ -85,27 +88,25 @@
     width = a_step * n_ba * pts_dev
     return pl.pallas_call(
         _dft_kernel,
-        grid=(n_aa // a_step,),
-        in_specs=[
-            pl.BlockSpec((rows, time_dev), lambda i: (0, 0)),
-            pl.BlockSpec((time_dev, width), lambda i: (0, i)),
-        ],
-        out_specs=pl.BlockSpec((n_ba, a_step, rows, pts_dev), lambda i: (0, i, 0, 0)),
-        out_shape=jax.ShapeDtypeStruct((n_ba, n_aa, rows, pts_dev), jnp.float32),
-    )(table_t, snapshots)
+        grid_spec=pltpu.PrefetchScalarGridSpec(
+            num_scalar_prefetch=1,
+            grid=(n_aa // a_step,),
+            in_specs=[
+                pl.BlockSpec((rows, time_dev), lambda i, c: (0, 0)),
+                pl.BlockSpec((time_dev, width), lambda i, c: (0, i)),
+            ],
+            out_specs=pl.BlockSpec((2, n_ba // 2, a_step, rows, pts_dev), lambda i, c: (0, 0, i, 0, 0)),
+        ),
+        out_shape=jax.ShapeDtypeStruct((2, n_ba // 2, n_aa, rows, pts_dev), jnp.float32),
+    )(core, table_t, snapshots)
 
 
 def sum_over_ba(partial, n_ba):
     u = lax.axis_index("ba")
     cores = 2
-    if n_ba % cores:
-        return lax.all_to_all(partial, "ba", 0, 0, tiled=True).sum(0, keepdims=True)
     chips = n_ba // cores
-    y, c = u // cores, u % cores
-    parts = partial.reshape(chips, cores, *partial.shape[1:])
-    send = lax.dynamic_index_in_dim(parts, cores - 1 - c, axis=1, keepdims=False)
-    keep = lax.dynamic_index_in_dim(parts, c, axis=1, keepdims=False)
-    chip_sum = keep + lax.ppermute(send, "ba", [(i, i ^ 1) for i in range(n_ba)])
+    y = u // cores
+    chip_sum = partial[1] + lax.ppermute(partial[0], "ba", [(i, i ^ 1) for i in range(n_ba)])
     total = lax.dynamic_index_in_dim(chip_sum, y, axis=0, keepdims=True)
     for shift in range(1, chips):
         out = lax.dynamic_index_in_dim(chip_sum, (y + shift) % chips, axis=0, keepdims=True)
@@ -123,7 +124,8 @@
     u = lax.axis_index("ba")
     table = spectral_rows(block_len, points, u * time_dev, time_dev)
     table_t = jnp.transpose(table, (2, 1, 0)).reshape(2 * FREQS, time_dev)
-    partial = partial_dft(table_t, snapshots, n_aa, n_ba)
+    core = (u % 2).astype(jnp.int32).reshape(1)
+    partial = partial_dft(table_t, snapshots, core, n_aa, n_ba)
     block_spec = sum_over_ba(partial, n_ba)
     spectra = lax.all_to_all(block_spec, "aa", split_axis=1, concat_axis=0, tiled=True)
     blocks = spectra.shape[0]

time: 140 us -> 137 us (0.979)
  local copies, waits for them, and re-layouts: 9.2 us -> 5.65 us
    dynamic_slice x2 -> x0, local copies, waits for them, and re-layouts: 4.56 us -> none  [the longest x1 2.97 us: sum_over_ba(): keep = lax.dynamic_index_in_dim(parts, c, axis=1, keepdims=False)]
    squeeze x0 -> x1, local copies, waits for them, and re-layouts: none -> 1.76 us  [sum_over_ba(): partial[0]]
where the time goes in v10:
time: 137 us
  blocking collectives  66.9 us (49%)
  waiting for transfers between devices  26.7 us (19%)
  Pallas kernels  20.5 us (15%)
  starting transfers between devices  6.46 us (5%)
  other arithmetic  6.34 us (5%)
  local copies, waits for them, and re-layouts  5.65 us (4%)
  matrix products  2.92 us (2%)
  between operations  1.41 us (1%)
    all_to_all x1, blocking collectives, local(): lax.all_to_all(block_spec, 'aa', split_axis=1, concat_axis=0, tiled=True)  25.6 us
    all_to_all x1, blocking collectives, all_sum(): mine = lax.all_to_all(pieces, axes, 0, 0, tiled=True).sum(0, keepdims=True)  23 us
    ppermute x3, waiting for transfers between devices, sum_over_ba(): total = total + lax.ppermute(out, 'ba', perm)  22.8 us
    all_to_all x1, blocking collectives, all_sum(): return lax.all_to_all(spread, axes, 0, 0, tiled=True).reshape(x.shape)  18.3 us
    pallas_call x1, Pallas kernels, factor(): pl.pallas_call(_factor_kernel, out_shape=(jax.ShapeDtypeStruct(gram.shape...  10.2 us
    pallas_call x1, Pallas kernels, partial_dft(): pl.pallas_call(_dft_kernel, grid_spec=pltpu.PrefetchScalarGridSpec(num_sc...  10.2 us
    ppermute x1, waiting for transfers between devices, sum_over_ba(): lax.ppermute(partial[0], 'ba', [(i, i ^ 1) for i in range(n_ba)])  3.92 us
    ppermute x1, starting transfers between devices, sum_over_ba(): lax.ppermute(partial[0], 'ba', [(i, i ^ 1) for i in range(n_ba)])  3.27 us
  transfers between devices with their start and end apart: 4, of which 4 were waited for; matrix products, arithmetic and copies ran while one was open for 0% of the time, Pallas kernels for 0%

profile of v10, /device:TPU:1, one launch (start us, length us, event | category | flops | bytes accessed | tf_op | source)
XLA Modules:
  0.0 136.8 jit_solution(6037523142806149742)
XLA Ops:
  0.7 0.6 multiply_reduce_fusion
  2.2 0.6 copy.7
  2.8 10.2 %shard_map.30 = f32[2,4,32,16,256]{4,3,2,1,0:T(8,128)} custom-call(s32[1]{0:T(128)} %bitcast.core_ref, f32[16,32]{1,0:T(8,128)} %bitcast.26, f32[32,65536]{1,0:T(8,128)} %snap_ref.1), custom_call_target="tpu_custom_call" | custom-call | tf_op jit(solution)/shard_map/pallas_call | solution.py:89
  13.0 1.8 %slice_bitcast_fusion = f32[4,32,16,256]{3,2,1,0:T(8,128)S(1)} fusion(f32[2,4,32,16,256]{4,3,2,1,0:T(8,128)} %shard_map.30), kind=kLoop, calls=%fused_computation | loop fusion | bytes 4194304 | tf_op jit(solution)/shard_map/squeeze | solution.py:109
  14.8 3.3 %collective-permute-start = (f32[4,32,16,256]{3,2,1,0:T(8,128)S(1)}, f32[4,32,16,256]{3,2,1,0:T(8,128)}, u32[]{:S(2)}, u32[]{:S(2)}) collective-permute-start(f32[4,32,16,256]{3,2,1,0:T(8,128)S(1)} %slice_bitcast_fusion), channel_id=1, source_target_pairs={{0,1},{1,0},{2,3},{3,2},{4,5},{5,4},{6,7},{7,6},{8,9},{9,8},{10,11... | collective-permute-start | bytes 6291464 | tf_op jit(solution)/shard_map/ppermute | solution.py:109
  18.0 3.9 %collective-permute-done = f32[4,32,16,256]{3,2,1,0:T(8,128)} collective-permute-done((f32[4,32,16,256]{3,2,1,0:T(8,128)S(1)}, f32[4,32,16,256]{3,2,1,0:T(8,128)}, u32[]{:S(2)}, u32[]{:S(2)}) %collective-permute-start) | collective-permute-done | bytes 2097184 | tf_op jit(solution)/shard_map/ppermute | solution.py:109
  22.0 2.7 %fusion = f32[4,32,16,256]{3,2,1,0:T(8,128)S(1)} fusion(f32[4,32,16,256]{3,2,1,0:T(8,128)} %collective-permute-done, f32[2,4,32,16,256]{4,3,2,1,0:T(8,128)} %shard_map.30), kind=kLoop, calls=%fused_computation.2 | loop fusion | flops 524288 | bytes 6291456 | tf_op jit(solution)/shard_map/add | solution.py:109
  24.7 0.9 constant_dynamic-slice_fusion.2
  25.6 2.1 %collective-permute-start.2 = (f32[1,32,16,256]{3,2,1,0:T(8,128)S(1)}, f32[1,32,16,256]{3,2,1,0:T(8,128)}, u32[]{:S(2)}, u32[]{:S(2)}) collective-permute-start(f32[1,32,16,256]{3,2,1,0:T(8,128)S(1)} %get-tuple-element.8), channel_id=1, source_target_pairs={{0,4},{1,5},{2,6},{3,7},{4,0},{5,1},{6,2},{7,3},{8,12},{9,13},{10,... | collective-permute-start | bytes 1572872 | tf_op jit(solution)/shard_map/ppermute | solution.py:114
  27.7 1.1 collective-permute-start.3
  28.8 12.0 %collective-permute-done.1 = f32[1,32,16,256]{3,2,1,0:T(8,128)} collective-permute-done((f32[1,32,16,256]{3,2,1,0:T(8,128)}, f32[1,32,16,256]{3,2,1,0:T(8,128)}, u32[]{:S(2)}, u32[]{:S(2)}) %collective-permute-start.1) | collective-permute-done | bytes 524320 | tf_op jit(solution)/shard_map/ppermute | solution.py:114
  40.8 10.2 %collective-permute-done.2 = f32[1,32,16,256]{3,2,1,0:T(8,128)} collective-permute-done((f32[1,32,16,256]{3,2,1,0:T(8,128)S(1)}, f32[1,32,16,256]{3,2,1,0:T(8,128)}, u32[]{:S(2)}, u32[]{:S(2)}) %collective-permute-start.2) | collective-permute-done | bytes 524320 | tf_op jit(solution)/shard_map/ppermute | solution.py:114
  51.0 0.6 collective-permute-done.3
  51.6 1.6 %add_bitcast_fusion = f32[1,32,16,256]{3,2,0,1:T(8,128)S(1)} fusion(f32[1,32,16,256]{3,2,1,0:T(8,128)} %collective-permute-done.3, f32[1,32,16,256]{3,2,1,0:T(8,128)} %collective-permute-done.2, f32[1,32,16,256]{3,2,1,0:T(8,128)} %collective-permute-done.1, f32[4,32,16,256]{3,2,1,0:T(8,128)S(1)} %fusion, s32[]{:T(128)S(6)} %select_n.56), kind=kLoop, calls=%fused_computation.5 | loop fusion | flops 393216 | bytes 2621444 | tf_op jit(solution)/shard_map/add | solution.py:114
  53.2 25.6 %all_to_all.24 = f32[1,32,16,256]{3,2,0,1:T(8,128)S(1)} all-to-all(f32[1,32,16,256]{3,2,0,1:T(8,128)S(1)} %add_bitcast_fusion), channel_id=1, replica_groups=mesh['aa'=32,'ba'=8] {'aa'}, dimensions={1} | all-to-all | bytes 1048576 | tf_op jit(solution)/shard_map/all_to_all | solution.py:130
  79.2 0.4 reshape.224
  79.6 0.6 fusion.5
  80.3 23.0 %all_to_all.25 = f32[256,1,128]{2,1,0:T(1,128)S(1)} all-to-all(f32[256,1,128]{2,1,0:T(1,128)S(1)} %bitcast.25), channel_id=1, replica_groups=mesh['aa'=32,'ba'=8] {'aa','ba'}, dimensions={0} | all-to-all | bytes 262144 | tf_op jit(solution)/shard_map/all_to_all | solution.py:65
  103.7 18.3 %all_to_all.26 = f32[256,1,128]{2,1,0:T(1,128)S(1)} all-to-all(f32[256,1,128]{2,1,0:T(1,128)S(1)} %broadcast_in_dim.2), channel_id=1, replica_groups=mesh['aa'=32,'ba'=8] {'aa','ba'}, dimensions={0} | all-to-all | bytes 262144 | tf_op jit(solution)/shard_map/all_to_all | solution.py:67
  122.0 0.5 broadcast.243
  122.5 0.9 reduce.4
  123.5 0.8 reshape.225.a_ref
  124.3 10.2 %shard_map.31 = (f32[8,64,64]{2,1,0:T(8,128)}, f32[8,64,64]{2,1,0:T(8,128)}) custom-call(f32[8,64,64]{2,1,0:T(8,128)} %reshape.225.a_ref), custom_call_target="tpu_custom_call" | custom-call | tf_op jit(solution)/shard_map/pallas_call | solution.py:56
  134.5 2.3 %convolution_multiply_fusion = f32[8,64,256]{2,1,0:T(8,128)} fusion(f32[8,64,64]{2,1,0:T(8,128)} %get-tuple-element.5, f32[8,64,256]{2,1,0:T(8,128)S(1)} %reshape.224), kind=kOutput, calls=%fused_computation.3 | convolution fusion | flops 100794368 | bytes 1179648 | tf_op jit(solution)/shard_map/fij,fjp->fip/dot_general | solution.py:139
  (11 shorter events, 1.1 us)
Async XLA Ops:
  14.8 7.2 %collective-permute-start = (f32[4,32,16,256]{3,2,1,0:T(8,128)S(1)}, f32[4,32,16,256]{3,2,1,0:T(8,128)}, u32[]{:S(2)}, u32[]{:S(2)}) collective-permute-start(f32[4,32,16,256]{3,2,1,0:T(8,128)S(1)} %slice_bitcast_fusion), channel_id=1, source_target_pairs={{0,1},{1,0},{2,3},{3,2},{4,5},{5,4},{6,7},{7,6},{8,9},{9,8},{10,11... | collective-permute-start | bytes 6291464 | tf_op jit(solution)/shard_map/ppermute | solution.py:109
  25.6 15.2 %collective-permute-start.1 = (f32[1,32,16,256]{3,2,1,0:T(8,128)}, f32[1,32,16,256]{3,2,1,0:T(8,128)}, u32[]{:S(2)}, u32[]{:S(2)}) collective-permute-start(f32[1,32,16,256]{3,2,1,0:T(8,128)} %get-tuple-element.6), channel_id=1, source_target_pairs={{0,2},{1,3},{2,4},{3,5},{4,6},{5,7},{6,0},{7,1},{8,10},{9,11},{10,... | collective-permute-start | bytes 1572872 | tf_op jit(solution)/shard_map/ppermute | solution.py:114
  25.6 25.4 %collective-permute-start.2 = (f32[1,32,16,256]{3,2,1,0:T(8,128)S(1)}, f32[1,32,16,256]{3,2,1,0:T(8,128)}, u32[]{:S(2)}, u32[]{:S(2)}) collective-permute-start(f32[1,32,16,256]{3,2,1,0:T(8,128)S(1)} %get-tuple-element.8), channel_id=1, source_target_pairs={{0,4},{1,5},{2,6},{3,7},{4,0},{5,1},{6,2},{7,3},{8,12},{9,13},{10,... | collective-permute-start | bytes 1572872 | tf_op jit(solution)/shard_map/ppermute | solution.py:114
  27.7 23.9 %collective-permute-start.3 = (f32[1,32,16,256]{3,2,1,0:T(8,128)S(1)}, f32[1,32,16,256]{3,2,1,0:T(8,128)}, u32[]{:S(2)}, u32[]{:S(2)}) collective-permute-start(f32[1,32,16,256]{3,2,1,0:T(8,128)S(1)} %get-tuple-element.7), channel_id=1, source_target_pairs={{0,6},{1,7},{2,0},{3,1},{4,2},{5,3},{6,4},{7,5},{8,14},{9,15},{10,... | collective-permute-start | bytes 1572872 | tf_op jit(solution)/shard_map/ppermute | solution.py:114

commit v11 on v10

--- a/solution.py
+++ b/solution.py
@@ -67,17 +67,23 @@
     return lax.all_to_all(spread, axes, 0, 0, tiled=True).reshape(x.shape)
 
 
-def _dft_kernel(core_ref, table_ref, snap_ref, out_ref):
-    _, chips, a_step, _, pts_dev = out_ref.shape
+def _dft_kernel(core_ref, table_ref, snap_ref, sent_ref, kept_ref):
+    chips, a_step, _, pts_dev = kept_ref.shape
     core = core_ref[0]
     res = jnp.dot(table_ref[...], snap_ref[...], precision=lax.Precision.HIGHEST,
                   preferred_element_type=jnp.float32)
     for a in range(a_step):
         for v in range(2 * chips):
-            cv = v % 2
-            keep = 1 - (cv + core - 2 * cv * core)
             start = (a * 2 * chips + v) * pts_dev
-            out_ref[keep, v // 2, a] = res[:, start:start + pts_dev]
+            piece = res[:, start:start + pts_dev]
+
+            @pl.when(core == v % 2)
+            def _():
+                kept_ref[v // 2, a] = piece
+
+            @pl.when(core != v % 2)
+            def _():
+                sent_ref[v // 2, a] = piece
 
 
 def partial_dft(table_t, snapshots, core, n_aa, n_ba):
@@ -86,6 +92,8 @@
     points = snapshots.shape[1]
     pts_dev = points // (n_aa * n_ba)
     width = a_step * n_ba * pts_dev
+    half = pl.BlockSpec((n_ba // 2, a_step, rows, pts_dev), lambda i, c: (0, i, 0, 0))
+    shape = jax.ShapeDtypeStruct((n_ba // 2, n_aa, rows, pts_dev), jnp.float32)
     return pl.pallas_call(
         _dft_kernel,
         grid_spec=pltpu.PrefetchScalarGridSpec(
@@ -95,18 +103,18 @@
                 pl.BlockSpec((rows, time_dev), lambda i, c: (0, 0)),
                 pl.BlockSpec((time_dev, width), lambda i, c: (0, i)),
             ],
-            out_specs=pl.BlockSpec((2, n_ba // 2, a_step, rows, pts_dev), lambda i, c: (0, 0, i, 0, 0)),
+            out_specs=[half, half],
         ),
-        out_shape=jax.ShapeDtypeStruct((2, n_ba // 2, n_aa, rows, pts_dev), jnp.float32),
+        out_shape=(shape, shape),
     )(core, table_t, snapshots)
 
 
-def sum_over_ba(partial, n_ba):
+def sum_over_ba(sent, kept, n_ba):
     u = lax.axis_index("ba")
     cores = 2
     chips = n_ba // cores
     y = u // cores
-    chip_sum = partial[1] + lax.ppermute(partial[0], "ba", [(i, i ^ 1) for i in range(n_ba)])
+    chip_sum = kept + lax.ppermute(sent, "ba", [(i, i ^ 1) for i in range(n_ba)])
     total = lax.dynamic_index_in_dim(chip_sum, y, axis=0, keepdims=True)
     for shift in range(1, chips):
         out = lax.dynamic_index_in_dim(chip_sum, (y + shift) % chips, axis=0, keepdims=True)
@@ -125,8 +133,8 @@
     table = spectral_rows(block_len, points, u * time_dev, time_dev)
     table_t = jnp.transpose(table, (2, 1, 0)).reshape(2 * FREQS, time_dev)
     core = (u % 2).astype(jnp.int32).reshape(1)
-    partial = partial_dft(table_t, snapshots, core, n_aa, n_ba)
-    block_spec = sum_over_ba(partial, n_ba)
+    sent, kept = partial_dft(table_t, snapshots, core, n_aa, n_ba)
+    block_spec = sum_over_ba(sent, kept, n_ba)
     spectra = lax.all_to_all(block_spec, "aa", split_axis=1, concat_axis=0, tiled=True)
     blocks = spectra.shape[0]
     columns = 2 * blocks

time: 137 us -> 138 us (level)
  waiting for transfers between devices: 26.7 us -> 29.6 us
    all_to_all x1, blocking collectives: 23 us -> 20.1 us  [all_sum(): mine = lax.all_to_all(pieces, axes, 0, 0, tiled=True).sum(0, keepdims=True)]
    ppermute x3, waiting for transfers between devices: 22.8 us -> 25.6 us  [sum_over_ba(): total = total + lax.ppermute(out, 'ba', perm)]
    squeeze x1 -> x0, local copies, waits for them, and re-layouts: 1.76 us -> none  [sum_over_ba(): partial[0]]
    all_to_all x1, blocking collectives: 25.6 us -> 27.3 us  [local(): lax.all_to_all(block_spec, 'aa', split_axis=1, concat_axis=0, tiled=True)]
where the time goes in v11:
time: 138 us
  blocking collectives  65.7 us (48%)
  waiting for transfers between devices  29.6 us (21%)
  Pallas kernels  21.2 us (15%)
  other arithmetic  6.33 us (5%)
  starting transfers between devices  5.26 us (4%)
  local copies, waits for them, and re-layouts  5.2 us (4%)
  matrix products  2.92 us (2%)
  between operations  1.4 us (1%)
    all_to_all x1, blocking collectives, local(): lax.all_to_all(block_spec, 'aa', split_axis=1, concat_axis=0, tiled=True)  27.3 us
    ppermute x3, waiting for transfers between devices, sum_over_ba(): total = total + lax.ppermute(out, 'ba', perm)  25.6 us
    all_to_all x1, blocking collectives, all_sum(): mine = lax.all_to_all(pieces, axes, 0, 0, tiled=True).sum(0, keepdims=True)  20.1 us
    all_to_all x1, blocking collectives, all_sum(): return lax.all_to_all(spread, axes, 0, 0, tiled=True).reshape(x.shape)  18.3 us
    pallas_call x1, Pallas kernels, partial_dft(): pl.pallas_call(_dft_kernel, grid_spec=pltpu.PrefetchScalarGridSpec(num_sc...  10.9 us
    pallas_call x1, Pallas kernels, factor(): pl.pallas_call(_factor_kernel, out_shape=(jax.ShapeDtypeStruct(gram.shape...  10.2 us
    ppermute x1, waiting for transfers between devices, sum_over_ba(): lax.ppermute(sent, 'ba', [(i, i ^ 1) for i in range(n_ba)])  4 us
    ppermute x1, starting transfers between devices, sum_over_ba(): lax.ppermute(sent, 'ba', [(i, i ^ 1) for i in range(n_ba)])  3.22 us
  transfers between devices with their start and end apart: 4, of which 4 were waited for; matrix products, arithmetic and copies ran while one was open for 0% of the time, Pallas kernels for 0%

profile of v11, /device:TPU:1, one launch (start us, length us, event | category | flops | bytes accessed | tf_op | source)
XLA Modules:
  0.0 137.7 jit_solution(10438668915821107681)
XLA Ops:
  0.6 0.6 multiply_reduce_fusion
  2.2 0.6 copy.7
  2.8 10.9 %shard_map.30 = (f32[4,32,16,256]{3,2,1,0:T(8,128)}, f32[4,32,16,256]{3,2,1,0:T(8,128)}) custom-call(s32[1]{0:T(128)} %bitcast.core_ref, f32[16,32]{1,0:T(8,128)} %bitcast.20, f32[32,65536]{1,0:T(8,128)} %snap_ref.1), custom_call_target="tpu_custom_call" | custom-call | tf_op jit(solution)/shard_map/pallas_call | solution.py:97
  13.7 3.2 %collective-permute-start = (f32[4,32,16,256]{3,2,1,0:T(8,128)}, f32[4,32,16,256]{3,2,1,0:T(8,128)S(1)}, u32[]{:S(2)}, u32[]{:S(2)}) collective-permute-start(f32[4,32,16,256]{3,2,1,0:T(8,128)} %get-tuple-element.7), channel_id=1, source_target_pairs={{0,1},{1,0},{2,3},{3,2},{4,5},{5,4},{6,7},{7,6},{8,9},{9,8},{10,11... | collective-permute-start | bytes 6291464 | tf_op jit(solution)/shard_map/ppermute | solution.py:117
  16.9 4.0 %collective-permute-done = f32[4,32,16,256]{3,2,1,0:T(8,128)S(1)} collective-permute-done((f32[4,32,16,256]{3,2,1,0:T(8,128)}, f32[4,32,16,256]{3,2,1,0:T(8,128)S(1)}, u32[]{:S(2)}, u32[]{:S(2)}) %collective-permute-start) | collective-permute-done | bytes 2097184 | tf_op jit(solution)/shard_map/ppermute | solution.py:117
  20.9 1.3 copy-done
  22.2 2.7 %add.93 = f32[4,32,16,256]{3,2,1,0:T(8,128)S(1)} add(f32[4,32,16,256]{3,2,1,0:T(8,128)} %get-tuple-element.6, f32[4,32,16,256]{3,2,1,0:T(8,128)} %copy-done) | non-fusion elementwise | flops 524288 | bytes 6291456 | tf_op jit(solution)/shard_map/add | solution.py:117
  24.9 1.0 constant_dynamic-slice_fusion.2
  25.9 1.0 collective-permute-start.3
  27.2 0.7 collective-permute-start.1
  27.9 11.4 %collective-permute-done.3 = f32[1,32,16,256]{3,2,1,0:T(8,128)} collective-permute-done((f32[1,32,16,256]{3,2,1,0:T(8,128)}, f32[1,32,16,256]{3,2,1,0:T(8,128)}, u32[]{:S(2)}, u32[]{:S(2)}) %collective-permute-start.3) | collective-permute-done | bytes 524320 | tf_op jit(solution)/shard_map/ppermute | solution.py:122
  39.3 2.0 %collective-permute-done.2 = f32[1,32,16,256]{3,2,1,0:T(8,128)} collective-permute-done((f32[1,32,16,256]{3,2,1,0:T(8,128)S(1)}, f32[1,32,16,256]{3,2,1,0:T(8,128)}, u32[]{:S(2)}, u32[]{:S(2)}) %collective-permute-start.2) | collective-permute-done | bytes 524320 | tf_op jit(solution)/shard_map/ppermute | solution.py:122
  41.3 12.2 %collective-permute-done.1 = f32[1,32,16,256]{3,2,1,0:T(8,128)} collective-permute-done((f32[1,32,16,256]{3,2,1,0:T(8,128)S(1)}, f32[1,32,16,256]{3,2,1,0:T(8,128)}, u32[]{:S(2)}, u32[]{:S(2)}) %collective-permute-start.1) | collective-permute-done | bytes 524320 | tf_op jit(solution)/shard_map/ppermute | solution.py:122
  53.6 1.6 %add_bitcast_fusion = f32[1,32,16,256]{3,2,0,1:T(8,128)S(1)} fusion(f32[1,32,16,256]{3,2,1,0:T(8,128)} %collective-permute-done.3, f32[1,32,16,256]{3,2,1,0:T(8,128)} %collective-permute-done.2, f32[1,32,16,256]{3,2,1,0:T(8,128)} %collective-permute-done.1, f32[4,32,16,256]{3,2,1,0:T(8,128)S(1)} %add.93, s32[]{:T(128)S(6)} %select_n.56), kind=kLoop, calls=%fused_computation.2 | loop fusion | flops 393216 | bytes 2621444 | tf_op jit(solution)/shard_map/add | solution.py:122
  55.1 27.3 %all_to_all.24 = f32[1,32,16,256]{3,2,0,1:T(8,128)S(1)} all-to-all(f32[1,32,16,256]{3,2,0,1:T(8,128)S(1)} %add_bitcast_fusion), channel_id=1, replica_groups=mesh['aa'=32,'ba'=8] {'aa'}, dimensions={1} | all-to-all | bytes 1048576 | tf_op jit(solution)/shard_map/all_to_all | solution.py:138
  82.9 0.4 reshape.224
  83.3 0.6 fusion.4
  84.0 20.1 %all_to_all.25 = f32[256,1,128]{2,1,0:T(1,128)S(1)} all-to-all(f32[256,1,128]{2,1,0:T(1,128)S(1)} %bitcast.19), channel_id=1, replica_groups=mesh['aa'=32,'ba'=8] {'aa','ba'}, dimensions={0} | all-to-all | bytes 262144 | tf_op jit(solution)/shard_map/all_to_all | solution.py:65
  104.5 18.3 %all_to_all.26 = f32[256,1,128]{2,1,0:T(1,128)S(1)} all-to-all(f32[256,1,128]{2,1,0:T(1,128)S(1)} %broadcast_in_dim.2), channel_id=1, replica_groups=mesh['aa'=32,'ba'=8] {'aa','ba'}, dimensions={0} | all-to-all | bytes 262144 | tf_op jit(solution)/shard_map/all_to_all | solution.py:67
  122.8 0.5 broadcast.243
  123.3 0.9 reduce.4
  124.3 0.8 reshape.225.a_ref
  125.1 10.2 %shard_map.31 = (f32[8,64,64]{2,1,0:T(8,128)}, f32[8,64,64]{2,1,0:T(8,128)}) custom-call(f32[8,64,64]{2,1,0:T(8,128)} %reshape.225.a_ref), custom_call_target="tpu_custom_call" | custom-call | tf_op jit(solution)/shard_map/pallas_call | solution.py:56
  135.3 2.3 %convolution_multiply_fusion = f32[8,64,256]{2,1,0:T(8,128)} fusion(f32[8,64,64]{2,1,0:T(8,128)} %get-tuple-element.9, f32[8,64,256]{2,1,0:T(8,128)S(1)} %reshape.224), kind=kOutput, calls=%fused_computation | convolution fusion | flops 100794368 | bytes 1179648 | tf_op jit(solution)/shard_map/fij,fjp->fip/dot_general | solution.py:147
  (12 shorter events, 1.5 us)
Async XLA Ops:
  13.7 7.2 %collective-permute-start = (f32[4,32,16,256]{3,2,1,0:T(8,128)}, f32[4,32,16,256]{3,2,1,0:T(8,128)S(1)}, u32[]{:S(2)}, u32[]{:S(2)}) collective-permute-start(f32[4,32,16,256]{3,2,1,0:T(8,128)} %get-tuple-element.7), channel_id=1, source_target_pairs={{0,1},{1,0},{2,3},{3,2},{4,5},{5,4},{6,7},{7,6},{8,9},{9,8},{10,11... | collective-permute-start | bytes 6291464 | tf_op jit(solution)/shard_map/ppermute | solution.py:117
  20.9 1.3 copy-start
  25.9 13.5 %collective-permute-start.3 = (f32[1,32,16,256]{3,2,1,0:T(8,128)}, f32[1,32,16,256]{3,2,1,0:T(8,128)}, u32[]{:S(2)}, u32[]{:S(2)}) collective-permute-start(f32[1,32,16,256]{3,2,1,0:T(8,128)} %get-tuple-element.11), channel_id=1, source_target_pairs={{0,6},{1,7},{2,0},{3,1},{4,2},{5,3},{6,4},{7,5},{8,14},{9,15},{10,... | collective-permute-start | bytes 1572872 | tf_op jit(solution)/shard_map/ppermute | solution.py:122
  26.9 14.5 %collective-permute-start.2 = (f32[1,32,16,256]{3,2,1,0:T(8,128)S(1)}, f32[1,32,16,256]{3,2,1,0:T(8,128)}, u32[]{:S(2)}, u32[]{:S(2)}) collective-permute-start(f32[1,32,16,256]{3,2,1,0:T(8,128)S(1)} %get-tuple-element.12), channel_id=1, source_target_pairs={{0,4},{1,5},{2,6},{3,7},{4,0},{5,1},{6,2},{7,3},{8,12},{9,13},{10,... | collective-permute-start | bytes 1572872 | tf_op jit(solution)/shard_map/ppermute | solution.py:122
  27.2 26.3 %collective-permute-start.1 = (f32[1,32,16,256]{3,2,1,0:T(8,128)S(1)}, f32[1,32,16,256]{3,2,1,0:T(8,128)}, u32[]{:S(2)}, u32[]{:S(2)}) collective-permute-start(f32[1,32,16,256]{3,2,1,0:T(8,128)S(1)} %get-tuple-element.10), channel_id=1, source_target_pairs={{0,2},{1,3},{2,4},{3,5},{4,6},{5,7},{6,0},{7,1},{8,10},{9,11},{10,... | collective-permute-start | bytes 1572872 | tf_op jit(solution)/shard_map/ppermute | solution.py:122

commit v12 on v10

--- a/solution.py
+++ b/solution.py
@@ -1,3 +1,4 @@
+import functools
 import math
 
 import jax
@@ -26,7 +27,7 @@
     return jnp.stack([cosine, sine], axis=1)
 
 
-def _factor_kernel(a_ref, upper_ref, inv_ref, m_ref):
+def _factor_kernel(scale, a_ref, cols_ref, upper_ref, modes_ref, m_ref):
     freqs, n, _ = a_ref.shape
     rows = lax.broadcasted_iota(jnp.int32, (freqs, n, 2 * n), 1)
     lanes = lax.broadcasted_iota(jnp.int32, (freqs, n, 2 * n), 2)
@@ -48,16 +49,18 @@
         lax.fori_loop(0, tile, step, 0)
     m = m_ref[...]
     upper_ref[...] = jnp.where(rows[:, :, :n] <= lanes[:, :, :n], m[:, :, :n], 0.0)
-    inv_ref[...] = m[:, :, n:]
+    for f in range(freqs):
+        modes_ref[f] = scale * jnp.dot(m[f, :, n:], cols_ref[f], precision=lax.Precision.HIGHEST,
+                                       preferred_element_type=jnp.float32)
 
 
-def factor(gram):
+def factor_and_modes(gram, cols, scale):
     freqs, n, _ = gram.shape
     return pl.pallas_call(
-        _factor_kernel,
-        out_shape=(jax.ShapeDtypeStruct(gram.shape, gram.dtype), jax.ShapeDtypeStruct(gram.shape, gram.dtype)),
+        functools.partial(_factor_kernel, scale),
+        out_shape=(jax.ShapeDtypeStruct(gram.shape, gram.dtype), jax.ShapeDtypeStruct(cols.shape, cols.dtype)),
         scratch_shapes=[pltpu.VMEM((freqs, n, 2 * n), jnp.float32)],
-    )(gram)
+    )(gram, cols)
 
 
 def all_sum(x, axes, count):
@@ -135,10 +138,7 @@
     )
     product = jnp.einsum("fip,fjp->fij", cols, cols, precision=lax.Precision.HIGHEST)
     gram_sum = all_sum(product, ("aa", "ba"), n_aa * n_ba)
-    upper_factor, inverse = factor(gram_sum)
-    pod_modes = math.sqrt(points) * jnp.einsum(
-        "fij,fjp->fip", inverse, cols, precision=lax.Precision.HIGHEST
-    )
+    upper_factor, pod_modes = factor_and_modes(gram_sum, cols, math.sqrt(points))
     return (upper_factor, pod_modes)
 
 

time: 137 us -> 136 us (level)
  matrix products: 2.92 us -> 0.6 us
    dot_general x1 -> x0, matrix products: 2.32 us -> none  [local(): jnp.einsum('fij,fjp->fip', inverse, cols, precision=lax.Precision.HIGHEST)]
where the time goes in v12:
time: 136 us; the launch traced here: 135 us
  blocking collectives  66.9 us (49%)
  waiting for transfers between devices  26.7 us (20%)
  Pallas kernels  21.2 us (16%)
  starting transfers between devices  6.46 us (5%)
  other arithmetic  6.34 us (5%)
  local copies, waits for them, and re-layouts  5.66 us (4%)
  between operations  1.41 us (1%)
    all_to_all x1, blocking collectives, local(): lax.all_to_all(block_spec, 'aa', split_axis=1, concat_axis=0, tiled=True)  25.6 us
    all_to_all x1, blocking collectives, all_sum(): mine = lax.all_to_all(pieces, axes, 0, 0, tiled=True).sum(0, keepdims=True)  23 us
    ppermute x3, waiting for transfers between devices, sum_over_ba(): total = total + lax.ppermute(out, 'ba', perm)  22.8 us
    all_to_all x1, blocking collectives, all_sum(): return lax.all_to_all(spread, axes, 0, 0, tiled=True).reshape(x.shape)  18.3 us
    pallas_call x1, Pallas kernels, factor_and_modes(): pl.pallas_call(functools.partial(_factor_kernel, scale), out_shape=(jax.S...  11 us
    pallas_call x1, Pallas kernels, partial_dft(): pl.pallas_call(_dft_kernel, grid_spec=pltpu.PrefetchScalarGridSpec(num_sc...  10.2 us
    ppermute x1, waiting for transfers between devices, sum_over_ba(): lax.ppermute(partial[0], 'ba', [(i, i ^ 1) for i in range(n_ba)])  3.92 us
    ppermute x1, starting transfers between devices, sum_over_ba(): lax.ppermute(partial[0], 'ba', [(i, i ^ 1) for i in range(n_ba)])  3.27 us
  transfers between devices with their start and end apart: 4, of which 4 were waited for; matrix products, arithmetic and copies ran while one was open for 0% of the time, Pallas kernels for 0%

profile of v12, /device:TPU:1, one launch (start us, length us, event | category | flops | bytes accessed | tf_op | source)
XLA Modules:
  0.0 135.3 jit_solution(13737533921306878398)
XLA Ops:
  0.7 0.6 multiply_reduce_fusion
  2.2 0.6 copy.7
  2.8 10.2 %shard_map.30 = f32[2,4,32,16,256]{4,3,2,1,0:T(8,128)} custom-call(s32[1]{0:T(128)} %bitcast.core_ref, f32[16,32]{1,0:T(8,128)} %bitcast.24, f32[32,65536]{1,0:T(8,128)} %snap_ref.1), custom_call_target="tpu_custom_call" | custom-call | tf_op jit(solution)/shard_map/pallas_call | solution.py:92
  13.0 1.8 %slice_bitcast_fusion = f32[4,32,16,256]{3,2,1,0:T(8,128)S(1)} fusion(f32[2,4,32,16,256]{4,3,2,1,0:T(8,128)} %shard_map.30), kind=kLoop, calls=%fused_computation | loop fusion | bytes 4194304 | tf_op jit(solution)/shard_map/squeeze | solution.py:112
  14.8 3.3 %collective-permute-start = (f32[4,32,16,256]{3,2,1,0:T(8,128)S(1)}, f32[4,32,16,256]{3,2,1,0:T(8,128)}, u32[]{:S(2)}, u32[]{:S(2)}) collective-permute-start(f32[4,32,16,256]{3,2,1,0:T(8,128)S(1)} %slice_bitcast_fusion), channel_id=1, source_target_pairs={{0,1},{1,0},{2,3},{3,2},{4,5},{5,4},{6,7},{7,6},{8,9},{9,8},{10,11... | collective-permute-start | bytes 6291464 | tf_op jit(solution)/shard_map/ppermute | solution.py:112
  18.0 3.9 %collective-permute-done = f32[4,32,16,256]{3,2,1,0:T(8,128)} collective-permute-done((f32[4,32,16,256]{3,2,1,0:T(8,128)S(1)}, f32[4,32,16,256]{3,2,1,0:T(8,128)}, u32[]{:S(2)}, u32[]{:S(2)}) %collective-permute-start) | collective-permute-done | bytes 2097184 | tf_op jit(solution)/shard_map/ppermute | solution.py:112
  22.0 2.7 %fusion = f32[4,32,16,256]{3,2,1,0:T(8,128)S(1)} fusion(f32[4,32,16,256]{3,2,1,0:T(8,128)} %collective-permute-done, f32[2,4,32,16,256]{4,3,2,1,0:T(8,128)} %shard_map.30), kind=kLoop, calls=%fused_computation.2 | loop fusion | flops 524288 | bytes 6291456 | tf_op jit(solution)/shard_map/add | solution.py:112
  24.7 0.9 constant_dynamic-slice_fusion.2
  25.6 2.1 %collective-permute-start.2 = (f32[1,32,16,256]{3,2,1,0:T(8,128)S(1)}, f32[1,32,16,256]{3,2,1,0:T(8,128)}, u32[]{:S(2)}, u32[]{:S(2)}) collective-permute-start(f32[1,32,16,256]{3,2,1,0:T(8,128)S(1)} %get-tuple-element.4), channel_id=1, source_target_pairs={{0,4},{1,5},{2,6},{3,7},{4,0},{5,1},{6,2},{7,3},{8,12},{9,13},{10,... | collective-permute-start | bytes 1572872 | tf_op jit(solution)/shard_map/ppermute | solution.py:117
  27.7 1.1 collective-permute-start.3
  28.8 12.0 %collective-permute-done.1 = f32[1,32,16,256]{3,2,1,0:T(8,128)} collective-permute-done((f32[1,32,16,256]{3,2,1,0:T(8,128)}, f32[1,32,16,256]{3,2,1,0:T(8,128)}, u32[]{:S(2)}, u32[]{:S(2)}) %collective-permute-start.1) | collective-permute-done | bytes 524320 | tf_op jit(solution)/shard_map/ppermute | solution.py:117
  40.8 10.2 %collective-permute-done.2 = f32[1,32,16,256]{3,2,1,0:T(8,128)} collective-permute-done((f32[1,32,16,256]{3,2,1,0:T(8,128)S(1)}, f32[1,32,16,256]{3,2,1,0:T(8,128)}, u32[]{:S(2)}, u32[]{:S(2)}) %collective-permute-start.2) | collective-permute-done | bytes 524320 | tf_op jit(solution)/shard_map/ppermute | solution.py:117
  51.0 0.6 collective-permute-done.3
  51.6 1.6 %add_bitcast_fusion = f32[1,32,16,256]{3,2,0,1:T(8,128)S(1)} fusion(f32[1,32,16,256]{3,2,1,0:T(8,128)} %collective-permute-done.3, f32[1,32,16,256]{3,2,1,0:T(8,128)} %collective-permute-done.2, f32[1,32,16,256]{3,2,1,0:T(8,128)} %collective-permute-done.1, f32[4,32,16,256]{3,2,1,0:T(8,128)S(1)} %fusion, s32[]{:T(128)S(6)} %select_n.56), kind=kLoop, calls=%fused_computation.4 | loop fusion | flops 393216 | bytes 2621444 | tf_op jit(solution)/shard_map/add | solution.py:117
  53.2 25.6 %all_to_all.24 = f32[1,32,16,256]{3,2,0,1:T(8,128)S(1)} all-to-all(f32[1,32,16,256]{3,2,0,1:T(8,128)S(1)} %add_bitcast_fusion), channel_id=1, replica_groups=mesh['aa'=32,'ba'=8] {'aa'}, dimensions={1} | all-to-all | bytes 1048576 | tf_op jit(solution)/shard_map/all_to_all | solution.py:133
  78.7 0.3 reshape.223
  79.2 0.4 reshape.224.cols_ref
  79.6 0.6 fusion.5
  80.3 23.0 %all_to_all.25 = f32[256,1,128]{2,1,0:T(1,128)S(1)} all-to-all(f32[256,1,128]{2,1,0:T(1,128)S(1)} %bitcast.23), channel_id=1, replica_groups=mesh['aa'=32,'ba'=8] {'aa','ba'}, dimensions={0} | all-to-all | bytes 262144 | tf_op jit(solution)/shard_map/all_to_all | solution.py:68
  103.7 18.3 %all_to_all.26 = f32[256,1,128]{2,1,0:T(1,128)S(1)} all-to-all(f32[256,1,128]{2,1,0:T(1,128)S(1)} %broadcast_in_dim.2), channel_id=1, replica_groups=mesh['aa'=32,'ba'=8] {'aa','ba'}, dimensions={0} | all-to-all | bytes 262144 | tf_op jit(solution)/shard_map/all_to_all | solution.py:70
  122.0 0.5 broadcast.243
  122.5 0.9 reduce.4
  123.5 0.8 reshape.225.a_ref
  124.3 11.0 %shard_map.31 = (f32[8,64,64]{2,1,0:T(8,128)}, f32[8,64,256]{2,1,0:T(8,128)}) custom-call(f32[8,64,64]{2,1,0:T(8,128)} %reshape.225.a_ref, f32[8,64,256]{2,1,0:T(8,128)} %copy-done), custom_call_target="tpu_custom_call" | custom-call | tf_op jit(solution)/shard_map/pallas_call | solution.py:59
  (12 shorter events, 0.8 us)
Async XLA Ops:
  14.8 7.2 %collective-permute-start = (f32[4,32,16,256]{3,2,1,0:T(8,128)S(1)}, f32[4,32,16,256]{3,2,1,0:T(8,128)}, u32[]{:S(2)}, u32[]{:S(2)}) collective-permute-start(f32[4,32,16,256]{3,2,1,0:T(8,128)S(1)} %slice_bitcast_fusion), channel_id=1, source_target_pairs={{0,1},{1,0},{2,3},{3,2},{4,5},{5,4},{6,7},{7,6},{8,9},{9,8},{10,11... | collective-permute-start | bytes 6291464 | tf_op jit(solution)/shard_map/ppermute | solution.py:112
  25.6 15.2 %collective-permute-start.1 = (f32[1,32,16,256]{3,2,1,0:T(8,128)}, f32[1,32,16,256]{3,2,1,0:T(8,128)}, u32[]{:S(2)}, u32[]{:S(2)}) collective-permute-start(f32[1,32,16,256]{3,2,1,0:T(8,128)} %get-tuple-element.2), channel_id=1, source_target_pairs={{0,2},{1,3},{2,4},{3,5},{4,6},{5,7},{6,0},{7,1},{8,10},{9,11},{10,... | collective-permute-start | bytes 1572872 | tf_op jit(solution)/shard_map/ppermute | solution.py:117
  25.6 25.4 %collective-permute-start.2 = (f32[1,32,16,256]{3,2,1,0:T(8,128)S(1)}, f32[1,32,16,256]{3,2,1,0:T(8,128)}, u32[]{:S(2)}, u32[]{:S(2)}) collective-permute-start(f32[1,32,16,256]{3,2,1,0:T(8,128)S(1)} %get-tuple-element.4), channel_id=1, source_target_pairs={{0,4},{1,5},{2,6},{3,7},{4,0},{5,1},{6,2},{7,3},{8,12},{9,13},{10,... | collective-permute-start | bytes 1572872 | tf_op jit(solution)/shard_map/ppermute | solution.py:117
  27.7 23.9 %collective-permute-start.3 = (f32[1,32,16,256]{3,2,1,0:T(8,128)S(1)}, f32[1,32,16,256]{3,2,1,0:T(8,128)}, u32[]{:S(2)}, u32[]{:S(2)}) collective-permute-start(f32[1,32,16,256]{3,2,1,0:T(8,128)S(1)} %get-tuple-element.3), channel_id=1, source_target_pairs={{0,6},{1,7},{2,0},{3,1},{4,2},{5,3},{6,4},{7,5},{8,14},{9,15},{10,... | collective-permute-start | bytes 1572872 | tf_op jit(solution)/shard_map/ppermute | solution.py:117
  79.6 44.7 %copy-start = (f32[8,64,256]{2,1,0:T(8,128)}, f32[8,64,256]{2,1,0:T(8,128)S(1)}, u32[]{:S(2)}) copy-start(f32[8,64,256]{2,1,0:T(8,128)S(1)} %reshape.224.cols_ref) | copy-start | bytes 1572868

commit v13 on v12

--- a/solution.py
+++ b/solution.py
@@ -84,7 +84,7 @@
 
 
 def partial_dft(table_t, snapshots, core, n_aa, n_ba):
-    a_step = math.gcd(4, n_aa)
+    a_step = math.gcd(8, n_aa)
     rows, time_dev = table_t.shape
     points = snapshots.shape[1]
     pts_dev = points // (n_aa * n_ba)

time: 136 us -> 134 us (0.985)
  Pallas kernels: 21.2 us -> 19.6 us
    pallas_call x1, Pallas kernels: 10.2 us -> 8.58 us  [partial_dft(): pl.pallas_call(_dft_kernel, grid_spec=pltpu.PrefetchScalarGridSpec(num_sc...]
where the time goes in v13:
time: 134 us
  blocking collectives  67.1 us (50%)
  waiting for transfers between devices  26.4 us (20%)
  Pallas kernels  19.6 us (15%)
  starting transfers between devices  6.82 us (5%)
  other arithmetic  6.34 us (5%)
  local copies, waits for them, and re-layouts  5.66 us (4%)
  between operations  1.41 us (1%)
    all_to_all x1, blocking collectives, local(): lax.all_to_all(block_spec, 'aa', split_axis=1, concat_axis=0, tiled=True)  25.7 us
    all_to_all x1, blocking collectives, all_sum(): mine = lax.all_to_all(pieces, axes, 0, 0, tiled=True).sum(0, keepdims=True)  23 us
    ppermute x3, waiting for transfers between devices, sum_over_ba(): total = total + lax.ppermute(out, 'ba', perm)  22.5 us
    all_to_all x1, blocking collectives, all_sum(): return lax.all_to_all(spread, axes, 0, 0, tiled=True).reshape(x.shape)  18.3 us
    pallas_call x1, Pallas kernels, factor_and_modes(): pl.pallas_call(functools.partial(_factor_kernel, scale), out_shape=(jax.S...  11 us
    pallas_call x1, Pallas kernels, partial_dft(): pl.pallas_call(_dft_kernel, grid_spec=pltpu.PrefetchScalarGridSpec(num_sc...  8.58 us
    ppermute x1, waiting for transfers between devices, sum_over_ba(): lax.ppermute(partial[0], 'ba', [(i, i ^ 1) for i in range(n_ba)])  3.92 us
    ppermute x3, starting transfers between devices, sum_over_ba(): total = total + lax.ppermute(out, 'ba', perm)  3.5 us
  transfers between devices with their start and end apart: 4, of which 4 were waited for; matrix products, arithmetic and copies ran while one was open for 0% of the time, Pallas kernels for 0%

profile of v13, /device:TPU:1, one launch (start us, length us, event | category | flops | bytes accessed | tf_op | source)
XLA Modules:
  0.0 133.9 jit_solution(168866148061900171)
XLA Ops:
  0.7 0.6 multiply_reduce_fusion
  2.2 0.6 copy.7
  2.8 8.6 %shard_map.30 = f32[2,4,32,16,256]{4,3,2,1,0:T(8,128)} custom-call(s32[1]{0:T(128)} %bitcast.core_ref, f32[16,32]{1,0:T(8,128)} %bitcast.24, f32[32,65536]{1,0:T(8,128)} %snap_ref.1), custom_call_target="tpu_custom_call" | custom-call | tf_op jit(solution)/shard_map/pallas_call | solution.py:92
  11.4 1.8 %slice_bitcast_fusion = f32[4,32,16,256]{3,2,1,0:T(8,128)S(1)} fusion(f32[2,4,32,16,256]{4,3,2,1,0:T(8,128)} %shard_map.30), kind=kLoop, calls=%fused_computation | loop fusion | bytes 4194304 | tf_op jit(solution)/shard_map/squeeze | solution.py:112
  13.1 3.3 %collective-permute-start = (f32[4,32,16,256]{3,2,1,0:T(8,128)S(1)}, f32[4,32,16,256]{3,2,1,0:T(8,128)}, u32[]{:S(2)}, u32[]{:S(2)}) collective-permute-start(f32[4,32,16,256]{3,2,1,0:T(8,128)S(1)} %slice_bitcast_fusion), channel_id=1, source_target_pairs={{0,1},{1,0},{2,3},{3,2},{4,5},{5,4},{6,7},{7,6},{8,9},{9,8},{10,11... | collective-permute-start | bytes 6291464 | tf_op jit(solution)/shard_map/ppermute | solution.py:112
  16.5 3.9 %collective-permute-done = f32[4,32,16,256]{3,2,1,0:T(8,128)} collective-permute-done((f32[4,32,16,256]{3,2,1,0:T(8,128)S(1)}, f32[4,32,16,256]{3,2,1,0:T(8,128)}, u32[]{:S(2)}, u32[]{:S(2)}) %collective-permute-start) | collective-permute-done | bytes 2097184 | tf_op jit(solution)/shard_map/ppermute | solution.py:112
  20.4 2.7 %fusion = f32[4,32,16,256]{3,2,1,0:T(8,128)S(1)} fusion(f32[4,32,16,256]{3,2,1,0:T(8,128)} %collective-permute-done, f32[2,4,32,16,256]{4,3,2,1,0:T(8,128)} %shard_map.30), kind=kLoop, calls=%fused_computation.2 | loop fusion | flops 524288 | bytes 6291456 | tf_op jit(solution)/shard_map/add | solution.py:112
  23.1 0.9 constant_dynamic-slice_fusion.2
  24.0 2.4 %collective-permute-start.2 = (f32[1,32,16,256]{3,2,1,0:T(8,128)S(1)}, f32[1,32,16,256]{3,2,1,0:T(8,128)}, u32[]{:S(2)}, u32[]{:S(2)}) collective-permute-start(f32[1,32,16,256]{3,2,1,0:T(8,128)S(1)} %get-tuple-element.4), channel_id=1, source_target_pairs={{0,4},{1,5},{2,6},{3,7},{4,0},{5,1},{6,2},{7,3},{8,12},{9,13},{10,... | collective-permute-start | bytes 1572872 | tf_op jit(solution)/shard_map/ppermute | solution.py:117
  26.4 1.1 collective-permute-start.3
  27.5 11.4 %collective-permute-done.1 = f32[1,32,16,256]{3,2,1,0:T(8,128)} collective-permute-done((f32[1,32,16,256]{3,2,1,0:T(8,128)}, f32[1,32,16,256]{3,2,1,0:T(8,128)}, u32[]{:S(2)}, u32[]{:S(2)}) %collective-permute-start.1) | collective-permute-done | bytes 524320 | tf_op jit(solution)/shard_map/ppermute | solution.py:117
  38.9 10.8 %collective-permute-done.2 = f32[1,32,16,256]{3,2,1,0:T(8,128)} collective-permute-done((f32[1,32,16,256]{3,2,1,0:T(8,128)S(1)}, f32[1,32,16,256]{3,2,1,0:T(8,128)}, u32[]{:S(2)}, u32[]{:S(2)}) %collective-permute-start.2) | collective-permute-done | bytes 524320 | tf_op jit(solution)/shard_map/ppermute | solution.py:117
  49.7 0.3 collective-permute-done.3
  50.0 1.6 %add_bitcast_fusion = f32[1,32,16,256]{3,2,0,1:T(8,128)S(1)} fusion(f32[1,32,16,256]{3,2,1,0:T(8,128)} %collective-permute-done.3, f32[1,32,16,256]{3,2,1,0:T(8,128)} %collective-permute-done.2, f32[1,32,16,256]{3,2,1,0:T(8,128)} %collective-permute-done.1, f32[4,32,16,256]{3,2,1,0:T(8,128)S(1)} %fusion, s32[]{:T(128)S(6)} %select_n.56), kind=kLoop, calls=%fused_computation.4 | loop fusion | flops 393216 | bytes 2621444 | tf_op jit(solution)/shard_map/add | solution.py:117
  51.6 25.7 %all_to_all.24 = f32[1,32,16,256]{3,2,0,1:T(8,128)S(1)} all-to-all(f32[1,32,16,256]{3,2,0,1:T(8,128)S(1)} %add_bitcast_fusion), channel_id=1, replica_groups=mesh['aa'=32,'ba'=8] {'aa'}, dimensions={1} | all-to-all | bytes 1048576 | tf_op jit(solution)/shard_map/all_to_all | solution.py:133
  77.3 0.3 reshape.223
  77.8 0.4 reshape.224.cols_ref
  78.2 0.6 fusion.5
  78.9 23.0 %all_to_all.25 = f32[256,1,128]{2,1,0:T(1,128)S(1)} all-to-all(f32[256,1,128]{2,1,0:T(1,128)S(1)} %bitcast.23), channel_id=1, replica_groups=mesh['aa'=32,'ba'=8] {'aa','ba'}, dimensions={0} | all-to-all | bytes 262144 | tf_op jit(solution)/shard_map/all_to_all | solution.py:68
  102.3 18.3 %all_to_all.26 = f32[256,1,128]{2,1,0:T(1,128)S(1)} all-to-all(f32[256,1,128]{2,1,0:T(1,128)S(1)} %broadcast_in_dim.2), channel_id=1, replica_groups=mesh['aa'=32,'ba'=8] {'aa','ba'}, dimensions={0} | all-to-all | bytes 262144 | tf_op jit(solution)/shard_map/all_to_all | solution.py:70
  120.6 0.5 broadcast.243
  121.1 0.9 reduce.4
  122.1 0.8 reshape.225.a_ref
  122.9 11.0 %shard_map.31 = (f32[8,64,64]{2,1,0:T(8,128)}, f32[8,64,256]{2,1,0:T(8,128)}) custom-call(f32[8,64,64]{2,1,0:T(8,128)} %reshape.225.a_ref, f32[8,64,256]{2,1,0:T(8,128)} %copy-done), custom_call_target="tpu_custom_call" | custom-call | tf_op jit(solution)/shard_map/pallas_call | solution.py:59
  (12 shorter events, 0.8 us)
Async XLA Ops:
  13.1 7.2 %collective-permute-start = (f32[4,32,16,256]{3,2,1,0:T(8,128)S(1)}, f32[4,32,16,256]{3,2,1,0:T(8,128)}, u32[]{:S(2)}, u32[]{:S(2)}) collective-permute-start(f32[4,32,16,256]{3,2,1,0:T(8,128)S(1)} %slice_bitcast_fusion), channel_id=1, source_target_pairs={{0,1},{1,0},{2,3},{3,2},{4,5},{5,4},{6,7},{7,6},{8,9},{9,8},{10,11... | collective-permute-start | bytes 6291464 | tf_op jit(solution)/shard_map/ppermute | solution.py:112
  24.0 14.9 %collective-permute-start.1 = (f32[1,32,16,256]{3,2,1,0:T(8,128)}, f32[1,32,16,256]{3,2,1,0:T(8,128)}, u32[]{:S(2)}, u32[]{:S(2)}) collective-permute-start(f32[1,32,16,256]{3,2,1,0:T(8,128)} %get-tuple-element.2), channel_id=1, source_target_pairs={{0,2},{1,3},{2,4},{3,5},{4,6},{5,7},{6,0},{7,1},{8,10},{9,11},{10,... | collective-permute-start | bytes 1572872 | tf_op jit(solution)/shard_map/ppermute | solution.py:117
  24.0 25.7 %collective-permute-start.2 = (f32[1,32,16,256]{3,2,1,0:T(8,128)S(1)}, f32[1,32,16,256]{3,2,1,0:T(8,128)}, u32[]{:S(2)}, u32[]{:S(2)}) collective-permute-start(f32[1,32,16,256]{3,2,1,0:T(8,128)S(1)} %get-tuple-element.4), channel_id=1, source_target_pairs={{0,4},{1,5},{2,6},{3,7},{4,0},{5,1},{6,2},{7,3},{8,12},{9,13},{10,... | collective-permute-start | bytes 1572872 | tf_op jit(solution)/shard_map/ppermute | solution.py:117
  26.4 23.6 %collective-permute-start.3 = (f32[1,32,16,256]{3,2,1,0:T(8,128)S(1)}, f32[1,32,16,256]{3,2,1,0:T(8,128)}, u32[]{:S(2)}, u32[]{:S(2)}) collective-permute-start(f32[1,32,16,256]{3,2,1,0:T(8,128)S(1)} %get-tuple-element.3), channel_id=1, source_target_pairs={{0,6},{1,7},{2,0},{3,1},{4,2},{5,3},{6,4},{7,5},{8,14},{9,15},{10,... | collective-permute-start | bytes 1572872 | tf_op jit(solution)/shard_map/ppermute | solution.py:117
  78.2 44.7 %copy-start = (f32[8,64,256]{2,1,0:T(8,128)}, f32[8,64,256]{2,1,0:T(8,128)S(1)}, u32[]{:S(2)}) copy-start(f32[8,64,256]{2,1,0:T(8,128)S(1)} %reshape.224.cols_ref) | copy-start | bytes 1572868

commit v14 on v13

--- a/solution.py
+++ b/solution.py
@@ -84,7 +84,7 @@
 
 
 def partial_dft(table_t, snapshots, core, n_aa, n_ba):
-    a_step = math.gcd(8, n_aa)
+    a_step = math.gcd(16, n_aa)
     rows, time_dev = table_t.shape
     points = snapshots.shape[1]
     pts_dev = points // (n_aa * n_ba)

time: 134 us -> 134 us (level)
  no operation moved by 1% of the time
where the time goes in v14:
time: 134 us
  blocking collectives  67.1 us (50%)
  waiting for transfers between devices  26.9 us (20%)
  Pallas kernels  19.4 us (14%)
  starting transfers between devices  6.57 us (5%)
  other arithmetic  6.34 us (5%)
  local copies, waits for them, and re-layouts  5.66 us (4%)
  between operations  1.41 us (1%)
    all_to_all x1, blocking collectives, local(): lax.all_to_all(block_spec, 'aa', split_axis=1, concat_axis=0, tiled=True)  25.4 us
    all_to_all x1, blocking collectives, all_sum(): mine = lax.all_to_all(pieces, axes, 0, 0, tiled=True).sum(0, keepdims=True)  23.5 us
    ppermute x3, waiting for transfers between devices, sum_over_ba(): total = total + lax.ppermute(out, 'ba', perm)  23 us
    all_to_all x1, blocking collectives, all_sum(): return lax.all_to_all(spread, axes, 0, 0, tiled=True).reshape(x.shape)  18.3 us
    pallas_call x1, Pallas kernels, factor_and_modes(): pl.pallas_call(functools.partial(_factor_kernel, scale), out_shape=(jax.S...  11 us
    pallas_call x1, Pallas kernels, partial_dft(): pl.pallas_call(_dft_kernel, grid_spec=pltpu.PrefetchScalarGridSpec(num_sc...  8.38 us
    ppermute x1, waiting for transfers between devices, sum_over_ba(): lax.ppermute(partial[0], 'ba', [(i, i ^ 1) for i in range(n_ba)])  3.92 us
    ppermute x1, starting transfers between devices, sum_over_ba(): lax.ppermute(partial[0], 'ba', [(i, i ^ 1) for i in range(n_ba)])  3.6 us
  transfers between devices with their start and end apart: 4, of which 4 were waited for; matrix products, arithmetic and copies ran while one was open for 0% of the time, Pallas kernels for 0%

profile of v14, /device:TPU:1, one launch (start us, length us, event | category | flops | bytes accessed | tf_op | source)
XLA Modules:
  0.0 134.0 jit_solution(2250748494252395832)
XLA Ops:
  0.7 0.6 multiply_reduce_fusion
  2.2 0.6 copy.7
  2.8 8.4 %shard_map.30 = f32[2,4,32,16,256]{4,3,2,1,0:T(8,128)} custom-call(s32[1]{0:T(128)} %bitcast.core_ref, f32[16,32]{1,0:T(8,128)} %bitcast.24, f32[32,65536]{1,0:T(8,128)} %snap_ref.1), custom_call_target="tpu_custom_call" | custom-call | tf_op jit(solution)/shard_map/pallas_call | solution.py:92
  11.2 1.8 %slice_bitcast_fusion = f32[4,32,16,256]{3,2,1,0:T(8,128)S(1)} fusion(f32[2,4,32,16,256]{4,3,2,1,0:T(8,128)} %shard_map.30), kind=kLoop, calls=%fused_computation | loop fusion | bytes 4194304 | tf_op jit(solution)/shard_map/squeeze | solution.py:112
  12.9 3.6 %collective-permute-start = (f32[4,32,16,256]{3,2,1,0:T(8,128)S(1)}, f32[4,32,16,256]{3,2,1,0:T(8,128)}, u32[]{:S(2)}, u32[]{:S(2)}) collective-permute-start(f32[4,32,16,256]{3,2,1,0:T(8,128)S(1)} %slice_bitcast_fusion), channel_id=1, source_target_pairs={{0,1},{1,0},{2,3},{3,2},{4,5},{5,4},{6,7},{7,6},{8,9},{9,8},{10,11... | collective-permute-start | bytes 6291464 | tf_op jit(solution)/shard_map/ppermute | solution.py:112
  16.5 3.9 %collective-permute-done = f32[4,32,16,256]{3,2,1,0:T(8,128)} collective-permute-done((f32[4,32,16,256]{3,2,1,0:T(8,128)S(1)}, f32[4,32,16,256]{3,2,1,0:T(8,128)}, u32[]{:S(2)}, u32[]{:S(2)}) %collective-permute-start) | collective-permute-done | bytes 2097184 | tf_op jit(solution)/shard_map/ppermute | solution.py:112
  20.4 2.7 %fusion = f32[4,32,16,256]{3,2,1,0:T(8,128)S(1)} fusion(f32[4,32,16,256]{3,2,1,0:T(8,128)} %collective-permute-done, f32[2,4,32,16,256]{4,3,2,1,0:T(8,128)} %shard_map.30), kind=kLoop, calls=%fused_computation.2 | loop fusion | flops 524288 | bytes 6291456 | tf_op jit(solution)/shard_map/add | solution.py:112
  23.1 0.9 constant_dynamic-slice_fusion.2
  24.1 1.9 %collective-permute-start.2 = (f32[1,32,16,256]{3,2,1,0:T(8,128)S(1)}, f32[1,32,16,256]{3,2,1,0:T(8,128)}, u32[]{:S(2)}, u32[]{:S(2)}) collective-permute-start(f32[1,32,16,256]{3,2,1,0:T(8,128)S(1)} %get-tuple-element.4), channel_id=1, source_target_pairs={{0,4},{1,5},{2,6},{3,7},{4,0},{5,1},{6,2},{7,3},{8,12},{9,13},{10,... | collective-permute-start | bytes 1572872 | tf_op jit(solution)/shard_map/ppermute | solution.py:117
  26.0 1.1 collective-permute-start.3
  27.1 12.4 %collective-permute-done.1 = f32[1,32,16,256]{3,2,1,0:T(8,128)} collective-permute-done((f32[1,32,16,256]{3,2,1,0:T(8,128)}, f32[1,32,16,256]{3,2,1,0:T(8,128)}, u32[]{:S(2)}, u32[]{:S(2)}) %collective-permute-start.1) | collective-permute-done | bytes 524320 | tf_op jit(solution)/shard_map/ppermute | solution.py:117
  39.5 9.8 %collective-permute-done.2 = f32[1,32,16,256]{3,2,1,0:T(8,128)} collective-permute-done((f32[1,32,16,256]{3,2,1,0:T(8,128)S(1)}, f32[1,32,16,256]{3,2,1,0:T(8,128)}, u32[]{:S(2)}, u32[]{:S(2)}) %collective-permute-start.2) | collective-permute-done | bytes 524320 | tf_op jit(solution)/shard_map/ppermute | solution.py:117
  49.3 0.8 collective-permute-done.3
  50.1 1.6 %add_bitcast_fusion = f32[1,32,16,256]{3,2,0,1:T(8,128)S(1)} fusion(f32[1,32,16,256]{3,2,1,0:T(8,128)} %collective-permute-done.3, f32[1,32,16,256]{3,2,1,0:T(8,128)} %collective-permute-done.2, f32[1,32,16,256]{3,2,1,0:T(8,128)} %collective-permute-done.1, f32[4,32,16,256]{3,2,1,0:T(8,128)S(1)} %fusion, s32[]{:T(128)S(6)} %select_n.56), kind=kLoop, calls=%fused_computation.4 | loop fusion | flops 393216 | bytes 2621444 | tf_op jit(solution)/shard_map/add | solution.py:117
  51.7 25.4 %all_to_all.24 = f32[1,32,16,256]{3,2,0,1:T(8,128)S(1)} all-to-all(f32[1,32,16,256]{3,2,0,1:T(8,128)S(1)} %add_bitcast_fusion), channel_id=1, replica_groups=mesh['aa'=32,'ba'=8] {'aa'}, dimensions={1} | all-to-all | bytes 1048576 | tf_op jit(solution)/shard_map/all_to_all | solution.py:133
  77.0 0.3 reshape.223
  77.5 0.4 reshape.224.cols_ref
  77.9 0.6 fusion.5
  78.6 23.5 %all_to_all.25 = f32[256,1,128]{2,1,0:T(1,128)S(1)} all-to-all(f32[256,1,128]{2,1,0:T(1,128)S(1)} %bitcast.23), channel_id=1, replica_groups=mesh['aa'=32,'ba'=8] {'aa','ba'}, dimensions={0} | all-to-all | bytes 262144 | tf_op jit(solution)/shard_map/all_to_all | solution.py:68
  102.4 18.3 %all_to_all.26 = f32[256,1,128]{2,1,0:T(1,128)S(1)} all-to-all(f32[256,1,128]{2,1,0:T(1,128)S(1)} %broadcast_in_dim.2), channel_id=1, replica_groups=mesh['aa'=32,'ba'=8] {'aa','ba'}, dimensions={0} | all-to-all | bytes 262144 | tf_op jit(solution)/shard_map/all_to_all | solution.py:70
  120.8 0.5 broadcast.243
  121.3 0.9 reduce.4
  122.2 0.8 reshape.225.a_ref
  123.0 11.0 %shard_map.31 = (f32[8,64,64]{2,1,0:T(8,128)}, f32[8,64,256]{2,1,0:T(8,128)}) custom-call(f32[8,64,64]{2,1,0:T(8,128)} %reshape.225.a_ref, f32[8,64,256]{2,1,0:T(8,128)} %copy-done), custom_call_target="tpu_custom_call" | custom-call | tf_op jit(solution)/shard_map/pallas_call | solution.py:59
  (12 shorter events, 0.8 us)
Async XLA Ops:
  12.9 7.5 %collective-permute-start = (f32[4,32,16,256]{3,2,1,0:T(8,128)S(1)}, f32[4,32,16,256]{3,2,1,0:T(8,128)}, u32[]{:S(2)}, u32[]{:S(2)}) collective-permute-start(f32[4,32,16,256]{3,2,1,0:T(8,128)S(1)} %slice_bitcast_fusion), channel_id=1, source_target_pairs={{0,1},{1,0},{2,3},{3,2},{4,5},{5,4},{6,7},{7,6},{8,9},{9,8},{10,11... | collective-permute-start | bytes 6291464 | tf_op jit(solution)/shard_map/ppermute | solution.py:112
  24.1 15.4 %collective-permute-start.1 = (f32[1,32,16,256]{3,2,1,0:T(8,128)}, f32[1,32,16,256]{3,2,1,0:T(8,128)}, u32[]{:S(2)}, u32[]{:S(2)}) collective-permute-start(f32[1,32,16,256]{3,2,1,0:T(8,128)} %get-tuple-element.2), channel_id=1, source_target_pairs={{0,2},{1,3},{2,4},{3,5},{4,6},{5,7},{6,0},{7,1},{8,10},{9,11},{10,... | collective-permute-start | bytes 1572872 | tf_op jit(solution)/shard_map/ppermute | solution.py:117
  24.1 25.2 %collective-permute-start.2 = (f32[1,32,16,256]{3,2,1,0:T(8,128)S(1)}, f32[1,32,16,256]{3,2,1,0:T(8,128)}, u32[]{:S(2)}, u32[]{:S(2)}) collective-permute-start(f32[1,32,16,256]{3,2,1,0:T(8,128)S(1)} %get-tuple-element.4), channel_id=1, source_target_pairs={{0,4},{1,5},{2,6},{3,7},{4,0},{5,1},{6,2},{7,3},{8,12},{9,13},{10,... | collective-permute-start | bytes 1572872 | tf_op jit(solution)/shard_map/ppermute | solution.py:117
  26.0 24.1 %collective-permute-start.3 = (f32[1,32,16,256]{3,2,1,0:T(8,128)S(1)}, f32[1,32,16,256]{3,2,1,0:T(8,128)}, u32[]{:S(2)}, u32[]{:S(2)}) collective-permute-start(f32[1,32,16,256]{3,2,1,0:T(8,128)S(1)} %get-tuple-element.3), channel_id=1, source_target_pairs={{0,6},{1,7},{2,0},{3,1},{4,2},{5,3},{6,4},{7,5},{8,14},{9,15},{10,... | collective-permute-start | bytes 1572872 | tf_op jit(solution)/shard_map/ppermute | solution.py:117
  77.9 45.2 %copy-start = (f32[8,64,256]{2,1,0:T(8,128)}, f32[8,64,256]{2,1,0:T(8,128)S(1)}, u32[]{:S(2)}) copy-start(f32[8,64,256]{2,1,0:T(8,128)S(1)} %reshape.224.cols_ref) | copy-start | bytes 1572868

commit v15 on v13

--- a/solution.py
+++ b/solution.py
@@ -28,10 +28,13 @@
 
 
 def _factor_kernel(scale, a_ref, cols_ref, upper_ref, modes_ref, m_ref):
-    freqs, n, _ = a_ref.shape
+    freqs, half, _ = a_ref.shape
+    n = 2 * half
     rows = lax.broadcasted_iota(jnp.int32, (freqs, n, 2 * n), 1)
     lanes = lax.broadcasted_iota(jnp.int32, (freqs, n, 2 * n), 2)
-    m_ref[...] = jnp.concatenate([a_ref[...], (rows[:, :, :n] == lanes[:, :, :n]).astype(jnp.float32)], axis=2)
+    packed = a_ref[...]
+    left = jnp.concatenate([packed[:, r // 2:r // 2 + 1, (r % 2) * n:(r % 2 + 1) * n] for r in range(n)], axis=1)
+    m_ref[...] = jnp.concatenate([left, (rows[:, :, :n] == lanes[:, :, :n]).astype(jnp.float32)], axis=2)
     tile = math.gcd(8, n)
     for lo in range(0, n, tile):
         def step(jj, carry, lo=lo):
@@ -60,7 +63,7 @@
         functools.partial(_factor_kernel, scale),
         out_shape=(jax.ShapeDtypeStruct(gram.shape, gram.dtype), jax.ShapeDtypeStruct(cols.shape, cols.dtype)),
         scratch_shapes=[pltpu.VMEM((freqs, n, 2 * n), jnp.float32)],
-    )(gram, cols)
+    )(gram.reshape(freqs, n // 2, 2 * n), cols)
 
 
 def all_sum(x, axes, count):

time: 134 us -> 131 us (0.978)
    all_to_all x1, blocking collectives: 23 us -> 21.6 us  [all_sum(): mine = lax.all_to_all(pieces, axes, 0, 0, tiled=True).sum(0, keepdims=True)]
  transfers between devices with their start and end apart: 4 -> 4, of which waited for: 4 -> 3; matrix products, arithmetic and copies ran while one was open for 0% -> 0% of each run, Pallas kernels for 0% -> 0%
where the time goes in v15:
time: 131 us
  blocking collectives  66.3 us (51%)
  waiting for transfers between devices  26.7 us (20%)
  Pallas kernels  19.9 us (15%)
  starting transfers between devices  6.09 us (5%)
  other arithmetic  5.39 us (4%)
  local copies, waits for them, and re-layouts  4.34 us (3%)
  between operations  1.39 us (1%)
    all_to_all x1, blocking collectives, local(): lax.all_to_all(block_spec, 'aa', split_axis=1, concat_axis=0, tiled=True)  26 us
    ppermute x3, waiting for transfers between devices, sum_over_ba(): total = total + lax.ppermute(out, 'ba', perm)  22.8 us
    all_to_all x1, blocking collectives, all_sum(): mine = lax.all_to_all(pieces, axes, 0, 0, tiled=True).sum(0, keepdims=True)  21.6 us
    all_to_all x1, blocking collectives, all_sum(): return lax.all_to_all(spread, axes, 0, 0, tiled=True).reshape(x.shape)  18.7 us
    pallas_call x1, Pallas kernels, factor_and_modes(): pl.pallas_call(functools.partial(_factor_kernel, scale), out_shape=(jax.S...  11.3 us
    pallas_call x1, Pallas kernels, partial_dft(): pl.pallas_call(_dft_kernel, grid_spec=pltpu.PrefetchScalarGridSpec(num_sc...  8.57 us
    ppermute x1, waiting for transfers between devices, sum_over_ba(): lax.ppermute(partial[0], 'ba', [(i, i ^ 1) for i in range(n_ba)])  3.92 us
    ppermute x1, starting transfers between devices, sum_over_ba(): lax.ppermute(partial[0], 'ba', [(i, i ^ 1) for i in range(n_ba)])  3.33 us
  transfers between devices with their start and end apart: 4, of which 3 were waited for; matrix products, arithmetic and copies ran while one was open for 0% of the time, Pallas kernels for 0%

profile of v15, /device:TPU:1, one launch (start us, length us, event | category | flops | bytes accessed | tf_op | source)
XLA Modules:
  0.0 130.7 jit_solution(17461389118457183387)
XLA Ops:
  0.6 0.6 multiply_reduce_fusion
  2.0 0.1 multiply_multiply_fusion.1
  2.2 0.6 copy.7
  2.8 8.6 %shard_map.30 = f32[2,4,32,16,256]{4,3,2,1,0:T(8,128)} custom-call(s32[1]{0:T(128)} %bitcast.core_ref, f32[16,32]{1,0:T(8,128)} %bitcast.26, f32[32,65536]{1,0:T(8,128)} %snap_ref.1), custom_call_target="tpu_custom_call" | custom-call | tf_op jit(solution)/shard_map/pallas_call | solution.py:95
  11.3 1.8 %slice_bitcast_fusion = f32[4,32,16,256]{3,2,1,0:T(8,128)S(1)} fusion(f32[2,4,32,16,256]{4,3,2,1,0:T(8,128)} %shard_map.30), kind=kLoop, calls=%fused_computation | loop fusion | bytes 4194304 | tf_op jit(solution)/shard_map/squeeze | solution.py:115
  13.1 3.3 %collective-permute-start = (f32[4,32,16,256]{3,2,1,0:T(8,128)S(1)}, f32[4,32,16,256]{3,2,1,0:T(8,128)}, u32[]{:S(2)}, u32[]{:S(2)}) collective-permute-start(f32[4,32,16,256]{3,2,1,0:T(8,128)S(1)} %slice_bitcast_fusion), channel_id=1, source_target_pairs={{0,1},{1,0},{2,3},{3,2},{4,5},{5,4},{6,7},{7,6},{8,9},{9,8},{10,11... | collective-permute-start | bytes 6291464 | tf_op jit(solution)/shard_map/ppermute | solution.py:115
  16.4 3.9 %collective-permute-done = f32[4,32,16,256]{3,2,1,0:T(8,128)} collective-permute-done((f32[4,32,16,256]{3,2,1,0:T(8,128)S(1)}, f32[4,32,16,256]{3,2,1,0:T(8,128)}, u32[]{:S(2)}, u32[]{:S(2)}) %collective-permute-start) | collective-permute-done | bytes 2097184 | tf_op jit(solution)/shard_map/ppermute | solution.py:115
  20.3 2.7 %fusion = f32[4,32,16,256]{3,2,1,0:T(8,128)S(1)} fusion(f32[4,32,16,256]{3,2,1,0:T(8,128)} %collective-permute-done, f32[2,4,32,16,256]{4,3,2,1,0:T(8,128)} %shard_map.30), kind=kLoop, calls=%fused_computation.2 | loop fusion | flops 524288 | bytes 6291456 | tf_op jit(solution)/shard_map/add | solution.py:115
  23.0 0.9 constant_dynamic-slice_fusion.2
  24.0 2.7 %collective-permute-start.3 = (f32[1,32,16,256]{3,2,1,0:T(8,128)S(1)}, f32[1,32,16,256]{3,2,1,0:T(8,128)}, u32[]{:S(2)}, u32[]{:S(2)}) collective-permute-start(f32[1,32,16,256]{3,2,1,0:T(8,128)S(1)} %get-tuple-element.3), channel_id=1, source_target_pairs={{0,6},{1,7},{2,0},{3,1},{4,2},{5,3},{6,4},{7,5},{8,14},{9,15},{10,... | collective-permute-start | bytes 1572872 | tf_op jit(solution)/shard_map/ppermute | solution.py:120
  26.7 0.1 collective-permute-start.2
  26.8 12.3 %collective-permute-done.1 = f32[1,32,16,256]{3,2,1,0:T(8,128)} collective-permute-done((f32[1,32,16,256]{3,2,1,0:T(8,128)}, f32[1,32,16,256]{3,2,1,0:T(8,128)}, u32[]{:S(2)}, u32[]{:S(2)}) %collective-permute-start.1) | collective-permute-done | bytes 524320 | tf_op jit(solution)/shard_map/ppermute | solution.py:120
  39.0 10.5 %collective-permute-done.2 = f32[1,32,16,256]{3,2,1,0:T(8,128)} collective-permute-done((f32[1,32,16,256]{3,2,1,0:T(8,128)S(1)}, f32[1,32,16,256]{3,2,1,0:T(8,128)}, u32[]{:S(2)}, u32[]{:S(2)}) %collective-permute-start.2) | collective-permute-done | bytes 524320 | tf_op jit(solution)/shard_map/ppermute | solution.py:120
  49.6 1.6 %add_bitcast_fusion = f32[1,32,16,256]{3,2,0,1:T(8,128)S(1)} fusion(f32[1,32,16,256]{3,2,1,0:T(8,128)} %collective-permute-done.3, f32[1,32,16,256]{3,2,1,0:T(8,128)} %collective-permute-done.2, f32[1,32,16,256]{3,2,1,0:T(8,128)} %collective-permute-done.1, f32[4,32,16,256]{3,2,1,0:T(8,128)S(1)} %fusion, s32[]{:T(128)S(6)} %select_n.56), kind=kLoop, calls=%fused_computation.4 | loop fusion | flops 393216 | bytes 2621444 | tf_op jit(solution)/shard_map/add | solution.py:120
  51.1 26.0 %all_to_all.24 = f32[1,32,16,256]{3,2,0,1:T(8,128)S(1)} all-to-all(f32[1,32,16,256]{3,2,0,1:T(8,128)S(1)} %add_bitcast_fusion), channel_id=1, replica_groups=mesh['aa'=32,'ba'=8] {'aa'}, dimensions={1} | all-to-all | bytes 1048576 | tf_op jit(solution)/shard_map/all_to_all | solution.py:136
  77.2 0.3 reshape.220
  77.5 0.2 copy.12
  77.7 0.4 reshape.221.cols_ref
  78.1 0.6 fusion.5
  78.7 0.1 all_to_all.18
  78.8 21.6 %all_to_all.25 = f32[256,1,128]{2,1,0:T(1,128)S(1)} all-to-all(f32[256,1,128]{2,1,0:T(1,128)S(1)} %bitcast.25), channel_id=1, replica_groups=mesh['aa'=32,'ba'=8] {'aa','ba'}, dimensions={0} | all-to-all | bytes 262144 | tf_op jit(solution)/shard_map/all_to_all | solution.py:71
  100.3 0.3 reduce_sum.19
  100.7 18.7 %all_to_all.26 = f32[256,1,128]{2,1,0:T(1,128)} all-to-all(f32[256,1,128]{2,1,0:T(1,128)S(1)} %broadcast_in_dim.2), channel_id=1, replica_groups=mesh['aa'=32,'ba'=8] {'aa','ba'}, dimensions={0} | all-to-all | bytes 262144 | tf_op jit(solution)/shard_map/all_to_all | solution.py:73
  119.4 11.3 %shard_map.31 = (f32[8,64,64]{2,1,0:T(8,128)}, f32[8,64,256]{2,1,0:T(8,128)}) custom-call(f32[8,32,128]{2,1,0:T(8,128)} %bitcast.24, f32[8,64,256]{2,1,0:T(8,128)} %copy-done), custom_call_target="tpu_custom_call" | custom-call | tf_op jit(solution)/shard_map/pallas_call | solution.py:62
  (9 shorter events, 0.1 us)
Async XLA Ops:
  13.1 7.2 %collective-permute-start = (f32[4,32,16,256]{3,2,1,0:T(8,128)S(1)}, f32[4,32,16,256]{3,2,1,0:T(8,128)}, u32[]{:S(2)}, u32[]{:S(2)}) collective-permute-start(f32[4,32,16,256]{3,2,1,0:T(8,128)S(1)} %slice_bitcast_fusion), channel_id=1, source_target_pairs={{0,1},{1,0},{2,3},{3,2},{4,5},{5,4},{6,7},{7,6},{8,9},{9,8},{10,11... | collective-permute-start | bytes 6291464 | tf_op jit(solution)/shard_map/ppermute | solution.py:115
  24.0 15.0 %collective-permute-start.1 = (f32[1,32,16,256]{3,2,1,0:T(8,128)}, f32[1,32,16,256]{3,2,1,0:T(8,128)}, u32[]{:S(2)}, u32[]{:S(2)}) collective-permute-start(f32[1,32,16,256]{3,2,1,0:T(8,128)} %get-tuple-element.2), channel_id=1, source_target_pairs={{0,2},{1,3},{2,4},{3,5},{4,6},{5,7},{6,0},{7,1},{8,10},{9,11},{10,... | collective-permute-start | bytes 1572872 | tf_op jit(solution)/shard_map/ppermute | solution.py:120
  24.0 15.0 %collective-permute-start.3 = (f32[1,32,16,256]{3,2,1,0:T(8,128)S(1)}, f32[1,32,16,256]{3,2,1,0:T(8,128)}, u32[]{:S(2)}, u32[]{:S(2)}) collective-permute-start(f32[1,32,16,256]{3,2,1,0:T(8,128)S(1)} %get-tuple-element.3), channel_id=1, source_target_pairs={{0,6},{1,7},{2,0},{3,1},{4,2},{5,3},{6,4},{7,5},{8,14},{9,15},{10,... | collective-permute-start | bytes 1572872 | tf_op jit(solution)/shard_map/ppermute | solution.py:120
  26.7 22.9 %collective-permute-start.2 = (f32[1,32,16,256]{3,2,1,0:T(8,128)S(1)}, f32[1,32,16,256]{3,2,1,0:T(8,128)}, u32[]{:S(2)}, u32[]{:S(2)}) collective-permute-start(f32[1,32,16,256]{3,2,1,0:T(8,128)S(1)} %get-tuple-element.4), channel_id=1, source_target_pairs={{0,4},{1,5},{2,6},{3,7},{4,0},{5,1},{6,2},{7,3},{8,12},{9,13},{10,... | collective-permute-start | bytes 1572872 | tf_op jit(solution)/shard_map/ppermute | solution.py:120
  78.0 41.4 %copy-start = (f32[8,64,256]{2,1,0:T(8,128)}, f32[8,64,256]{2,1,0:T(8,128)S(1)}, u32[]{:S(2)}) copy-start(f32[8,64,256]{2,1,0:T(8,128)S(1)} %reshape.221.cols_ref) | copy-start | bytes 1572868
